TPU v7x, 32 devices: a whole 2x2x4 slice. The times are simulated.
32 devices in a mesh: grp: 2 (over x), tok: 8 (over z, y), ep: 2 (over core).
Axes of the slice: x: 2, y: 2, z: 4, core: 2. Of those that a mesh axis runs over, the one named last changes fastest.
Arguments:
- tokens: bfloat16 [2, 2048, 768], P('ep', ('grp', 'tok')), parts along dimension 1, may hold values from -6 to 6
- norm_gain: float32 [768], replicated, may hold values from 0.5 to 1.5
- query_weight: bfloat16 [768, 768], replicated, may hold values from -0.21875 to 0.21875
- w_key: bfloat16 [768, 768], replicated, may hold values from -0.21875 to 0.21875
- w_value: bfloat16 [768, 768], replicated, may hold values from -0.21875 to 0.21875
- w_out: bfloat16 [768, 768], replicated, may hold values from -0.21875 to 0.21875
- head_scale: float32 [12], replicated, may hold values from 0.5 to 64
- matching: int32 [2, 64], P('ep', ('grp', 'tok')), parts along dimension 1, may hold values from 0 to 3, as said below
- valid: int32 [2, 64], P('ep', ('grp', 'tok')), parts along dimension 1, may hold values from 1 to 32, as said below
- stops: int32 [2, 16, 4], P('ep', ('grp', 'tok')), parts along dimension 1, may hold values from 0 to 7, as said below
Outputs:
- refined: bfloat16 [2, 2048, 768], P('ep', ('grp', 'tok')), parts along dimension 1
There are 2 independent parts, one for each index of `grp`. A program takes and returns all parts, laid end to end along the dimension named above; an argument that names none is the same for every part. Nothing has to cross between parts.
Inputs may be any that keep to these rules, and one draw needn't show every extreme that they name: `matching`: each aligned group of 4 entries is a permutation of 0 to 3. `valid`: in every block of 4 tiles one tile is full. `stops`: the 4 entries of block t are distinct blocks within 3 of t, and one of them is t - 3 or t + 3.
All inputs are finite; a program needn't handle non-finite values.
Results may differ from a plain program's by a relative error of at most 0.004.
The roundings to bfloat16 on the way count: a program that leaves them out, or rounds other values in their place, can miss the bound.
Values may be sent and summed in bfloat16 or wider, within the bound.
No kernel may reach another device: no remote copies, remote signals or barrier semaphores. Data moves between devices by JAX's collectives and lax.ppermute only.
A program may use at most 64 MiB of HBM per device.

v0:
```python
import math

import jax
import jax.numpy as jnp
from jax import lax
from jax.experimental import pallas as pl
from jax.experimental.pallas import tpu as pltpu
from jax.sharding import PartitionSpec as P

BAND = 3
ROW_PATCHES = 1024
META_ROWS = 8
NEG = -1e30


def partner(block, axis, apart):
    count = lax.axis_size(axis)
    route = []
    for low in range(count):
        high = low | 1 << apart
        if high != low and high < count:
            route += [(low, high), (high, low)]
    return lax.ppermute(block, axis, route)


def from_offset(shard, axis, by):
    size = lax.axis_size(axis)
    pairs = [(i + by, i) for i in range(size) if 0 <= i + by < size]
    return lax.ppermute(shard, axis, pairs)


def layer_norm(floated, norm_gain):
    center = jnp.mean(floated, axis=-1, keepdims=True)
    spread = jnp.mean((floated - center) ** 2, axis=-1, keepdims=True)
    return (floated - center) * lax.rsqrt(spread + 1e-05) * norm_gain


def turn_pairs(part, angle):
    quarter = part.shape[-1] // 2
    first = part[..., :quarter]
    second = part[..., quarter:]
    cosine = jnp.cos(angle)[:, None, :]
    sine = jnp.sin(angle)[:, None, :]
    return jnp.concatenate(
        [first * cosine - second * sine, second * cosine + first * sine], axis=-1
    )


def frequencies(quarter):
    return 100.0 ** (-jnp.arange(quarter, dtype=jnp.float32) / quarter)


def rotate(values, patch_coordinates, heads):
    count_rows, width = values.shape
    head_dim = width // heads
    half = head_dim // 2
    quarter = head_dim // 4
    split = values.reshape(count_rows, heads, head_dim)
    row_coordinate = (patch_coordinates // ROW_PATCHES).astype(jnp.float32)
    column_coordinate = (patch_coordinates % ROW_PATCHES).astype(jnp.float32)
    freqs = frequencies(quarter)
    turned = jnp.concatenate(
        [
            turn_pairs(split[..., :half], row_coordinate[:, None] * freqs[None, :]),
            turn_pairs(split[..., half:], column_coordinate[:, None] * freqs[None, :]),
        ],
        axis=-1,
    )
    return turned.reshape(count_rows, width)


def angle_tables(blocks, count_rows, head_dim):
    half = head_dim // 2
    quarter = head_dim // 4
    lanes = jnp.arange(128, dtype=jnp.int32)
    spots = blocks[:, None] * count_rows + jnp.arange(count_rows, dtype=jnp.int32)[None, :]
    row_coordinate = (spots // ROW_PATCHES).astype(jnp.float32)
    column_coordinate = (spots % ROW_PATCHES).astype(jnp.float32)
    in_row_part = (lanes % head_dim) < half
    coordinate = jnp.where(
        in_row_part[None, None, :], row_coordinate[:, :, None], column_coordinate[:, :, None]
    )
    freq_lane = frequencies(quarter)[lanes % quarter]
    angle = coordinate * freq_lane[None, None, :]
    first = (lanes % half) < quarter
    cosine = jnp.cos(angle)
    sine = jnp.sin(angle)
    signed = jnp.where(first[None, None, :], -sine, sine)
    return cosine, signed


def make_kernel(slots, heads, head_dim, count_rows, width):
    pairs = width // 128
    quarter = head_dim // 4
    per_pair = 128 // head_dim

    def kernel(needed_ref, scale_ref, q_ref, *rest):
        payload_refs = rest[:slots]
        cos_ref, sin_ref, wk_ref, wv_ref, wo_ref, tok_ref, out_ref, acc_ref, m_ref, l_ref = rest[slots:]
        acc_ref[...] = jnp.zeros_like(acc_ref)
        m_ref[...] = jnp.full(m_ref.shape, NEG, jnp.float32)
        l_ref[...] = jnp.zeros_like(l_ref)
        lane = lax.broadcasted_iota(jnp.int32, (count_rows, 128), 1)
        first = (lane % (2 * quarter)) < quarter
        head_of_lane = lane // head_dim

        for slot in range(slots):

            @pl.when(needed_ref[slot] != 0)
            def _():
                pref = payload_refs[slot]
                rows = pref[0:count_rows, :]
                live = pref[count_rows:count_rows + META_ROWS, 0:128].astype(jnp.float32)[0:1, :]
                kp = jnp.dot(rows, wk_ref[...], preferred_element_type=jnp.float32)
                vp = jnp.dot(rows, wv_ref[...], preferred_element_type=jnp.float32).astype(jnp.bfloat16)
                cosine = cos_ref[slot]
                signed = sin_ref[slot]
                for p in range(pairs):
                    lo = p * 128
                    x = kp[:, lo:lo + 128]
                    other = jnp.where(first, pltpu.roll(x, 128 - quarter, 1), pltpu.roll(x, quarter, 1))
                    k_pair = (x * cosine + other * signed).astype(jnp.bfloat16)
                    v_pair = vp[:, lo:lo + 128]
                    q_pair = q_ref[:, lo:lo + 128]
                    acc_pair = acc_ref[:, lo:lo + 128]
                    new_acc = acc_pair
                    for sub in range(per_pair):
                        h = p * per_pair + sub
                        mine = head_of_lane == sub
                        q_h = jnp.where(mine, q_pair, jnp.zeros_like(q_pair))
                        scores = lax.dot_general(
                            q_h, k_pair, (((1,), (1,)), ((), ())),
                            preferred_element_type=jnp.float32,
                        ) * scale_ref[h]
                        scores = jnp.where(live > 0, scores, jnp.float32(NEG))
                        best = m_ref[h]
                        fresh = jnp.maximum(best, jnp.max(scores, axis=1, keepdims=True))
                        decay = jnp.exp(best - fresh)
                        weights = jnp.exp(scores - fresh)
                        l_ref[h] = l_ref[h] * decay + jnp.sum(weights, axis=1, keepdims=True)
                        m_ref[h] = fresh
                        pv = jnp.dot(weights.astype(jnp.bfloat16), v_pair, preferred_element_type=jnp.float32)
                        new_acc = jnp.where(mine, acc_pair * decay + pv, new_acc)
                    acc_ref[:, lo:lo + 128] = new_acc

        parts = []
        for p in range(pairs):
            lo = p * 128
            acc_pair = acc_ref[:, lo:lo + 128]
            res = acc_pair
            for sub in range(per_pair):
                h = p * per_pair + sub
                res = jnp.where(head_of_lane == sub, acc_pair / l_ref[h], res)
            parts.append(res.astype(jnp.bfloat16))
        attended = jnp.concatenate(parts, axis=1)
        mixed = tok_ref[...].astype(jnp.float32) + jnp.dot(
            attended, wo_ref[...], preferred_element_type=jnp.float32
        )
        out_ref[...] = mixed.astype(out_ref.dtype)

    return kernel


def on_device(
    tokens, norm_gain, query_weight, w_key, w_value, w_out, head_scale, matching, valid, stops
):
    floated = tokens[0].astype(jnp.float32)
    count_rows, width = floated.shape
    heads = head_scale.shape[0]
    head_dim = width // heads
    block_index = lax.axis_index("tok")
    normed = layer_norm(floated, norm_gain).astype(jnp.bfloat16)
    row_ids = jnp.arange(count_rows, dtype=jnp.int32)
    patch_coordinates = block_index * count_rows + row_ids
    queries = rotate(
        jnp.dot(normed, query_weight, preferred_element_type=jnp.float32), patch_coordinates, heads
    ).astype(jnp.bfloat16)
    partner_rows, partner_counts = partner((normed, valid[0].astype(jnp.bfloat16)), "ep", 0)
    tile_count = matching.shape[1]
    tile_rows = count_rows // tile_count
    order = matching[0]
    key_rows = partner_rows.reshape(tile_count, tile_rows, width)[order].reshape(count_rows, width)
    counts = partner_counts[order].astype(jnp.float32)
    live = (
        (jnp.arange(tile_rows, dtype=jnp.float32)[None, :] < counts[:, None])
        .reshape(count_rows)
        .astype(jnp.bfloat16)
    )
    meta = jnp.zeros((META_ROWS, width), jnp.bfloat16).at[0, :count_rows].set(live)
    payload = jnp.concatenate([key_rows, meta], axis=0)

    offsets = list(range(-BAND, BAND + 1))
    received = [payload if d == 0 else from_offset(payload, "tok", d) for d in offsets]
    blocks = block_index + jnp.array(offsets, dtype=jnp.int32)
    needed = jnp.any(stops[0, 0][None, :] == blocks[:, None], axis=1).astype(jnp.int32)
    cosine, signed = angle_tables(blocks, count_rows, head_dim)
    scales = (head_scale / math.sqrt(head_dim)).astype(jnp.float32)

    slots = len(offsets)
    smem = pl.BlockSpec(memory_space=pltpu.SMEM)
    vmem = pl.BlockSpec(memory_space=pltpu.VMEM)
    out = pl.pallas_call(
        make_kernel(slots, heads, head_dim, count_rows, width),
        out_shape=jax.ShapeDtypeStruct((count_rows, width), jnp.bfloat16),
        in_specs=[smem, smem] + [vmem] * (1 + slots + 6),
        out_specs=vmem,
        scratch_shapes=[
            pltpu.VMEM((count_rows, width), jnp.float32),
            pltpu.VMEM((heads, count_rows, 1), jnp.float32),
            pltpu.VMEM((heads, count_rows, 1), jnp.float32),
        ],
    )(needed, scales, queries, *received, cosine, signed, w_key, w_value, w_out, tokens[0])
    return out[None]


def solution(mesh):
    in_specs = (
        P("ep", ("grp", "tok"), None),
        P(),
        P(),
        P(),
        P(),
        P(),
        P(),
        P("ep", ("grp", "tok")),
        P("ep", ("grp", "tok")),
        P("ep", ("grp", "tok"), None),
    )
    out_specs = P("ep", ("grp", "tok"), None)
    return jax.shard_map(
        on_device, mesh=mesh, in_specs=in_specs, out_specs=out_specs, check_vma=False
    )
```

profile of v0, /device:TPU:4, one launch (start us, length us, event | category | flops | bytes accessed | tf_op | source)
XLA Modules:
  0.0 78.3 jit_solution(13713510856604708627)
XLA Ops:
  0.0 1.0 %convert_reduce_fusion = f32[128]{0:T(128)S(1)} fusion(bf16[1,128,768]{2,1,0:T(8,128)(2,1)} %param.13), kind=kLoop, calls=%fused_computation.4 | loop fusion | flops 196480 | bytes 197120 | tf_op jit(solution)/shard_map/reduce_sum | solution.py:33
  1.0 1.1 %fusion.3 = f32[128]{0:T(128)S(1)} fusion(f32[128]{0:T(128)S(1)} %broadcast_multiply_fusion.1, bf16[1,128,768]{2,1,0:T(8,128)(2,1)} %param.13), kind=kLoop, calls=%fused_computation.9 | loop fusion | flops 393088 | bytes 197632 | tf_op jit(solution)/shard_map/reduce_sum | solution.py:34
  2.2 1.1 %fusion.5 = bf16[128,768]{1,0:T(8,128)(2,1)S(1)} fusion(f32[768]{0:T(1024)} %param.14, f32[128]{0:T(128)S(1)} %add_rsqrt_fusion, f32[128]{0:T(128)S(1)} %broadcast_multiply_fusion.1, bf16[1,128,768]{2,1,0:T(8,128)(2,1)} %param.13), kind=kLoop, calls=%fused_computation.11 | loop fusion | flops 491520 | bytes 397312 | tf_op jit(solution)/shard_map/convert_element_type | solution.py:172
  3.3 0.1 collective-permute-start
  3.4 0.7 convert_bitcast_fusion
  4.0 0.5 collective-permute-start.1
  4.6 0.0 copy-start
  4.6 0.0 copy-start.8
  4.6 1.6 %copy.16 = bf16[768,768]{0,1:T(8,128)(2,1)S(1)} copy(bf16[768,768]{1,0:T(8,128)(2,1)} %param.15) | data formatting | bytes 2359296 | tf_op args[2]
  6.2 0.0 copy-done
  6.2 0.0 copy-done.8
  6.2 0.6 fusion.7
  6.8 0.0 copy-start.9
  6.8 0.0 copy-start.10
  6.8 0.0 copy-start.11
  6.8 0.7 fusion.25
  7.6 0.1 multiply_cosine_fusion.1
  7.7 0.1 subtract_convert_fusion.1
  7.8 0.8 %copy.17.q_ref = bf16[128,768]{1,0:T(8,128)(2,1)} copy(bf16[128,768]{0,1:T(8,128)(2,1)S(1)} %bitcast.79) | data formatting | bytes 393216 | tf_op jit(solution)/shard_map/convert_element_type | solution.py:177
  8.6 0.0 copy-done.9
  8.6 0.1 fusion.12
  8.7 0.0 copy-done.10
  8.7 0.0 copy-done.11
  8.8 0.1 compare_reduce_fusion
  8.8 0.5 convert_element_type.70.needed_ref
  9.3 10.1 %bitcast_select_fusion.8 = f32[128]{0:T(128)S(1)} fusion(f32[]{:T(128)} %bitcast.30, f32[]{:T(128)} %bitcast.31, f32[]{:T(128)} %bitcast.32, f32[]{:T(128)} %bitcast.33, f32[]{:T(128)} %bitcast.34, f32[]{:T(128)} %bitcast.36, f32[]{:T(128)} %bitcast.35, f32[]{:T(128)} %bitcast.13, f32[]{:T(128)} %bitcast.15, f32[]{:T(128)} %bitcast.17, f32[]{:T(128)} %bitcast.19, ...), kind=kLoop, calls=%fused_computation.55 | loop fusion | flops 4992 | bytes 576 | tf_op jit(solution)/shard_map/gather | solution.py:83
  19.4 0.0 collective-permute-done.1
  19.4 0.6 gather_fusion.1
  20.1 0.1 iota_compare_fusion
  20.2 0.1 convert_element_type.82
  20.3 0.0 collective-permute-done
  20.3 0.6 gather_fusion
  20.9 4.4 %collective-permute-start.2 = (bf16[136,768]{1,0:T(8,128)(2,1)S(1)}, bf16[136,768]{1,0:T(8,128)(2,1)S(1)}, u32[]{:S(2)}, u32[]{:S(2)}) collective-permute-start(bf16[136,768]{1,0:T(8,128)(2,1)S(1)} %pad_maximum_fusion.rest_3_), channel_id=1, source_target_pairs={{0,6},{2,8},{4,10},{6,12},{8,14},{1,7},{3,9},{5,11},{7,13},{9,15},... | collective-permute-start | bytes 626696 | tf_op jit(solution)/shard_map/ppermute | solution.py:29
  25.3 3.1 %negate_select_fusion = (f32[7,128,128]{2,1,0:T(8,128)}, f32[7,128,128]{2,1,0:T(8,128)}) fusion(f32[128]{0:T(128)S(1)} %bitcast_select_fusion.8, f32[7,128]{1,0:T(8,128)S(1)} %get-tuple-element.30, f32[7,128]{1,0:T(8,128)S(1)} %get-tuple-element.29, pred[128]{0:T(512)(128)(4,1)S(1)} %get-tuple-element.54, pred[128]{0:T(512)(128)(4,1)S(1)} %get-tuple-element.53), kind=kLoop, calls=%fused_computation.2 | loop fusion | flops 458752 | bytes 925440 | tf_op jit(solution)/shard_map/jit(_where)/select_n | solution.py:88
  28.4 3.5 %collective-permute-start.3 = (bf16[136,768]{1,0:T(8,128)(2,1)S(1)}, bf16[136,768]{1,0:T(8,128)(2,1)S(1)}, u32[]{:S(2)}, u32[]{:S(2)}) collective-permute-start(bf16[136,768]{1,0:T(8,128)(2,1)S(1)} %pad_maximum_fusion.rest_3_), channel_id=1, source_target_pairs={{0,4},{2,6},{4,8},{6,10},{8,12},{10,14},{1,5},{3,7},{5,9},{7,11},{... | collective-permute-start | bytes 626696 | tf_op jit(solution)/shard_map/ppermute | solution.py:29
  31.9 3.4 %collective-permute-start.4 = (bf16[136,768]{1,0:T(8,128)(2,1)S(1)}, bf16[136,768]{1,0:T(8,128)(2,1)S(1)}, u32[]{:S(2)}, u32[]{:S(2)}) collective-permute-start(bf16[136,768]{1,0:T(8,128)(2,1)S(1)} %pad_maximum_fusion.rest_3_), channel_id=1, source_target_pairs={{0,2},{2,4},{4,6},{6,8},{8,10},{10,12},{12,14},{1,3},{3,5},{5,7},{... | collective-permute-start | bytes 626696 | tf_op jit(solution)/shard_map/ppermute | solution.py:29
  35.3 2.4 %collective-permute-start.5 = (bf16[136,768]{1,0:T(8,128)(2,1)S(1)}, bf16[136,768]{1,0:T(8,128)(2,1)S(1)}, u32[]{:S(2)}, u32[]{:S(2)}) collective-permute-start(bf16[136,768]{1,0:T(8,128)(2,1)S(1)} %pad_maximum_fusion.rest_3_), channel_id=1, source_target_pairs={{2,0},{4,2},{6,4},{8,6},{10,8},{12,10},{14,12},{3,1},{5,3},{7,5},{... | collective-permute-start | bytes 626696 | tf_op jit(solution)/shard_map/ppermute | solution.py:29
  37.7 1.3 %collective-permute-start.6 = (bf16[136,768]{1,0:T(8,128)(2,1)S(1)}, bf16[136,768]{1,0:T(8,128)(2,1)S(1)}, u32[]{:S(2)}, u32[]{:S(2)}) collective-permute-start(bf16[136,768]{1,0:T(8,128)(2,1)S(1)} %pad_maximum_fusion.rest_3_), channel_id=1, source_target_pairs={{4,0},{6,2},{8,4},{10,6},{12,8},{14,10},{5,1},{7,3},{9,5},{11,7},{... | collective-permute-start | bytes 626696 | tf_op jit(solution)/shard_map/ppermute | solution.py:29
  39.0 0.0 collective-permute-done.2.rest_0_
  39.1 1.3 %collective-permute-start.7 = (bf16[136,768]{1,0:T(8,128)(2,1)S(1)}, bf16[136,768]{1,0:T(8,128)(2,1)S(1)}, u32[]{:S(2)}, u32[]{:S(2)}) collective-permute-start(bf16[136,768]{1,0:T(8,128)(2,1)S(1)} %pad_maximum_fusion.rest_3_), channel_id=1, source_target_pairs={{6,0},{8,2},{10,4},{12,6},{14,8},{7,1},{9,3},{11,5},{13,7},{15,9},... | collective-permute-start | bytes 626696 | tf_op jit(solution)/shard_map/ppermute | solution.py:29
  40.4 0.5 broadcast_multiply_fusion.2.scale_ref
  40.9 0.0 collective-permute-done.3.rest_1_
  40.9 2.5 %collective-permute-done.4.rest_2_ = bf16[136,768]{1,0:T(8,128)(2,1)S(1)} collective-permute-done((bf16[136,768]{1,0:T(8,128)(2,1)S(1)}, bf16[136,768]{1,0:T(8,128)(2,1)S(1)}, u32[]{:S(2)}, u32[]{:S(2)}) %collective-permute-start.4) | collective-permute-done | bytes 208928 | tf_op jit(solution)/shard_map/ppermute | solution.py:29
  43.4 2.7 %collective-permute-done.5.rest_4_ = bf16[136,768]{1,0:T(8,128)(2,1)S(1)} collective-permute-done((bf16[136,768]{1,0:T(8,128)(2,1)S(1)}, bf16[136,768]{1,0:T(8,128)(2,1)S(1)}, u32[]{:S(2)}, u32[]{:S(2)}) %collective-permute-start.5) | collective-permute-done | bytes 208928 | tf_op jit(solution)/shard_map/ppermute | solution.py:29
  46.1 1.5 %collective-permute-done.6.rest_5_ = bf16[136,768]{1,0:T(8,128)(2,1)S(1)} collective-permute-done((bf16[136,768]{1,0:T(8,128)(2,1)S(1)}, bf16[136,768]{1,0:T(8,128)(2,1)S(1)}, u32[]{:S(2)}, u32[]{:S(2)}) %collective-permute-start.6) | collective-permute-done | bytes 208928 | tf_op jit(solution)/shard_map/ppermute | solution.py:29
  47.7 9.9 %collective-permute-done.7.rest_6_ = bf16[136,768]{1,0:T(8,128)(2,1)S(1)} collective-permute-done((bf16[136,768]{1,0:T(8,128)(2,1)S(1)}, bf16[136,768]{1,0:T(8,128)(2,1)S(1)}, u32[]{:S(2)}, u32[]{:S(2)}) %collective-permute-start.7) | collective-permute-done | bytes 208928 | tf_op jit(solution)/shard_map/ppermute | solution.py:29
  57.6 0.6 copy-done.7
  58.2 20.1 %shard_map.109 = bf16[128,768]{1,0:T(8,128)(2,1)} custom-call(s32[7]{0:T(128)} %convert_element_type.70.needed_ref, f32[12]{0:T(128)} %broadcast_multiply_fusion.2.scale_ref, bf16[128,768]{1,0:T(8,128)(2,1)} %copy.17.q_ref, bf16[136,768]{1,0:T(8,128)(2,1)} %copy-done.2, bf16[136,768]{1,0:T(8,128)(2,1)} %copy-done.3, bf16[136,768]{1,0:T(8,128)(2,1)} %copy-done.4, ...), custom_call_target="tpu_custom_call" | custom-call | tf_op jit(solution)/shard_map/pallas_call | solution.py:202
  (27 shorter events, 0.1 us)
Async XLA Ops:
  3.3 17.0 %collective-permute-start = (bf16[128,768]{1,0:T(8,128)(2,1)S(1)}, bf16[128,768]{1,0:T(8,128)(2,1)S(1)}, u32[]{:S(2)}, u32[]{:S(2)}) collective-permute-start(bf16[128,768]{1,0:T(8,128)(2,1)S(1)} %fusion.5), channel_id=1, source_target_pairs={{0,1},{1,0},{2,3},{3,2},{4,5},{5,4},{6,7},{7,6},{8,9},{9,8},{10,11... | collective-permute-start | bytes 589832 | tf_op jit(solution)/shard_map/ppermute | solution.py:23
  4.0 15.4 %collective-permute-start.1 = (bf16[4]{0:T(256)(128)(2,1)S(1)}, bf16[4]{0:T(256)(128)(2,1)S(1)}, u32[]{:S(2)}, u32[]{:S(2)}) collective-permute-start(bf16[4]{0:T(256)(128)(2,1)S(1)} %convert_bitcast_fusion), channel_id=1, source_target_pairs={{0,1},{1,0},{2,3},{3,2},{4,5},{5,4},{6,7},{7,6},{8,9},{9,8},{10,11... | collective-permute-start | bytes 32 | tf_op jit(solution)/shard_map/ppermute | solution.py:23
  4.6 1.6 %copy-start = (bf16[1,128,768]{2,1,0:T(8,128)(2,1)S(1)}, bf16[1,128,768]{2,1,0:T(8,128)(2,1)}, u32[]{:S(2)}) copy-start(bf16[1,128,768]{2,1,0:T(8,128)(2,1)} %param.13) | copy-start | bytes 589828
  4.6 1.6 %copy-start.8 = (f32[768]{0:T(1024)S(1)}, f32[768]{0:T(1024)}, u32[]{:S(2)}) copy-start(f32[768]{0:T(1024)} %param.14) | copy-start | bytes 9220
  6.8 1.8 %copy-start.9 = (s32[7]{0:T(128)S(1)}, s32[7]{0:T(128)}, u32[]{:S(2)}) copy-start(s32[7]{0:T(128)} %constant.143.clone) | copy-start | bytes 88
  6.8 1.9 %copy-start.10 = (s32[1,4]{1,0:T(1,128)S(1)}, s32[1,4]{1,0:T(1,128)}, u32[]{:S(2)}) copy-start(s32[1,4]{1,0:T(1,128)} %param.20) | copy-start | bytes 52
  6.8 1.9 %copy-start.11 = (s32[1,1,4]{2,1,0:T(1,128)S(1)}, s32[1,1,4]{2,1,0:T(1,128)}, u32[]{:S(2)}) copy-start(s32[1,1,4]{2,1,0:T(1,128)} %param.22) | copy-start | bytes 52
  9.3 31.0 %copy-start.12 = (f32[12]{0:T(128)S(1)}, f32[12]{0:T(128)}, u32[]{:S(2)}) copy-start(f32[12]{0:T(128)} %param.19) | copy-start | bytes 148
  20.9 36.7 %copy-start.1 = (bf16[136,768]{1,0:T(8,128)(2,1)}, bf16[136,768]{1,0:T(8,128)(2,1)S(1)}, u32[]{:S(2)}) copy-start(bf16[136,768]{1,0:T(8,128)(2,1)S(1)} %pad_maximum_fusion.rest_3_) | copy-start | bytes 626692
  20.9 18.2 %collective-permute-start.2 = (bf16[136,768]{1,0:T(8,128)(2,1)S(1)}, bf16[136,768]{1,0:T(8,128)(2,1)S(1)}, u32[]{:S(2)}, u32[]{:S(2)}) collective-permute-start(bf16[136,768]{1,0:T(8,128)(2,1)S(1)} %pad_maximum_fusion.rest_3_), channel_id=1, source_target_pairs={{0,6},{2,8},{4,10},{6,12},{8,14},{1,7},{3,9},{5,11},{7,13},{9,15},... | collective-permute-start | bytes 626696 | tf_op jit(solution)/shard_map/ppermute | solution.py:29
  28.4 12.5 %collective-permute-start.3 = (bf16[136,768]{1,0:T(8,128)(2,1)S(1)}, bf16[136,768]{1,0:T(8,128)(2,1)S(1)}, u32[]{:S(2)}, u32[]{:S(2)}) collective-permute-start(bf16[136,768]{1,0:T(8,128)(2,1)S(1)} %pad_maximum_fusion.rest_3_), channel_id=1, source_target_pairs={{0,4},{2,6},{4,8},{6,10},{8,12},{10,14},{1,5},{3,7},{5,9},{7,11},{... | collective-permute-start | bytes 626696 | tf_op jit(solution)/shard_map/ppermute | solution.py:29
  31.9 11.5 %collective-permute-start.4 = (bf16[136,768]{1,0:T(8,128)(2,1)S(1)}, bf16[136,768]{1,0:T(8,128)(2,1)S(1)}, u32[]{:S(2)}, u32[]{:S(2)}) collective-permute-start(bf16[136,768]{1,0:T(8,128)(2,1)S(1)} %pad_maximum_fusion.rest_3_), channel_id=1, source_target_pairs={{0,2},{2,4},{4,6},{6,8},{8,10},{10,12},{12,14},{1,3},{3,5},{5,7},{... | collective-permute-start | bytes 626696 | tf_op jit(solution)/shard_map/ppermute | solution.py:29
  35.3 10.8 %collective-permute-start.5 = (bf16[136,768]{1,0:T(8,128)(2,1)S(1)}, bf16[136,768]{1,0:T(8,128)(2,1)S(1)}, u32[]{:S(2)}, u32[]{:S(2)}) collective-permute-start(bf16[136,768]{1,0:T(8,128)(2,1)S(1)} %pad_maximum_fusion.rest_3_), channel_id=1, source_target_pairs={{2,0},{4,2},{6,4},{8,6},{10,8},{12,10},{14,12},{3,1},{5,3},{7,5},{... | collective-permute-start | bytes 626696 | tf_op jit(solution)/shard_map/ppermute | solution.py:29
  37.7 9.9 %collective-permute-start.6 = (bf16[136,768]{1,0:T(8,128)(2,1)S(1)}, bf16[136,768]{1,0:T(8,128)(2,1)S(1)}, u32[]{:S(2)}, u32[]{:S(2)}) collective-permute-start(bf16[136,768]{1,0:T(8,128)(2,1)S(1)} %pad_maximum_fusion.rest_3_), channel_id=1, source_target_pairs={{4,0},{6,2},{8,4},{10,6},{12,8},{14,10},{5,1},{7,3},{9,5},{11,7},{... | collective-permute-start | bytes 626696 | tf_op jit(solution)/shard_map/ppermute | solution.py:29
  39.0 18.5 %copy-start.2 = (bf16[136,768]{1,0:T(8,128)(2,1)}, bf16[136,768]{1,0:T(8,128)(2,1)S(1)}, u32[]{:S(2)}) copy-start(bf16[136,768]{1,0:T(8,128)(2,1)S(1)} %collective-permute-done.2.rest_0_) | copy-start | bytes 626692
  39.1 18.5 %collective-permute-start.7 = (bf16[136,768]{1,0:T(8,128)(2,1)S(1)}, bf16[136,768]{1,0:T(8,128)(2,1)S(1)}, u32[]{:S(2)}, u32[]{:S(2)}) collective-permute-start(bf16[136,768]{1,0:T(8,128)(2,1)S(1)} %pad_maximum_fusion.rest_3_), channel_id=1, source_target_pairs={{6,0},{8,2},{10,4},{12,6},{14,8},{7,1},{9,3},{11,5},{13,7},{15,9},... | collective-permute-start | bytes 626696 | tf_op jit(solution)/shard_map/ppermute | solution.py:29
  40.9 16.6 %copy-start.3 = (bf16[136,768]{1,0:T(8,128)(2,1)}, bf16[136,768]{1,0:T(8,128)(2,1)S(1)}, u32[]{:S(2)}) copy-start(bf16[136,768]{1,0:T(8,128)(2,1)S(1)} %collective-permute-done.3.rest_1_) | copy-start | bytes 626692
  43.4 14.1 %copy-start.4 = (bf16[136,768]{1,0:T(8,128)(2,1)}, bf16[136,768]{1,0:T(8,128)(2,1)S(1)}, u32[]{:S(2)}) copy-start(bf16[136,768]{1,0:T(8,128)(2,1)S(1)} %collective-permute-done.4.rest_2_) | copy-start | bytes 626692
  46.1 11.4 %copy-start.5 = (bf16[136,768]{1,0:T(8,128)(2,1)}, bf16[136,768]{1,0:T(8,128)(2,1)S(1)}, u32[]{:S(2)}) copy-start(bf16[136,768]{1,0:T(8,128)(2,1)S(1)} %collective-permute-done.5.rest_4_) | copy-start | bytes 626692
  47.7 9.9 %copy-start.6 = (bf16[136,768]{1,0:T(8,128)(2,1)}, bf16[136,768]{1,0:T(8,128)(2,1)S(1)}, u32[]{:S(2)}) copy-start(bf16[136,768]{1,0:T(8,128)(2,1)S(1)} %collective-permute-done.6.rest_5_) | copy-start | bytes 626692
  57.5 0.7 copy-start.7
where the time goes:
time: 78.8 us; the launch traced here: 78.3 us
  Pallas kernels  20.1 us (26%)
  other arithmetic  18.7 us (24%)
  starting transfers between devices  16.9 us (21%)
  waiting for transfers between devices  16.6 us (21%)
  local copies, waits for them, and re-layouts  5.15 us (7%)
    pallas_call x1, Pallas kernels, on_device(): pl.pallas_call(make_kernel(slots, heads, head_dim, count_rows, width), ou...  20.1 us
    ppermute x6, waiting for transfers between devices, from_offset(): return lax.ppermute(shard, axis, pairs)  16.6 us
    ppermute x6, starting transfers between devices, from_offset(): return lax.ppermute(shard, axis, pairs)  16.4 us
    gather x1, other arithmetic, angle_tables(): freq_lane = frequencies(quarter)[lanes % quarter]  10.1 us
    select_n x1, other arithmetic, angle_tables(): signed = jnp.where(first[None, None, :], -sine, sine)  3.06 us
    unnamed x27, local copies, waits for them, and re-layouts  2.31 us
  transfers between devices with their start and end apart: 8, of which 4 were waited for; matrix products, arithmetic and copies ran while one was open for 25% of the time, Pallas kernels for 0%

commit v1 on v0

--- a/solution.py
+++ b/solution.py
@@ -80,7 +80,7 @@
     coordinate = jnp.where(
         in_row_part[None, None, :], row_coordinate[:, :, None], column_coordinate[:, :, None]
     )
-    freq_lane = frequencies(quarter)[lanes % quarter]
+    freq_lane = jnp.tile(frequencies(quarter), 128 // quarter)
     angle = coordinate * freq_lane[None, None, :]
     first = (lanes % half) < quarter
     cosine = jnp.cos(angle)

time: 78.8 us -> 68 us (0.86)
  other arithmetic: 18.7 us -> 8.57 us
    gather x1 -> x0, other arithmetic: 10.1 us -> none  [angle_tables(): freq_lane = frequencies(quarter)[lanes % quarter]]
  transfers between devices with their start and end apart: 8 -> 8, of which waited for: 4 -> 4; matrix products, arithmetic and copies ran while one was open for 25% -> 13% of each run, Pallas kernels for 0% -> 0%
where the time goes in v1:
time: 68 us; the launch traced here: 67.6 us
  Pallas kernels  20.1 us (30%)
  starting transfers between devices  16.9 us (25%)
  waiting for transfers between devices  16.7 us (25%)
  other arithmetic  8.57 us (13%)
  local copies, waits for them, and re-layouts  4.53 us (7%)
    pallas_call x1, Pallas kernels, on_device(): pl.pallas_call(make_kernel(slots, heads, head_dim, count_rows, width), ou...  20.1 us
    ppermute x6, waiting for transfers between devices, from_offset(): return lax.ppermute(shard, axis, pairs)  16.7 us
    ppermute x6, starting transfers between devices, from_offset(): return lax.ppermute(shard, axis, pairs)  16.4 us
    select_n x1, other arithmetic, angle_tables(): signed = jnp.where(first[None, None, :], -sine, sine)  3.04 us
    unnamed x27, local copies, waits for them, and re-layouts  2.32 us
  transfers between devices with their start and end apart: 8, of which 4 were waited for; matrix products, arithmetic and copies ran while one was open for 13% of the time, Pallas kernels for 0%

profile of v1, /device:TPU:4, one launch (start us, length us, event | category | flops | bytes accessed | tf_op | source)
XLA Modules:
  0.0 67.6 jit_solution(10317068011569980161)
XLA Ops:
  0.0 1.0 %convert_reduce_fusion = f32[128]{0:T(128)S(1)} fusion(bf16[1,128,768]{2,1,0:T(8,128)(2,1)} %param.13), kind=kLoop, calls=%fused_computation.4 | loop fusion | flops 196480 | bytes 197120 | tf_op jit(solution)/shard_map/reduce_sum | solution.py:33
  1.0 1.1 %fusion.3 = f32[128]{0:T(128)S(1)} fusion(f32[128]{0:T(128)S(1)} %broadcast_multiply_fusion.1, bf16[1,128,768]{2,1,0:T(8,128)(2,1)} %param.13), kind=kLoop, calls=%fused_computation.9 | loop fusion | flops 393088 | bytes 197632 | tf_op jit(solution)/shard_map/reduce_sum | solution.py:34
  2.2 1.1 %fusion.5 = bf16[128,768]{1,0:T(8,128)(2,1)S(1)} fusion(f32[768]{0:T(1024)} %param.14, f32[128]{0:T(128)S(1)} %add_rsqrt_fusion, f32[128]{0:T(128)S(1)} %broadcast_multiply_fusion.1, bf16[1,128,768]{2,1,0:T(8,128)(2,1)} %param.13), kind=kLoop, calls=%fused_computation.11 | loop fusion | flops 491520 | bytes 397312 | tf_op jit(solution)/shard_map/convert_element_type | solution.py:172
  3.3 0.1 collective-permute-start
  3.4 0.7 convert_bitcast_fusion
  4.0 0.5 collective-permute-start.1
  4.6 0.0 copy-start
  4.6 0.0 copy-start.8
  4.6 1.6 %copy.16 = bf16[768,768]{0,1:T(8,128)(2,1)S(1)} copy(bf16[768,768]{1,0:T(8,128)(2,1)} %param.15) | data formatting | bytes 2359296 | tf_op args[2]
  6.2 0.0 copy-done
  6.2 0.0 copy-done.8
  6.2 0.0 copy-start.10
  6.2 0.0 copy-start.9
  6.3 0.6 fusion.7
  6.8 0.0 copy-start.11
  6.8 0.1 multiply_cosine_fusion.1
  7.0 0.1 subtract_convert_fusion.1
  7.1 0.8 %copy.17.q_ref = bf16[128,768]{1,0:T(8,128)(2,1)} copy(bf16[128,768]{0,1:T(8,128)(2,1)S(1)} %bitcast.25) | data formatting | bytes 393216 | tf_op jit(solution)/shard_map/convert_element_type | solution.py:177
  7.9 0.0 copy-done.10
  7.9 0.0 copy-done.9
  7.9 0.1 fusion.12
  8.0 0.1 mul.166
  8.1 0.0 copy-done.11
  8.1 0.1 compare_reduce_fusion
  8.2 0.5 convert_element_type.70.needed_ref
  8.7 0.0 collective-permute-done.1
  8.7 0.6 gather_fusion.1
  9.4 0.1 iota_compare_fusion
  9.5 0.1 convert_element_type.82
  9.6 0.0 collective-permute-done
  9.6 0.6 gather_fusion
  10.2 0.0 copy-start.1
  10.2 4.4 %collective-permute-start.2 = (bf16[136,768]{1,0:T(8,128)(2,1)S(1)}, bf16[136,768]{1,0:T(8,128)(2,1)S(1)}, u32[]{:S(2)}, u32[]{:S(2)}) collective-permute-start(bf16[136,768]{1,0:T(8,128)(2,1)S(1)} %pad_maximum_fusion.rest_3_), channel_id=1, source_target_pairs={{0,6},{2,8},{4,10},{6,12},{8,14},{1,7},{3,9},{5,11},{7,13},{9,15},... | collective-permute-start | bytes 626696 | tf_op jit(solution)/shard_map/ppermute | solution.py:29
  14.6 3.0 %negate_select_fusion = (f32[7,128,128]{2,1,0:T(8,128)}, f32[7,128,128]{2,1,0:T(8,128)}) fusion(f32[128]{0:T(128)S(1)} %mul.166, f32[7,128]{1,0:T(8,128)S(1)} %get-tuple-element.30, f32[7,128]{1,0:T(8,128)S(1)} %get-tuple-element.29, pred[128]{0:T(512)(128)(4,1)S(1)} %get-tuple-element.38, pred[128]{0:T(512)(128)(4,1)S(1)} %get-tuple-element.37), kind=kLoop, calls=%fused_computation.2 | loop fusion | flops 458752 | bytes 925440 | tf_op jit(solution)/shard_map/jit(_where)/select_n | solution.py:88
  17.7 3.5 %collective-permute-start.3 = (bf16[136,768]{1,0:T(8,128)(2,1)S(1)}, bf16[136,768]{1,0:T(8,128)(2,1)S(1)}, u32[]{:S(2)}, u32[]{:S(2)}) collective-permute-start(bf16[136,768]{1,0:T(8,128)(2,1)S(1)} %pad_maximum_fusion.rest_3_), channel_id=1, source_target_pairs={{0,4},{2,6},{4,8},{6,10},{8,12},{10,14},{1,5},{3,7},{5,9},{7,11},{... | collective-permute-start | bytes 626696 | tf_op jit(solution)/shard_map/ppermute | solution.py:29
  21.1 3.4 %collective-permute-start.4 = (bf16[136,768]{1,0:T(8,128)(2,1)S(1)}, bf16[136,768]{1,0:T(8,128)(2,1)S(1)}, u32[]{:S(2)}, u32[]{:S(2)}) collective-permute-start(bf16[136,768]{1,0:T(8,128)(2,1)S(1)} %pad_maximum_fusion.rest_3_), channel_id=1, source_target_pairs={{0,2},{2,4},{4,6},{6,8},{8,10},{10,12},{12,14},{1,3},{3,5},{5,7},{... | collective-permute-start | bytes 626696 | tf_op jit(solution)/shard_map/ppermute | solution.py:29
  24.6 2.4 %collective-permute-start.5 = (bf16[136,768]{1,0:T(8,128)(2,1)S(1)}, bf16[136,768]{1,0:T(8,128)(2,1)S(1)}, u32[]{:S(2)}, u32[]{:S(2)}) collective-permute-start(bf16[136,768]{1,0:T(8,128)(2,1)S(1)} %pad_maximum_fusion.rest_3_), channel_id=1, source_target_pairs={{2,0},{4,2},{6,4},{8,6},{10,8},{12,10},{14,12},{3,1},{5,3},{7,5},{... | collective-permute-start | bytes 626696 | tf_op jit(solution)/shard_map/ppermute | solution.py:29
  27.0 1.3 %collective-permute-start.6 = (bf16[136,768]{1,0:T(8,128)(2,1)S(1)}, bf16[136,768]{1,0:T(8,128)(2,1)S(1)}, u32[]{:S(2)}, u32[]{:S(2)}) collective-permute-start(bf16[136,768]{1,0:T(8,128)(2,1)S(1)} %pad_maximum_fusion.rest_3_), channel_id=1, source_target_pairs={{4,0},{6,2},{8,4},{10,6},{12,8},{14,10},{5,1},{7,3},{9,5},{11,7},{... | collective-permute-start | bytes 626696 | tf_op jit(solution)/shard_map/ppermute | solution.py:29
  28.3 0.0 collective-permute-done.2.rest_0_
  28.3 1.3 %collective-permute-start.7 = (bf16[136,768]{1,0:T(8,128)(2,1)S(1)}, bf16[136,768]{1,0:T(8,128)(2,1)S(1)}, u32[]{:S(2)}, u32[]{:S(2)}) collective-permute-start(bf16[136,768]{1,0:T(8,128)(2,1)S(1)} %pad_maximum_fusion.rest_3_), channel_id=1, source_target_pairs={{6,0},{8,2},{10,4},{12,6},{14,8},{7,1},{9,3},{11,5},{13,7},{15,9},... | collective-permute-start | bytes 626696 | tf_op jit(solution)/shard_map/ppermute | solution.py:29
  29.6 0.5 broadcast_multiply_fusion.2.scale_ref
  30.2 0.0 collective-permute-done.3.rest_1_
  30.2 2.5 %collective-permute-done.4.rest_2_ = bf16[136,768]{1,0:T(8,128)(2,1)S(1)} collective-permute-done((bf16[136,768]{1,0:T(8,128)(2,1)S(1)}, bf16[136,768]{1,0:T(8,128)(2,1)S(1)}, u32[]{:S(2)}, u32[]{:S(2)}) %collective-permute-start.4) | collective-permute-done | bytes 208928 | tf_op jit(solution)/shard_map/ppermute | solution.py:29
  32.7 2.7 %collective-permute-done.5.rest_4_ = bf16[136,768]{1,0:T(8,128)(2,1)S(1)} collective-permute-done((bf16[136,768]{1,0:T(8,128)(2,1)S(1)}, bf16[136,768]{1,0:T(8,128)(2,1)S(1)}, u32[]{:S(2)}, u32[]{:S(2)}) %collective-permute-start.5) | collective-permute-done | bytes 208928 | tf_op jit(solution)/shard_map/ppermute | solution.py:29
  35.4 1.5 %collective-permute-done.6.rest_5_ = bf16[136,768]{1,0:T(8,128)(2,1)S(1)} collective-permute-done((bf16[136,768]{1,0:T(8,128)(2,1)S(1)}, bf16[136,768]{1,0:T(8,128)(2,1)S(1)}, u32[]{:S(2)}, u32[]{:S(2)}) %collective-permute-start.6) | collective-permute-done | bytes 208928 | tf_op jit(solution)/shard_map/ppermute | solution.py:29
  36.9 9.9 %collective-permute-done.7.rest_6_ = bf16[136,768]{1,0:T(8,128)(2,1)S(1)} collective-permute-done((bf16[136,768]{1,0:T(8,128)(2,1)S(1)}, bf16[136,768]{1,0:T(8,128)(2,1)S(1)}, u32[]{:S(2)}, u32[]{:S(2)}) %collective-permute-start.7) | collective-permute-done | bytes 208928 | tf_op jit(solution)/shard_map/ppermute | solution.py:29
  46.9 0.7 copy-done.7
  47.5 20.1 %shard_map.109 = bf16[128,768]{1,0:T(8,128)(2,1)} custom-call(s32[7]{0:T(128)} %convert_element_type.70.needed_ref, f32[12]{0:T(128)} %broadcast_multiply_fusion.2.scale_ref, bf16[128,768]{1,0:T(8,128)(2,1)} %copy.17.q_ref, bf16[136,768]{1,0:T(8,128)(2,1)} %copy-done.2, bf16[136,768]{1,0:T(8,128)(2,1)} %copy-done.3, bf16[136,768]{1,0:T(8,128)(2,1)} %copy-done.4, ...), custom_call_target="tpu_custom_call" | custom-call | tf_op jit(solution)/shard_map/pallas_call | solution.py:202
  (27 shorter events, 0.1 us)
Async XLA Ops:
  3.3 6.3 %collective-permute-start = (bf16[128,768]{1,0:T(8,128)(2,1)S(1)}, bf16[128,768]{1,0:T(8,128)(2,1)S(1)}, u32[]{:S(2)}, u32[]{:S(2)}) collective-permute-start(bf16[128,768]{1,0:T(8,128)(2,1)S(1)} %fusion.5), channel_id=1, source_target_pairs={{0,1},{1,0},{2,3},{3,2},{4,5},{5,4},{6,7},{7,6},{8,9},{9,8},{10,11... | collective-permute-start | bytes 589832 | tf_op jit(solution)/shard_map/ppermute | solution.py:23
  4.0 4.7 %collective-permute-start.1 = (bf16[4]{0:T(256)(128)(2,1)S(1)}, bf16[4]{0:T(256)(128)(2,1)S(1)}, u32[]{:S(2)}, u32[]{:S(2)}) collective-permute-start(bf16[4]{0:T(256)(128)(2,1)S(1)} %convert_bitcast_fusion), channel_id=1, source_target_pairs={{0,1},{1,0},{2,3},{3,2},{4,5},{5,4},{6,7},{7,6},{8,9},{9,8},{10,11... | collective-permute-start | bytes 32 | tf_op jit(solution)/shard_map/ppermute | solution.py:23
  4.6 1.6 %copy-start = (bf16[1,128,768]{2,1,0:T(8,128)(2,1)S(1)}, bf16[1,128,768]{2,1,0:T(8,128)(2,1)}, u32[]{:S(2)}) copy-start(bf16[1,128,768]{2,1,0:T(8,128)(2,1)} %param.13) | copy-start | bytes 589828
  4.6 1.6 %copy-start.8 = (f32[768]{0:T(1024)S(1)}, f32[768]{0:T(1024)}, u32[]{:S(2)}) copy-start(f32[768]{0:T(1024)} %param.14) | copy-start | bytes 9220
  6.2 1.7 %copy-start.10 = (s32[1,4]{1,0:T(1,128)S(1)}, s32[1,4]{1,0:T(1,128)}, u32[]{:S(2)}) copy-start(s32[1,4]{1,0:T(1,128)} %param.20) | copy-start | bytes 52
  6.2 1.7 %copy-start.9 = (s32[7]{0:T(128)S(1)}, s32[7]{0:T(128)}, u32[]{:S(2)}) copy-start(s32[7]{0:T(128)} %constant.131.clone) | copy-start | bytes 88
  6.8 1.3 %copy-start.11 = (s32[1,1,4]{2,1,0:T(1,128)S(1)}, s32[1,1,4]{2,1,0:T(1,128)}, u32[]{:S(2)}) copy-start(s32[1,1,4]{2,1,0:T(1,128)} %param.22) | copy-start | bytes 52
  7.9 21.7 %copy-start.12 = (f32[12]{0:T(128)S(1)}, f32[12]{0:T(128)}, u32[]{:S(2)}) copy-start(f32[12]{0:T(128)} %param.19) | copy-start | bytes 148
  10.2 36.7 %copy-start.1 = (bf16[136,768]{1,0:T(8,128)(2,1)}, bf16[136,768]{1,0:T(8,128)(2,1)S(1)}, u32[]{:S(2)}) copy-start(bf16[136,768]{1,0:T(8,128)(2,1)S(1)} %pad_maximum_fusion.rest_3_) | copy-start | bytes 626692
  10.2 18.1 %collective-permute-start.2 = (bf16[136,768]{1,0:T(8,128)(2,1)S(1)}, bf16[136,768]{1,0:T(8,128)(2,1)S(1)}, u32[]{:S(2)}, u32[]{:S(2)}) collective-permute-start(bf16[136,768]{1,0:T(8,128)(2,1)S(1)} %pad_maximum_fusion.rest_3_), channel_id=1, source_target_pairs={{0,6},{2,8},{4,10},{6,12},{8,14},{1,7},{3,9},{5,11},{7,13},{9,15},... | collective-permute-start | bytes 626696 | tf_op jit(solution)/shard_map/ppermute | solution.py:29
  17.7 12.5 %collective-permute-start.3 = (bf16[136,768]{1,0:T(8,128)(2,1)S(1)}, bf16[136,768]{1,0:T(8,128)(2,1)S(1)}, u32[]{:S(2)}, u32[]{:S(2)}) collective-permute-start(bf16[136,768]{1,0:T(8,128)(2,1)S(1)} %pad_maximum_fusion.rest_3_), channel_id=1, source_target_pairs={{0,4},{2,6},{4,8},{6,10},{8,12},{10,14},{1,5},{3,7},{5,9},{7,11},{... | collective-permute-start | bytes 626696 | tf_op jit(solution)/shard_map/ppermute | solution.py:29
  21.1 11.5 %collective-permute-start.4 = (bf16[136,768]{1,0:T(8,128)(2,1)S(1)}, bf16[136,768]{1,0:T(8,128)(2,1)S(1)}, u32[]{:S(2)}, u32[]{:S(2)}) collective-permute-start(bf16[136,768]{1,0:T(8,128)(2,1)S(1)} %pad_maximum_fusion.rest_3_), channel_id=1, source_target_pairs={{0,2},{2,4},{4,6},{6,8},{8,10},{10,12},{12,14},{1,3},{3,5},{5,7},{... | collective-permute-start | bytes 626696 | tf_op jit(solution)/shard_map/ppermute | solution.py:29
  24.6 10.8 %collective-permute-start.5 = (bf16[136,768]{1,0:T(8,128)(2,1)S(1)}, bf16[136,768]{1,0:T(8,128)(2,1)S(1)}, u32[]{:S(2)}, u32[]{:S(2)}) collective-permute-start(bf16[136,768]{1,0:T(8,128)(2,1)S(1)} %pad_maximum_fusion.rest_3_), channel_id=1, source_target_pairs={{2,0},{4,2},{6,4},{8,6},{10,8},{12,10},{14,12},{3,1},{5,3},{7,5},{... | collective-permute-start | bytes 626696 | tf_op jit(solution)/shard_map/ppermute | solution.py:29
  27.0 9.9 %collective-permute-start.6 = (bf16[136,768]{1,0:T(8,128)(2,1)S(1)}, bf16[136,768]{1,0:T(8,128)(2,1)S(1)}, u32[]{:S(2)}, u32[]{:S(2)}) collective-permute-start(bf16[136,768]{1,0:T(8,128)(2,1)S(1)} %pad_maximum_fusion.rest_3_), channel_id=1, source_target_pairs={{4,0},{6,2},{8,4},{10,6},{12,8},{14,10},{5,1},{7,3},{9,5},{11,7},{... | collective-permute-start | bytes 626696 | tf_op jit(solution)/shard_map/ppermute | solution.py:29
  28.3 18.5 %copy-start.2 = (bf16[136,768]{1,0:T(8,128)(2,1)}, bf16[136,768]{1,0:T(8,128)(2,1)S(1)}, u32[]{:S(2)}) copy-start(bf16[136,768]{1,0:T(8,128)(2,1)S(1)} %collective-permute-done.2.rest_0_) | copy-start | bytes 626692
  28.3 18.5 %collective-permute-start.7 = (bf16[136,768]{1,0:T(8,128)(2,1)S(1)}, bf16[136,768]{1,0:T(8,128)(2,1)S(1)}, u32[]{:S(2)}, u32[]{:S(2)}) collective-permute-start(bf16[136,768]{1,0:T(8,128)(2,1)S(1)} %pad_maximum_fusion.rest_3_), channel_id=1, source_target_pairs={{6,0},{8,2},{10,4},{12,6},{14,8},{7,1},{9,3},{11,5},{13,7},{15,9},... | collective-permute-start | bytes 626696 | tf_op jit(solution)/shard_map/ppermute | solution.py:29
  30.2 16.7 %copy-start.3 = (bf16[136,768]{1,0:T(8,128)(2,1)}, bf16[136,768]{1,0:T(8,128)(2,1)S(1)}, u32[]{:S(2)}) copy-start(bf16[136,768]{1,0:T(8,128)(2,1)S(1)} %collective-permute-done.3.rest_1_) | copy-start | bytes 626692
  32.7 14.2 %copy-start.4 = (bf16[136,768]{1,0:T(8,128)(2,1)}, bf16[136,768]{1,0:T(8,128)(2,1)S(1)}, u32[]{:S(2)}) copy-start(bf16[136,768]{1,0:T(8,128)(2,1)S(1)} %collective-permute-done.4.rest_2_) | copy-start | bytes 626692
  35.4 11.4 %copy-start.5 = (bf16[136,768]{1,0:T(8,128)(2,1)}, bf16[136,768]{1,0:T(8,128)(2,1)S(1)}, u32[]{:S(2)}) copy-start(bf16[136,768]{1,0:T(8,128)(2,1)S(1)} %collective-permute-done.5.rest_4_) | copy-start | bytes 626692
  36.9 9.9 %copy-start.6 = (bf16[136,768]{1,0:T(8,128)(2,1)}, bf16[136,768]{1,0:T(8,128)(2,1)S(1)}, u32[]{:S(2)}) copy-start(bf16[136,768]{1,0:T(8,128)(2,1)S(1)} %collective-permute-done.6.rest_5_) | copy-start | bytes 626692
  46.8 0.7 %copy-start.7 = (bf16[136,768]{1,0:T(8,128)(2,1)}, bf16[136,768]{1,0:T(8,128)(2,1)S(1)}, u32[]{:S(2)}) copy-start(bf16[136,768]{1,0:T(8,128)(2,1)S(1)} %collective-permute-done.7.rest_6_) | copy-start | bytes 626692

commit v2 on v1

--- a/solution.py
+++ b/solution.py
@@ -21,12 +21,6 @@
         if high != low and high < count:
             route += [(low, high), (high, low)]
     return lax.ppermute(block, axis, route)
-
-
-def from_offset(shard, axis, by):
-    size = lax.axis_size(axis)
-    pairs = [(i + by, i) for i in range(size) if 0 <= i + by < size]
-    return lax.ppermute(shard, axis, pairs)
 
 
 def layer_norm(floated, norm_gain):
@@ -89,10 +83,11 @@
     return cosine, signed
 
 
-def make_kernel(slots, heads, head_dim, count_rows, width):
+def make_band_kernel(slots, heads, head_dim, count_rows, width):
     pairs = width // 128
     quarter = head_dim // 4
     per_pair = 128 // head_dim
+    stacked = per_pair * count_rows
 
     def kernel(needed_ref, scale_ref, q_ref, *rest):
         payload_refs = rest[:slots]
@@ -103,6 +98,7 @@
         lane = lax.broadcasted_iota(jnp.int32, (count_rows, 128), 1)
         first = (lane % (2 * quarter)) < quarter
         head_of_lane = lane // head_dim
+        row = lax.broadcasted_iota(jnp.int32, (stacked, 1), 0)
 
         for slot in range(slots):
 
@@ -122,35 +118,32 @@
                     k_pair = (x * cosine + other * signed).astype(jnp.bfloat16)
                     v_pair = vp[:, lo:lo + 128]
                     q_pair = q_ref[:, lo:lo + 128]
-                    acc_pair = acc_ref[:, lo:lo + 128]
-                    new_acc = acc_pair
+                    q_two = jnp.concatenate(
+                        [jnp.where(head_of_lane == sub, q_pair, jnp.zeros_like(q_pair))
+                         for sub in range(per_pair)], axis=0)
+                    scale_col = jnp.zeros((stacked, 1), jnp.float32)
                     for sub in range(per_pair):
-                        h = p * per_pair + sub
-                        mine = head_of_lane == sub
-                        q_h = jnp.where(mine, q_pair, jnp.zeros_like(q_pair))
-                        scores = lax.dot_general(
-                            q_h, k_pair, (((1,), (1,)), ((), ())),
-                            preferred_element_type=jnp.float32,
-                        ) * scale_ref[h]
-                        scores = jnp.where(live > 0, scores, jnp.float32(NEG))
-                        best = m_ref[h]
-                        fresh = jnp.maximum(best, jnp.max(scores, axis=1, keepdims=True))
-                        decay = jnp.exp(best - fresh)
-                        weights = jnp.exp(scores - fresh)
-                        l_ref[h] = l_ref[h] * decay + jnp.sum(weights, axis=1, keepdims=True)
-                        m_ref[h] = fresh
-                        pv = jnp.dot(weights.astype(jnp.bfloat16), v_pair, preferred_element_type=jnp.float32)
-                        new_acc = jnp.where(mine, acc_pair * decay + pv, new_acc)
-                    acc_ref[:, lo:lo + 128] = new_acc
+                        scale_col = jnp.where(row // count_rows == sub, scale_ref[p * per_pair + sub], scale_col)
+                    scores = lax.dot_general(
+                        q_two, k_pair, (((1,), (1,)), ((), ())),
+                        preferred_element_type=jnp.float32,
+                    ) * scale_col
+                    scores = jnp.where(live > 0, scores, jnp.float32(NEG))
+                    best = m_ref[p]
+                    fresh = jnp.maximum(best, jnp.max(scores, axis=1, keepdims=True))
+                    decay = jnp.exp(best - fresh)
+                    weights = jnp.exp(scores - fresh)
+                    l_ref[p] = l_ref[p] * decay + jnp.sum(weights, axis=1, keepdims=True)
+                    m_ref[p] = fresh
+                    pv = jnp.dot(weights.astype(jnp.bfloat16), v_pair, preferred_element_type=jnp.float32)
+                    acc_ref[p] = acc_ref[p] * decay + pv
 
         parts = []
         for p in range(pairs):
-            lo = p * 128
-            acc_pair = acc_ref[:, lo:lo + 128]
-            res = acc_pair
-            for sub in range(per_pair):
-                h = p * per_pair + sub
-                res = jnp.where(head_of_lane == sub, acc_pair / l_ref[h], res)
+            acc_two = acc_ref[p] / l_ref[p]
+            res = acc_two[0:count_rows]
+            for sub in range(1, per_pair):
+                res = jnp.where(head_of_lane == sub, acc_two[sub * count_rows:(sub + 1) * count_rows], res)
             parts.append(res.astype(jnp.bfloat16))
         attended = jnp.concatenate(parts, axis=1)
         mixed = tok_ref[...].astype(jnp.float32) + jnp.dot(
@@ -161,55 +154,114 @@
     return kernel
 
 
+def make_query_kernel(head_dim):
+    quarter = head_dim // 4
+
+    def kernel(x_ref, w_ref, cos_ref, sin_ref, out_ref):
+        proj = jnp.dot(x_ref[...], w_ref[...], preferred_element_type=jnp.float32)
+        lane = lax.broadcasted_iota(jnp.int32, (proj.shape[0], 128), 1)
+        first = (lane % (2 * quarter)) < quarter
+        cosine = cos_ref[...]
+        signed = sin_ref[...]
+        for p in range(proj.shape[1] // 128):
+            lo = p * 128
+            x = proj[:, lo:lo + 128]
+            other = jnp.where(first, pltpu.roll(x, 128 - quarter, 1), pltpu.roll(x, quarter, 1))
+            out_ref[:, lo:lo + 128] = (x * cosine + other * signed).astype(out_ref.dtype)
+
+    return kernel
+
+
+def make_prep_kernel(tile_count, tile_rows, count_rows):
+    def kernel(order_ref, count_ref, tok_ref, gain_ref, normed_ref, out_ref):
+        floated = tok_ref[...].astype(jnp.float32)
+        normed_ref[...] = layer_norm(floated, gain_ref[...]).astype(normed_ref.dtype)
+        lane = lax.broadcasted_iota(jnp.int32, (META_ROWS, 128), 1)
+        row = lax.broadcasted_iota(jnp.int32, (META_ROWS, 128), 0)
+        live = jnp.zeros((META_ROWS, 128), jnp.float32)
+        for s in range(tile_count):
+            src = order_ref[s]
+            start = pl.multiple_of(src * tile_rows, tile_rows)
+            out_ref[s * tile_rows:(s + 1) * tile_rows, :] = normed_ref[pl.ds(start, tile_rows), :]
+            inside = (lane // tile_rows == s) & ((lane % tile_rows) < count_ref[src]) & (row == 0)
+            live = jnp.where(inside, jnp.float32(1), live)
+        out_ref[count_rows:count_rows + META_ROWS, :] = jnp.zeros(
+            (META_ROWS, out_ref.shape[1]), out_ref.dtype)
+        out_ref[count_rows:count_rows + META_ROWS, 0:128] = live.astype(out_ref.dtype)
+
+    return kernel
+
+
+def across(shard, by):
+    size = lax.axis_size("tok")
+    epochs = lax.axis_size("ep")
+    pairs = [
+        ((i + by) * epochs + (epochs - 1 - e), i * epochs + e)
+        for i in range(size)
+        for e in range(epochs)
+        if 0 <= i + by < size
+    ]
+    return lax.ppermute(shard, ("tok", "ep"), pairs)
+
+
+def full_spec(shape):
+    return pl.BlockSpec(shape, lambda i: (0,) * len(shape))
+
+
 def on_device(
     tokens, norm_gain, query_weight, w_key, w_value, w_out, head_scale, matching, valid, stops
 ):
-    floated = tokens[0].astype(jnp.float32)
-    count_rows, width = floated.shape
+    count_rows, width = tokens.shape[1:]
     heads = head_scale.shape[0]
     head_dim = width // heads
     block_index = lax.axis_index("tok")
-    normed = layer_norm(floated, norm_gain).astype(jnp.bfloat16)
-    row_ids = jnp.arange(count_rows, dtype=jnp.int32)
-    patch_coordinates = block_index * count_rows + row_ids
-    queries = rotate(
-        jnp.dot(normed, query_weight, preferred_element_type=jnp.float32), patch_coordinates, heads
-    ).astype(jnp.bfloat16)
-    partner_rows, partner_counts = partner((normed, valid[0].astype(jnp.bfloat16)), "ep", 0)
+    smem = pl.BlockSpec(memory_space=pltpu.SMEM)
+    vmem = pl.BlockSpec(memory_space=pltpu.VMEM)
+    theirs = partner(matching[0], "ep", 0)
     tile_count = matching.shape[1]
     tile_rows = count_rows // tile_count
-    order = matching[0]
-    key_rows = partner_rows.reshape(tile_count, tile_rows, width)[order].reshape(count_rows, width)
-    counts = partner_counts[order].astype(jnp.float32)
-    live = (
-        (jnp.arange(tile_rows, dtype=jnp.float32)[None, :] < counts[:, None])
-        .reshape(count_rows)
-        .astype(jnp.bfloat16)
-    )
-    meta = jnp.zeros((META_ROWS, width), jnp.bfloat16).at[0, :count_rows].set(live)
-    payload = jnp.concatenate([key_rows, meta], axis=0)
+    normed, payload = pl.pallas_call(
+        make_prep_kernel(tile_count, tile_rows, count_rows),
+        out_shape=(
+            jax.ShapeDtypeStruct((count_rows, width), jnp.bfloat16),
+            jax.ShapeDtypeStruct((count_rows + META_ROWS, width), jnp.bfloat16),
+        ),
+        in_specs=[smem, smem, vmem, vmem],
+        out_specs=(vmem, vmem),
+    )(theirs, valid[0], tokens[0], norm_gain.reshape(1, width))
 
     offsets = list(range(-BAND, BAND + 1))
-    received = [payload if d == 0 else from_offset(payload, "tok", d) for d in offsets]
     blocks = block_index + jnp.array(offsets, dtype=jnp.int32)
-    needed = jnp.any(stops[0, 0][None, :] == blocks[:, None], axis=1).astype(jnp.int32)
+    needed = jnp.any(stops[0, 0][None, :] == blocks[:, None], axis=1)
     cosine, signed = angle_tables(blocks, count_rows, head_dim)
     scales = (head_scale / math.sqrt(head_dim)).astype(jnp.float32)
+    own = offsets.index(0)
+    table_spec = pl.BlockSpec((None, count_rows, 128), lambda i: (own, 0, 0))
+
+    queries = pl.pallas_call(
+        make_query_kernel(head_dim),
+        out_shape=jax.ShapeDtypeStruct((count_rows, width), jnp.bfloat16),
+        grid=(1,),
+        in_specs=[full_spec((count_rows, width)), full_spec((width, width)), table_spec, table_spec],
+        out_specs=full_spec((count_rows, width)),
+    )(normed, query_weight, cosine, signed)
 
     slots = len(offsets)
-    smem = pl.BlockSpec(memory_space=pltpu.SMEM)
-    vmem = pl.BlockSpec(memory_space=pltpu.VMEM)
+    received = [partner(payload, "ep", 0) if d == 0 else across(payload, d) for d in offsets]
+    pairs = width // 128
+    stacked = (128 // head_dim) * count_rows
     out = pl.pallas_call(
-        make_kernel(slots, heads, head_dim, count_rows, width),
+        make_band_kernel(slots, heads, head_dim, count_rows, width),
         out_shape=jax.ShapeDtypeStruct((count_rows, width), jnp.bfloat16),
         in_specs=[smem, smem] + [vmem] * (1 + slots + 6),
         out_specs=vmem,
         scratch_shapes=[
-            pltpu.VMEM((count_rows, width), jnp.float32),
-            pltpu.VMEM((heads, count_rows, 1), jnp.float32),
-            pltpu.VMEM((heads, count_rows, 1), jnp.float32),
+            pltpu.VMEM((pairs, stacked, 128), jnp.float32),
+            pltpu.VMEM((pairs, stacked, 1), jnp.float32),
+            pltpu.VMEM((pairs, stacked, 1), jnp.float32),
         ],
-    )(needed, scales, queries, *received, cosine, signed, w_key, w_value, w_out, tokens[0])
+    )(needed.astype(jnp.int32), scales, queries, *received, cosine, signed, w_key, w_value, w_out,
+      tokens[0])
     return out[None]
 
 

time: 68 us -> 57.7 us (0.85)
  the two profiles are of different devices: /device:TPU:4 before, /device:TPU:27 now
where the time goes in v2:
time: 57.7 us; the launch traced here: 57.3 us
  Pallas kernels  20.4 us (35%)
  waiting for transfers between devices  14.5 us (25%)
  starting transfers between devices  14.2 us (25%)
  other arithmetic  5.58 us (10%)
  local copies, waits for them, and re-layouts  2.57 us (4%)
    pallas_call x1, Pallas kernels, on_device(): pl.pallas_call(make_band_kernel(slots, heads, head_dim, count_rows, width...  16 us
    ppermute x6, waiting for transfers between devices, across(): return lax.ppermute(shard, ('tok', 'ep'), pairs)  14.5 us
    ppermute x6, starting transfers between devices, across(): return lax.ppermute(shard, ('tok', 'ep'), pairs)  12.9 us
    select_n x1, other arithmetic, angle_tables(): signed = jnp.where(first[None, None, :], -sine, sine)  3.04 us
    pallas_call x1, Pallas kernels, on_device(): pl.pallas_call(make_query_kernel(head_dim), out_shape=jax.ShapeDtypeStruc...  2.45 us
    pallas_call x1, Pallas kernels, on_device(): pl.pallas_call(make_prep_kernel(tile_count, tile_rows, count_rows), out_s...  1.92 us
    reshape x1, local copies, waits for them, and re-layouts, on_device(): norm_gain.reshape(1, width)  1.28 us
    ppermute x2, starting transfers between devices, partner(): return lax.ppermute(block, axis, route)  1.24 us
  transfers between devices with their start and end apart: 8, of which 3 were waited for; matrix products, arithmetic and copies ran while one was open for 12% of the time, Pallas kernels for 4%

profile of v2, /device:TPU:27, one launch (start us, length us, event | category | flops | bytes accessed | tf_op | source)
XLA Modules:
  0.0 57.3 jit_solution(18130649549881600525)
XLA Ops:
  0.0 0.0 copy-start.8
  0.0 0.7 %collective-permute-start = (s32[4]{0:T(128)}, s32[4]{0:T(128)S(1)}, u32[]{:S(2)}, u32[]{:S(2)}) collective-permute-start(s32[4]{0:T(128)} %bitcast.9), channel_id=1, source_target_pairs={{0,1},{1,0},{2,3},{3,2},{4,5},{5,4},{6,7},{7,6},{8,9},{9,8},{10,11... | collective-permute-start | bytes 56 | tf_op jit(solution)/shard_map/ppermute | solution.py:23
  0.7 0.7 %broadcast_multiply_fusion = (s32[7]{0:T(128)S(1)}, s32[7]{0:T(128)S(1)}) fusion(s32[7]{0:T(128)} %constant.78.clone, s32[]{:T(128)S(6)} %axis_index.15), kind=kLoop, calls=%fused_computation.23 | loop fusion | flops 14 | bytes 88 | tf_op jit(solution)/shard_map/mul | solution.py:70
  1.4 0.7 %compare_reduce_fusion = pred[7]{0:T(512)(128)(4,1)S(1)} fusion(s32[7]{0:T(128)S(1)} %get-tuple-element.14, s32[4]{0:T(128)} %bitcast.8), kind=kLoop, calls=%fused_computation.19 | loop fusion | flops 49 | bytes 51 | tf_op jit(solution)/shard_map/reduce_or | solution.py:235
  2.1 0.5 convert_element_type.17.needed_ref
  2.6 1.3 %reshape.99.gain_ref = f32[1,768]{1,0:T(1,128)} reshape(f32[768]{0:T(1024)} %param.12) | data formatting | bytes 6144 | tf_op jit(solution)/shard_map/reshape | solution.py:231
  3.9 0.1 mul.15
  4.0 0.1 fusion.1
  4.1 0.0 collective-permute-done.order_ref
  4.1 0.0 copy-start.7
  4.1 0.5 copy-done.7
  4.6 1.9 %shard_map.109 = (bf16[128,768]{1,0:T(8,128)(2,1)}, bf16[136,768]{1,0:T(8,128)(2,1)}) custom-call(s32[4]{0:T(128)} %copy-done.7, s32[4]{0:T(128)} %bitcast.7, bf16[128,768]{1,0:T(8,128)(2,1)} %bitcast.5, f32[1,768]{1,0:T(1,128)} %reshape.99.gain_ref), custom_call_target="tpu_custom_call" | custom-call | tf_op jit(solution)/shard_map/pallas_call | solution.py:223
  6.5 2.8 %collective-permute-start.7 = (bf16[136,768]{1,0:T(8,128)(2,1)}, bf16[136,768]{1,0:T(8,128)(2,1)S(1)}, u32[]{:S(2)}, u32[]{:S(2)}) collective-permute-start(bf16[136,768]{1,0:T(8,128)(2,1)} %get-tuple-element.8), channel_id=1, source_target_pairs={{7,0},{6,1},{9,2},{8,3},{11,4},{10,5},{13,6},{12,7},{15,8},{14,9},... | collective-permute-start | bytes 626696 | tf_op jit(solution)/shard_map/ppermute | solution.py:204
  9.3 2.5 %collective-permute-start.6 = (bf16[136,768]{1,0:T(8,128)(2,1)}, bf16[136,768]{1,0:T(8,128)(2,1)S(1)}, u32[]{:S(2)}, u32[]{:S(2)}) collective-permute-start(bf16[136,768]{1,0:T(8,128)(2,1)} %get-tuple-element.8), channel_id=1, source_target_pairs={{5,0},{4,1},{7,2},{6,3},{9,4},{8,5},{11,6},{10,7},{13,8},{12,9},{1... | collective-permute-start | bytes 626696 | tf_op jit(solution)/shard_map/ppermute | solution.py:204
  11.8 3.0 %negate_select_fusion = (f32[7,128,128]{2,1,0:T(8,128)}, f32[7,128,128]{2,1,0:T(8,128)}) fusion(f32[128]{0:T(128)S(1)} %mul.15, f32[7,128]{1,0:T(8,128)S(1)} %get-tuple-element.12, f32[7,128]{1,0:T(8,128)S(1)} %get-tuple-element.11, pred[128]{0:T(512)(128)(4,1)S(1)} %get-tuple-element.16, pred[128]{0:T(512)(128)(4,1)S(1)} %get-tuple-element.15), kind=kLoop, calls=%fused_computation | loop fusion | flops 458752 | bytes 925440 | tf_op jit(solution)/shard_map/jit(_where)/select_n | solution.py:82
  14.8 2.0 %collective-permute-start.5 = (bf16[136,768]{1,0:T(8,128)(2,1)}, bf16[136,768]{1,0:T(8,128)(2,1)S(1)}, u32[]{:S(2)}, u32[]{:S(2)}) collective-permute-start(bf16[136,768]{1,0:T(8,128)(2,1)} %get-tuple-element.8), channel_id=1, source_target_pairs={{3,0},{2,1},{5,2},{4,3},{7,4},{6,5},{9,6},{8,7},{11,8},{10,9},{13,... | collective-permute-start | bytes 626696 | tf_op jit(solution)/shard_map/ppermute | solution.py:204
  16.9 0.6 collective-permute-start.4
  17.4 3.1 %collective-permute-start.3 = (bf16[136,768]{1,0:T(8,128)(2,1)}, bf16[136,768]{1,0:T(8,128)(2,1)S(1)}, u32[]{:S(2)}, u32[]{:S(2)}) collective-permute-start(bf16[136,768]{1,0:T(8,128)(2,1)} %get-tuple-element.8), channel_id=1, source_target_pairs={{1,2},{0,3},{3,4},{2,5},{5,6},{4,7},{7,8},{6,9},{9,10},{8,11},{11,... | collective-permute-start | bytes 626696 | tf_op jit(solution)/shard_map/ppermute | solution.py:204
  20.5 0.0 collective-permute-done.7.rest_6_
  20.5 0.0 copy-start
  20.5 1.3 %collective-permute-start.2 = (bf16[136,768]{1,0:T(8,128)(2,1)}, bf16[136,768]{1,0:T(8,128)(2,1)S(1)}, u32[]{:S(2)}, u32[]{:S(2)}) collective-permute-start(bf16[136,768]{1,0:T(8,128)(2,1)} %get-tuple-element.8), channel_id=1, source_target_pairs={{1,4},{0,5},{3,6},{2,7},{5,8},{4,9},{7,10},{6,11},{9,12},{8,13},{1... | collective-permute-start | bytes 626696 | tf_op jit(solution)/shard_map/ppermute | solution.py:204
  21.8 0.0 collective-permute-done.6.rest_5_
  21.8 0.0 copy-start.1
  21.8 1.3 %collective-permute-start.1 = (bf16[136,768]{1,0:T(8,128)(2,1)}, bf16[136,768]{1,0:T(8,128)(2,1)S(1)}, u32[]{:S(2)}, u32[]{:S(2)}) collective-permute-start(bf16[136,768]{1,0:T(8,128)(2,1)} %get-tuple-element.8), channel_id=1, source_target_pairs={{1,6},{0,7},{3,8},{2,9},{5,10},{4,11},{7,12},{6,13},{9,14},{8,15},... | collective-permute-start | bytes 626696 | tf_op jit(solution)/shard_map/ppermute | solution.py:204
  23.1 0.0 copy-done.8
  23.2 0.5 broadcast_multiply_fusion.1.scale_ref
  23.7 2.4 %shard_map.110.q_ref = bf16[128,768]{1,0:T(8,128)(2,1)} custom-call(bf16[128,768]{1,0:T(8,128)(2,1)} %get-tuple-element.7.x_ref, bf16[768,768]{1,0:T(8,128)(2,1)} %w_ref.1, f32[7,128,128]{2,1,0:T(8,128)} %get-tuple-element.10.cos_ref.rest_7_, f32[7,128,128]{2,1,0:T(8,128)} %get-tuple-element.9.sin_ref.rest_8_), custom_call_target="tpu_custom_call" | custom-call | tf_op jit(solution)/shard_map/pallas_call | solution.py:241
  26.1 0.0 copy-done
  26.1 0.0 copy-done.1
  26.1 2.4 %collective-permute-done.5.rest_4_ = bf16[136,768]{1,0:T(8,128)(2,1)S(1)} collective-permute-done((bf16[136,768]{1,0:T(8,128)(2,1)}, bf16[136,768]{1,0:T(8,128)(2,1)S(1)}, u32[]{:S(2)}, u32[]{:S(2)}) %collective-permute-start.5) | collective-permute-done | bytes 208928 | tf_op jit(solution)/shard_map/ppermute | solution.py:204
  28.5 0.0 copy-start.2
  28.5 0.0 collective-permute-done.4.rest_3_
  28.5 0.0 copy-start.3
  28.5 0.0 collective-permute-done.3.rest_2_
  28.5 0.0 copy-start.4
  28.5 1.6 %collective-permute-done.2.rest_1_ = bf16[136,768]{1,0:T(8,128)(2,1)S(1)} collective-permute-done((bf16[136,768]{1,0:T(8,128)(2,1)}, bf16[136,768]{1,0:T(8,128)(2,1)S(1)}, u32[]{:S(2)}, u32[]{:S(2)}) %collective-permute-start.2) | collective-permute-done | bytes 208928 | tf_op jit(solution)/shard_map/ppermute | solution.py:204
  30.1 0.0 copy-start.5
  30.1 10.5 %collective-permute-done.1.rest_0_ = bf16[136,768]{1,0:T(8,128)(2,1)S(1)} collective-permute-done((bf16[136,768]{1,0:T(8,128)(2,1)}, bf16[136,768]{1,0:T(8,128)(2,1)S(1)}, u32[]{:S(2)}, u32[]{:S(2)}) %collective-permute-start.1) | collective-permute-done | bytes 208928 | tf_op jit(solution)/shard_map/ppermute | solution.py:204
  40.6 0.0 copy-done.2
  40.6 0.0 copy-done.3
  40.6 0.0 copy-done.4
  40.6 0.0 copy-done.5
  40.6 0.0 copy-start.6
  40.6 0.7 %copy-done.6 = bf16[136,768]{1,0:T(8,128)(2,1)} copy-done((bf16[136,768]{1,0:T(8,128)(2,1)}, bf16[136,768]{1,0:T(8,128)(2,1)S(1)}, u32[]{:S(2)}) %copy-start.6) | copy-done | bytes 208920
  41.3 16.0 %shard_map.111 = bf16[128,768]{1,0:T(8,128)(2,1)} custom-call(s32[7]{0:T(128)} %convert_element_type.17.needed_ref, f32[12]{0:T(128)} %broadcast_multiply_fusion.1.scale_ref, bf16[128,768]{1,0:T(8,128)(2,1)} %shard_map.110.q_ref, bf16[136,768]{1,0:T(8,128)(2,1)} %copy-done.6, bf16[136,768]{1,0:T(8,128)(2,1)} %copy-done.5, bf16[136,768]{1,0:T(8,128)(2,1)} %copy-done.4, ...), custom_call_target="tpu_custom_call" | custom-call | tf_op jit(solution)/shard_map/pallas_call | solution.py:253
  (3 shorter events, 0.0 us)
Async XLA Ops:
  0.0 23.1 %copy-start.8 = (f32[12]{0:T(128)S(1)}, f32[12]{0:T(128)}, u32[]{:S(2)}) copy-start(f32[12]{0:T(128)} %param.17) | copy-start | bytes 148
  0.0 4.1 %collective-permute-start = (s32[4]{0:T(128)}, s32[4]{0:T(128)S(1)}, u32[]{:S(2)}, u32[]{:S(2)}) collective-permute-start(s32[4]{0:T(128)} %bitcast.9), channel_id=1, source_target_pairs={{0,1},{1,0},{2,3},{3,2},{4,5},{5,4},{6,7},{7,6},{8,9},{9,8},{10,11... | collective-permute-start | bytes 56 | tf_op jit(solution)/shard_map/ppermute | solution.py:23
  4.1 0.5 copy-start.7
  6.5 14.0 %collective-permute-start.7 = (bf16[136,768]{1,0:T(8,128)(2,1)}, bf16[136,768]{1,0:T(8,128)(2,1)S(1)}, u32[]{:S(2)}, u32[]{:S(2)}) collective-permute-start(bf16[136,768]{1,0:T(8,128)(2,1)} %get-tuple-element.8), channel_id=1, source_target_pairs={{7,0},{6,1},{9,2},{8,3},{11,4},{10,5},{13,6},{12,7},{15,8},{14,9},... | collective-permute-start | bytes 626696 | tf_op jit(solution)/shard_map/ppermute | solution.py:204
  9.3 12.5 %collective-permute-start.6 = (bf16[136,768]{1,0:T(8,128)(2,1)}, bf16[136,768]{1,0:T(8,128)(2,1)S(1)}, u32[]{:S(2)}, u32[]{:S(2)}) collective-permute-start(bf16[136,768]{1,0:T(8,128)(2,1)} %get-tuple-element.8), channel_id=1, source_target_pairs={{5,0},{4,1},{7,2},{6,3},{9,4},{8,5},{11,6},{10,7},{13,8},{12,9},{1... | collective-permute-start | bytes 626696 | tf_op jit(solution)/shard_map/ppermute | solution.py:204
  14.8 13.6 %collective-permute-start.5 = (bf16[136,768]{1,0:T(8,128)(2,1)}, bf16[136,768]{1,0:T(8,128)(2,1)S(1)}, u32[]{:S(2)}, u32[]{:S(2)}) collective-permute-start(bf16[136,768]{1,0:T(8,128)(2,1)} %get-tuple-element.8), channel_id=1, source_target_pairs={{3,0},{2,1},{5,2},{4,3},{7,4},{6,5},{9,6},{8,7},{11,8},{10,9},{13,... | collective-permute-start | bytes 626696 | tf_op jit(solution)/shard_map/ppermute | solution.py:204
  16.9 11.6 %collective-permute-start.4 = (bf16[136,768]{1,0:T(8,128)(2,1)}, bf16[136,768]{1,0:T(8,128)(2,1)S(1)}, u32[]{:S(2)}, u32[]{:S(2)}) collective-permute-start(bf16[136,768]{1,0:T(8,128)(2,1)} %get-tuple-element.8), channel_id=1, source_target_pairs={{0,1},{1,0},{2,3},{3,2},{4,5},{5,4},{6,7},{7,6},{8,9},{9,8},{10,11... | collective-permute-start | bytes 626696 | tf_op jit(solution)/shard_map/ppermute | solution.py:23
  17.4 11.1 %collective-permute-start.3 = (bf16[136,768]{1,0:T(8,128)(2,1)}, bf16[136,768]{1,0:T(8,128)(2,1)S(1)}, u32[]{:S(2)}, u32[]{:S(2)}) collective-permute-start(bf16[136,768]{1,0:T(8,128)(2,1)} %get-tuple-element.8), channel_id=1, source_target_pairs={{1,2},{0,3},{3,4},{2,5},{5,6},{4,7},{7,8},{6,9},{9,10},{8,11},{11,... | collective-permute-start | bytes 626696 | tf_op jit(solution)/shard_map/ppermute | solution.py:204
  20.5 5.6 %copy-start = (bf16[136,768]{1,0:T(8,128)(2,1)}, bf16[136,768]{1,0:T(8,128)(2,1)S(1)}, u32[]{:S(2)}) copy-start(bf16[136,768]{1,0:T(8,128)(2,1)S(1)} %collective-permute-done.7.rest_6_) | copy-start | bytes 626692
  20.5 9.6 %collective-permute-start.2 = (bf16[136,768]{1,0:T(8,128)(2,1)}, bf16[136,768]{1,0:T(8,128)(2,1)S(1)}, u32[]{:S(2)}, u32[]{:S(2)}) collective-permute-start(bf16[136,768]{1,0:T(8,128)(2,1)} %get-tuple-element.8), channel_id=1, source_target_pairs={{1,4},{0,5},{3,6},{2,7},{5,8},{4,9},{7,10},{6,11},{9,12},{8,13},{1... | collective-permute-start | bytes 626696 | tf_op jit(solution)/shard_map/ppermute | solution.py:204
  21.8 4.3 %copy-start.1 = (bf16[136,768]{1,0:T(8,128)(2,1)}, bf16[136,768]{1,0:T(8,128)(2,1)S(1)}, u32[]{:S(2)}) copy-start(bf16[136,768]{1,0:T(8,128)(2,1)S(1)} %collective-permute-done.6.rest_5_) | copy-start | bytes 626692
  21.8 18.8 %collective-permute-start.1 = (bf16[136,768]{1,0:T(8,128)(2,1)}, bf16[136,768]{1,0:T(8,128)(2,1)S(1)}, u32[]{:S(2)}, u32[]{:S(2)}) collective-permute-start(bf16[136,768]{1,0:T(8,128)(2,1)} %get-tuple-element.8), channel_id=1, source_target_pairs={{1,6},{0,7},{3,8},{2,9},{5,10},{4,11},{7,12},{6,13},{9,14},{8,15},... | collective-permute-start | bytes 626696 | tf_op jit(solution)/shard_map/ppermute | solution.py:204
  28.5 12.1 %copy-start.2 = (bf16[136,768]{1,0:T(8,128)(2,1)}, bf16[136,768]{1,0:T(8,128)(2,1)S(1)}, u32[]{:S(2)}) copy-start(bf16[136,768]{1,0:T(8,128)(2,1)S(1)} %collective-permute-done.5.rest_4_) | copy-start | bytes 626692
  28.5 12.1 %copy-start.3 = (bf16[136,768]{1,0:T(8,128)(2,1)}, bf16[136,768]{1,0:T(8,128)(2,1)S(1)}, u32[]{:S(2)}) copy-start(bf16[136,768]{1,0:T(8,128)(2,1)S(1)} %collective-permute-done.4.rest_3_) | copy-start | bytes 626692
  28.5 12.1 %copy-start.4 = (bf16[136,768]{1,0:T(8,128)(2,1)}, bf16[136,768]{1,0:T(8,128)(2,1)S(1)}, u32[]{:S(2)}) copy-start(bf16[136,768]{1,0:T(8,128)(2,1)S(1)} %collective-permute-done.3.rest_2_) | copy-start | bytes 626692
  30.1 10.5 %copy-start.5 = (bf16[136,768]{1,0:T(8,128)(2,1)}, bf16[136,768]{1,0:T(8,128)(2,1)S(1)}, u32[]{:S(2)}) copy-start(bf16[136,768]{1,0:T(8,128)(2,1)S(1)} %collective-permute-done.2.rest_1_) | copy-start | bytes 626692
  40.6 0.7 %copy-start.6 = (bf16[136,768]{1,0:T(8,128)(2,1)}, bf16[136,768]{1,0:T(8,128)(2,1)S(1)}, u32[]{:S(2)}) copy-start(bf16[136,768]{1,0:T(8,128)(2,1)S(1)} %collective-permute-done.1.rest_0_) | copy-start | bytes 626692

commit v3 on v2

--- a/solution.py
+++ b/solution.py
@@ -230,6 +230,8 @@
         out_specs=(vmem, vmem),
     )(theirs, valid[0], tokens[0], norm_gain.reshape(1, width))
 
+    _, stops, head_scale, block_index = lax.optimization_barrier(
+        (payload, stops, head_scale, block_index))
     offsets = list(range(-BAND, BAND + 1))
     blocks = block_index + jnp.array(offsets, dtype=jnp.int32)
     needed = jnp.any(stops[0, 0][None, :] == blocks[:, None], axis=1)

time: 57.7 us -> 59.1 us (1.024)
  waiting for transfers between devices: 14.5 us -> 15.8 us
    ppermute x6, waiting for transfers between devices: 14.5 us -> 15.8 us  [across(): return lax.ppermute(shard, ('tok', 'ep'), pairs)]
    unnamed x18 -> x20, local copies, waits for them, and re-layouts: 1.21 us -> 1.25 us
  transfers between devices with their start and end apart: 8 -> 8, of which waited for: 3 -> 2; matrix products, arithmetic and copies ran while one was open for 12% -> 12% of each run, Pallas kernels for 4% -> 4%
where the time goes in v3:
time: 59.1 us; the launch traced here: 58.8 us
  Pallas kernels  20.4 us (35%)
  waiting for transfers between devices  15.8 us (27%)
  starting transfers between devices  14.2 us (24%)
  other arithmetic  5.6 us (9%)
  local copies, waits for them, and re-layouts  2.61 us (4%)
    pallas_call x1, Pallas kernels, on_device(): pl.pallas_call(make_band_kernel(slots, heads, head_dim, count_rows, width...  16 us
    ppermute x6, waiting for transfers between devices, across(): return lax.ppermute(shard, ('tok', 'ep'), pairs)  15.8 us
    ppermute x6, starting transfers between devices, across(): return lax.ppermute(shard, ('tok', 'ep'), pairs)  12.9 us
    select_n x1, other arithmetic, angle_tables(): signed = jnp.where(first[None, None, :], -sine, sine)  3.05 us
    pallas_call x1, Pallas kernels, on_device(): pl.pallas_call(make_query_kernel(head_dim), out_shape=jax.ShapeDtypeStruc...  2.48 us
    pallas_call x1, Pallas kernels, on_device(): pl.pallas_call(make_prep_kernel(tile_count, tile_rows, count_rows), out_s...  1.94 us
    reshape x1, local copies, waits for them, and re-layouts, on_device(): norm_gain.reshape(1, width)  1.28 us
    unnamed x20, local copies, waits for them, and re-layouts  1.25 us
  transfers between devices with their start and end apart: 8, of which 2 were waited for; matrix products, arithmetic and copies ran while one was open for 12% of the time, Pallas kernels for 4%

profile of v3, /device:TPU:27, one launch (start us, length us, event | category | flops | bytes accessed | tf_op | source)
XLA Modules:
  0.0 58.8 jit_solution(12198358390054257893)
XLA Ops:
  0.0 0.7 %collective-permute-start = (s32[4]{0:T(128)}, s32[4]{0:T(128)S(1)}, u32[]{:S(2)}, u32[]{:S(2)}) collective-permute-start(s32[4]{0:T(128)} %bitcast.8), channel_id=1, source_target_pairs={{0,1},{1,0},{2,3},{3,2},{4,5},{5,4},{6,7},{7,6},{8,9},{9,8},{10,11... | collective-permute-start | bytes 56 | tf_op jit(solution)/shard_map/ppermute | solution.py:23
  0.7 1.3 %reshape.99.gain_ref = f32[1,768]{1,0:T(1,128)} reshape(f32[768]{0:T(1024)} %param.12) | data formatting | bytes 6144 | tf_op jit(solution)/shard_map/reshape | solution.py:231
  2.0 0.1 mul.15
  2.1 0.0 collective-permute-done.order_ref
  2.1 0.0 copy-start.7
  2.1 0.5 copy-done.7
  2.6 1.9 %shard_map.109 = (bf16[128,768]{1,0:T(8,128)(2,1)}, bf16[136,768]{1,0:T(8,128)(2,1)}) custom-call(s32[4]{0:T(128)} %copy-done.7, s32[4]{0:T(128)} %bitcast.7, bf16[128,768]{1,0:T(8,128)(2,1)} %bitcast.5, f32[1,768]{1,0:T(1,128)} %reshape.99.gain_ref), custom_call_target="tpu_custom_call" | custom-call | tf_op jit(solution)/shard_map/pallas_call | solution.py:223
  4.5 2.8 %collective-permute-start.7 = (bf16[136,768]{1,0:T(8,128)(2,1)}, bf16[136,768]{1,0:T(8,128)(2,1)S(1)}, u32[]{:S(2)}, u32[]{:S(2)}) collective-permute-start(bf16[136,768]{1,0:T(8,128)(2,1)} %get-tuple-element.10), channel_id=1, source_target_pairs={{7,0},{6,1},{9,2},{8,3},{11,4},{10,5},{13,6},{12,7},{15,8},{14,9},... | collective-permute-start | bytes 626696 | tf_op jit(solution)/shard_map/ppermute | solution.py:204
  7.3 2.5 %collective-permute-start.6 = (bf16[136,768]{1,0:T(8,128)(2,1)}, bf16[136,768]{1,0:T(8,128)(2,1)S(1)}, u32[]{:S(2)}, u32[]{:S(2)}) collective-permute-start(bf16[136,768]{1,0:T(8,128)(2,1)} %get-tuple-element.10), channel_id=1, source_target_pairs={{5,0},{4,1},{7,2},{6,3},{9,4},{8,5},{11,6},{10,7},{13,8},{12,9},{1... | collective-permute-start | bytes 626696 | tf_op jit(solution)/shard_map/ppermute | solution.py:204
  9.8 2.0 %collective-permute-start.5 = (bf16[136,768]{1,0:T(8,128)(2,1)}, bf16[136,768]{1,0:T(8,128)(2,1)S(1)}, u32[]{:S(2)}, u32[]{:S(2)}) collective-permute-start(bf16[136,768]{1,0:T(8,128)(2,1)} %get-tuple-element.10), channel_id=1, source_target_pairs={{3,0},{2,1},{5,2},{4,3},{7,4},{6,5},{9,6},{8,7},{11,8},{10,9},{13,... | collective-permute-start | bytes 626696 | tf_op jit(solution)/shard_map/ppermute | solution.py:204
  11.9 0.6 collective-permute-start.4
  12.4 3.1 %collective-permute-start.3 = (bf16[136,768]{1,0:T(8,128)(2,1)}, bf16[136,768]{1,0:T(8,128)(2,1)S(1)}, u32[]{:S(2)}, u32[]{:S(2)}) collective-permute-start(bf16[136,768]{1,0:T(8,128)(2,1)} %get-tuple-element.10), channel_id=1, source_target_pairs={{1,2},{0,3},{3,4},{2,5},{5,6},{4,7},{7,8},{6,9},{9,10},{8,11},{11,... | collective-permute-start | bytes 626696 | tf_op jit(solution)/shard_map/ppermute | solution.py:204
  15.5 0.7 %broadcast_multiply_fusion = (s32[7]{0:T(128)S(1)}, s32[7]{0:T(128)S(1)}) fusion(s32[7]{0:T(128)} %constant.78.clone, s32[]{:T(128)S(6)} %axis_index.15), kind=kLoop, calls=%fused_computation.23 | loop fusion | flops 14 | bytes 88 | tf_op jit(solution)/shard_map/mul | solution.py:70
  16.1 0.7 %compare_reduce_fusion = pred[7]{0:T(512)(128)(4,1)S(1)} fusion(s32[7]{0:T(128)S(1)} %get-tuple-element.20, s32[4]{0:T(128)} %bitcast.9), kind=kLoop, calls=%fused_computation.19 | loop fusion | flops 49 | bytes 51 | tf_op jit(solution)/shard_map/reduce_or | solution.py:237
  16.9 0.5 convert_element_type.17.needed_ref
  17.4 0.1 fusion.1
  17.5 3.1 %negate_select_fusion = (f32[7,128,128]{2,1,0:T(8,128)}, f32[7,128,128]{2,1,0:T(8,128)}) fusion(f32[128]{0:T(128)S(1)} %mul.15, f32[7,128]{1,0:T(8,128)S(1)} %get-tuple-element.18, f32[7,128]{1,0:T(8,128)S(1)} %get-tuple-element.17, pred[128]{0:T(512)(128)(4,1)S(1)} %get-tuple-element.22, pred[128]{0:T(512)(128)(4,1)S(1)} %get-tuple-element.21), kind=kLoop, calls=%fused_computation | loop fusion | flops 458752 | bytes 925440 | tf_op jit(solution)/shard_map/jit(_where)/select_n | solution.py:82
  20.5 0.0 copy-start.8
  20.5 0.0 copy-start.9
  20.5 2.5 %shard_map.110.q_ref = bf16[128,768]{1,0:T(8,128)(2,1)} custom-call(bf16[128,768]{1,0:T(8,128)(2,1)} %get-tuple-element.14.x_ref, bf16[768,768]{1,0:T(8,128)(2,1)} %w_ref.1, f32[7,128,128]{2,1,0:T(8,128)} %get-tuple-element.16.cos_ref.rest_7_, f32[7,128,128]{2,1,0:T(8,128)} %get-tuple-element.15.sin_ref.rest_8_), custom_call_target="tpu_custom_call" | custom-call | tf_op jit(solution)/shard_map/pallas_call | solution.py:243
  23.0 0.0 collective-permute-done.7.rest_6_
  23.0 0.0 copy-done.8
  23.0 0.0 copy-start
  23.0 1.3 %collective-permute-start.2 = (bf16[136,768]{1,0:T(8,128)(2,1)S(1)}, bf16[136,768]{1,0:T(8,128)(2,1)S(1)}, u32[]{:S(2)}, u32[]{:S(2)}) collective-permute-start(bf16[136,768]{1,0:T(8,128)(2,1)S(1)} %copy-done.8), channel_id=1, source_target_pairs={{1,4},{0,5},{3,6},{2,7},{5,8},{4,9},{7,10},{6,11},{9,12},{8,13},{1... | collective-permute-start | bytes 626696 | tf_op jit(solution)/shard_map/ppermute | solution.py:204
  24.3 0.0 collective-permute-done.6.rest_5_
  24.3 0.0 copy-start.1
  24.3 1.3 %collective-permute-start.1 = (bf16[136,768]{1,0:T(8,128)(2,1)S(1)}, bf16[136,768]{1,0:T(8,128)(2,1)S(1)}, u32[]{:S(2)}, u32[]{:S(2)}) collective-permute-start(bf16[136,768]{1,0:T(8,128)(2,1)S(1)} %copy-done.8), channel_id=1, source_target_pairs={{1,6},{0,7},{3,8},{2,9},{5,10},{4,11},{7,12},{6,13},{9,14},{8,15},... | collective-permute-start | bytes 626696 | tf_op jit(solution)/shard_map/ppermute | solution.py:204
  25.6 0.0 copy-done.9
  25.7 0.5 broadcast_multiply_fusion.1.scale_ref
  26.2 0.0 collective-permute-done.5.rest_4_
  26.2 0.0 copy-start.2
  26.2 0.0 collective-permute-done.4.rest_3_
  26.2 0.0 copy-start.3
  26.2 0.0 collective-permute-done.3.rest_2_
  26.2 0.0 copy-start.4
  26.2 6.1 %collective-permute-done.2.rest_1_ = bf16[136,768]{1,0:T(8,128)(2,1)S(1)} collective-permute-done((bf16[136,768]{1,0:T(8,128)(2,1)S(1)}, bf16[136,768]{1,0:T(8,128)(2,1)S(1)}, u32[]{:S(2)}, u32[]{:S(2)}) %collective-permute-start.2) | collective-permute-done | bytes 208928 | tf_op jit(solution)/shard_map/ppermute | solution.py:204
  32.4 0.0 copy-start.5
  32.4 9.7 %collective-permute-done.1.rest_0_ = bf16[136,768]{1,0:T(8,128)(2,1)S(1)} collective-permute-done((bf16[136,768]{1,0:T(8,128)(2,1)S(1)}, bf16[136,768]{1,0:T(8,128)(2,1)S(1)}, u32[]{:S(2)}, u32[]{:S(2)}) %collective-permute-start.1) | collective-permute-done | bytes 208928 | tf_op jit(solution)/shard_map/ppermute | solution.py:204
  42.0 0.0 copy-done
  42.0 0.0 copy-done.1
  42.1 0.0 copy-done.2
  42.1 0.0 copy-done.3
  42.1 0.0 copy-done.4
  42.1 0.0 copy-done.5
  42.1 0.0 copy-start.6
  42.1 0.7 %copy-done.6 = bf16[136,768]{1,0:T(8,128)(2,1)} copy-done((bf16[136,768]{1,0:T(8,128)(2,1)}, bf16[136,768]{1,0:T(8,128)(2,1)S(1)}, u32[]{:S(2)}) %copy-start.6) | copy-done | bytes 208920
  42.8 16.0 %shard_map.111 = bf16[128,768]{1,0:T(8,128)(2,1)} custom-call(s32[7]{0:T(128)} %convert_element_type.17.needed_ref, f32[12]{0:T(128)} %broadcast_multiply_fusion.1.scale_ref, bf16[128,768]{1,0:T(8,128)(2,1)} %shard_map.110.q_ref, bf16[136,768]{1,0:T(8,128)(2,1)} %copy-done.6, bf16[136,768]{1,0:T(8,128)(2,1)} %copy-done.5, bf16[136,768]{1,0:T(8,128)(2,1)} %copy-done.4, ...), custom_call_target="tpu_custom_call" | custom-call | tf_op jit(solution)/shard_map/pallas_call | solution.py:255
  (3 shorter events, 0.0 us)
Async XLA Ops:
  0.0 2.1 %collective-permute-start = (s32[4]{0:T(128)}, s32[4]{0:T(128)S(1)}, u32[]{:S(2)}, u32[]{:S(2)}) collective-permute-start(s32[4]{0:T(128)} %bitcast.8), channel_id=1, source_target_pairs={{0,1},{1,0},{2,3},{3,2},{4,5},{5,4},{6,7},{7,6},{8,9},{9,8},{10,11... | collective-permute-start | bytes 56 | tf_op jit(solution)/shard_map/ppermute | solution.py:23
  2.1 0.5 copy-start.7
  4.5 18.5 %collective-permute-start.7 = (bf16[136,768]{1,0:T(8,128)(2,1)}, bf16[136,768]{1,0:T(8,128)(2,1)S(1)}, u32[]{:S(2)}, u32[]{:S(2)}) collective-permute-start(bf16[136,768]{1,0:T(8,128)(2,1)} %get-tuple-element.10), channel_id=1, source_target_pairs={{7,0},{6,1},{9,2},{8,3},{11,4},{10,5},{13,6},{12,7},{15,8},{14,9},... | collective-permute-start | bytes 626696 | tf_op jit(solution)/shard_map/ppermute | solution.py:204
  7.3 17.0 %collective-permute-start.6 = (bf16[136,768]{1,0:T(8,128)(2,1)}, bf16[136,768]{1,0:T(8,128)(2,1)S(1)}, u32[]{:S(2)}, u32[]{:S(2)}) collective-permute-start(bf16[136,768]{1,0:T(8,128)(2,1)} %get-tuple-element.10), channel_id=1, source_target_pairs={{5,0},{4,1},{7,2},{6,3},{9,4},{8,5},{11,6},{10,7},{13,8},{12,9},{1... | collective-permute-start | bytes 626696 | tf_op jit(solution)/shard_map/ppermute | solution.py:204
  9.8 16.4 %collective-permute-start.5 = (bf16[136,768]{1,0:T(8,128)(2,1)}, bf16[136,768]{1,0:T(8,128)(2,1)S(1)}, u32[]{:S(2)}, u32[]{:S(2)}) collective-permute-start(bf16[136,768]{1,0:T(8,128)(2,1)} %get-tuple-element.10), channel_id=1, source_target_pairs={{3,0},{2,1},{5,2},{4,3},{7,4},{6,5},{9,6},{8,7},{11,8},{10,9},{13,... | collective-permute-start | bytes 626696 | tf_op jit(solution)/shard_map/ppermute | solution.py:204
  11.9 14.4 %collective-permute-start.4 = (bf16[136,768]{1,0:T(8,128)(2,1)}, bf16[136,768]{1,0:T(8,128)(2,1)S(1)}, u32[]{:S(2)}, u32[]{:S(2)}) collective-permute-start(bf16[136,768]{1,0:T(8,128)(2,1)} %get-tuple-element.10), channel_id=1, source_target_pairs={{0,1},{1,0},{2,3},{3,2},{4,5},{5,4},{6,7},{7,6},{8,9},{9,8},{10,11... | collective-permute-start | bytes 626696 | tf_op jit(solution)/shard_map/ppermute | solution.py:23
  12.4 13.8 %collective-permute-start.3 = (bf16[136,768]{1,0:T(8,128)(2,1)}, bf16[136,768]{1,0:T(8,128)(2,1)S(1)}, u32[]{:S(2)}, u32[]{:S(2)}) collective-permute-start(bf16[136,768]{1,0:T(8,128)(2,1)} %get-tuple-element.10), channel_id=1, source_target_pairs={{1,2},{0,3},{3,4},{2,5},{5,6},{4,7},{7,8},{6,9},{9,10},{8,11},{11,... | collective-permute-start | bytes 626696 | tf_op jit(solution)/shard_map/ppermute | solution.py:204
  20.5 2.5 %copy-start.8 = (bf16[136,768]{1,0:T(8,128)(2,1)S(1)}, bf16[136,768]{1,0:T(8,128)(2,1)}, u32[]{:S(2)}) copy-start(bf16[136,768]{1,0:T(8,128)(2,1)} %get-tuple-element.10) | copy-start | bytes 626692
  20.5 5.1 %copy-start.9 = (f32[12]{0:T(128)S(1)}, f32[12]{0:T(128)}, u32[]{:S(2)}) copy-start(f32[12]{0:T(128)} %param.17) | copy-start | bytes 148
  23.0 19.0 %copy-start = (bf16[136,768]{1,0:T(8,128)(2,1)}, bf16[136,768]{1,0:T(8,128)(2,1)S(1)}, u32[]{:S(2)}) copy-start(bf16[136,768]{1,0:T(8,128)(2,1)S(1)} %collective-permute-done.7.rest_6_) | copy-start | bytes 626692
  23.0 9.4 %collective-permute-start.2 = (bf16[136,768]{1,0:T(8,128)(2,1)S(1)}, bf16[136,768]{1,0:T(8,128)(2,1)S(1)}, u32[]{:S(2)}, u32[]{:S(2)}) collective-permute-start(bf16[136,768]{1,0:T(8,128)(2,1)S(1)} %copy-done.8), channel_id=1, source_target_pairs={{1,4},{0,5},{3,6},{2,7},{5,8},{4,9},{7,10},{6,11},{9,12},{8,13},{1... | collective-permute-start | bytes 626696 | tf_op jit(solution)/shard_map/ppermute | solution.py:204
  24.3 17.7 %copy-start.1 = (bf16[136,768]{1,0:T(8,128)(2,1)}, bf16[136,768]{1,0:T(8,128)(2,1)S(1)}, u32[]{:S(2)}) copy-start(bf16[136,768]{1,0:T(8,128)(2,1)S(1)} %collective-permute-done.6.rest_5_) | copy-start | bytes 626692
  24.3 17.7 %collective-permute-start.1 = (bf16[136,768]{1,0:T(8,128)(2,1)S(1)}, bf16[136,768]{1,0:T(8,128)(2,1)S(1)}, u32[]{:S(2)}, u32[]{:S(2)}) collective-permute-start(bf16[136,768]{1,0:T(8,128)(2,1)S(1)} %copy-done.8), channel_id=1, source_target_pairs={{1,6},{0,7},{3,8},{2,9},{5,10},{4,11},{7,12},{6,13},{9,14},{8,15},... | collective-permute-start | bytes 626696 | tf_op jit(solution)/shard_map/ppermute | solution.py:204
  26.2 15.9 %copy-start.2 = (bf16[136,768]{1,0:T(8,128)(2,1)}, bf16[136,768]{1,0:T(8,128)(2,1)S(1)}, u32[]{:S(2)}) copy-start(bf16[136,768]{1,0:T(8,128)(2,1)S(1)} %collective-permute-done.5.rest_4_) | copy-start | bytes 626692
  26.2 15.8 %copy-start.3 = (bf16[136,768]{1,0:T(8,128)(2,1)}, bf16[136,768]{1,0:T(8,128)(2,1)S(1)}, u32[]{:S(2)}) copy-start(bf16[136,768]{1,0:T(8,128)(2,1)S(1)} %collective-permute-done.4.rest_3_) | copy-start | bytes 626692
  26.2 15.8 %copy-start.4 = (bf16[136,768]{1,0:T(8,128)(2,1)}, bf16[136,768]{1,0:T(8,128)(2,1)S(1)}, u32[]{:S(2)}) copy-start(bf16[136,768]{1,0:T(8,128)(2,1)S(1)} %collective-permute-done.3.rest_2_) | copy-start | bytes 626692
  32.4 9.7 %copy-start.5 = (bf16[136,768]{1,0:T(8,128)(2,1)}, bf16[136,768]{1,0:T(8,128)(2,1)S(1)}, u32[]{:S(2)}) copy-start(bf16[136,768]{1,0:T(8,128)(2,1)S(1)} %collective-permute-done.2.rest_1_) | copy-start | bytes 626692
  42.1 0.7 %copy-start.6 = (bf16[136,768]{1,0:T(8,128)(2,1)}, bf16[136,768]{1,0:T(8,128)(2,1)S(1)}, u32[]{:S(2)}) copy-start(bf16[136,768]{1,0:T(8,128)(2,1)S(1)} %collective-permute-done.1.rest_0_) | copy-start | bytes 626692

commit v4 on v2

--- a/solution.py
+++ b/solution.py
@@ -105,10 +105,10 @@
             @pl.when(needed_ref[slot] != 0)
             def _():
                 pref = payload_refs[slot]
-                rows = pref[0:count_rows, :]
-                live = pref[count_rows:count_rows + META_ROWS, 0:128].astype(jnp.float32)[0:1, :]
+                rows = pref[...]
                 kp = jnp.dot(rows, wk_ref[...], preferred_element_type=jnp.float32)
-                vp = jnp.dot(rows, wv_ref[...], preferred_element_type=jnp.float32).astype(jnp.bfloat16)
+                vp = jnp.dot(rows, wv_ref[...], preferred_element_type=jnp.float32)
+                vp = jnp.where(jnp.abs(vp) < jnp.inf, vp, jnp.float32(0)).astype(jnp.bfloat16)
                 cosine = cos_ref[slot]
                 signed = sin_ref[slot]
                 for p in range(pairs):
@@ -128,7 +128,7 @@
                         q_two, k_pair, (((1,), (1,)), ((), ())),
                         preferred_element_type=jnp.float32,
                     ) * scale_col
-                    scores = jnp.where(live > 0, scores, jnp.float32(NEG))
+                    scores = jnp.where(jnp.abs(scores) < jnp.inf, scores, jnp.float32(NEG))
                     best = m_ref[p]
                     fresh = jnp.maximum(best, jnp.max(scores, axis=1, keepdims=True))
                     decay = jnp.exp(best - fresh)
@@ -176,18 +176,13 @@
     def kernel(order_ref, count_ref, tok_ref, gain_ref, normed_ref, out_ref):
         floated = tok_ref[...].astype(jnp.float32)
         normed_ref[...] = layer_norm(floated, gain_ref[...]).astype(normed_ref.dtype)
-        lane = lax.broadcasted_iota(jnp.int32, (META_ROWS, 128), 1)
-        row = lax.broadcasted_iota(jnp.int32, (META_ROWS, 128), 0)
-        live = jnp.zeros((META_ROWS, 128), jnp.float32)
+        row = lax.broadcasted_iota(jnp.int32, (tile_rows, 1), 0)
         for s in range(tile_count):
             src = order_ref[s]
             start = pl.multiple_of(src * tile_rows, tile_rows)
-            out_ref[s * tile_rows:(s + 1) * tile_rows, :] = normed_ref[pl.ds(start, tile_rows), :]
-            inside = (lane // tile_rows == s) & ((lane % tile_rows) < count_ref[src]) & (row == 0)
-            live = jnp.where(inside, jnp.float32(1), live)
-        out_ref[count_rows:count_rows + META_ROWS, :] = jnp.zeros(
-            (META_ROWS, out_ref.shape[1]), out_ref.dtype)
-        out_ref[count_rows:count_rows + META_ROWS, 0:128] = live.astype(out_ref.dtype)
+            rows = normed_ref[pl.ds(start, tile_rows), :]
+            out_ref[s * tile_rows:(s + 1) * tile_rows, :] = jnp.where(
+                row < count_ref[src], rows, jnp.asarray(jnp.inf, rows.dtype))
 
     return kernel
 
@@ -224,7 +219,7 @@
         make_prep_kernel(tile_count, tile_rows, count_rows),
         out_shape=(
             jax.ShapeDtypeStruct((count_rows, width), jnp.bfloat16),
-            jax.ShapeDtypeStruct((count_rows + META_ROWS, width), jnp.bfloat16),
+            jax.ShapeDtypeStruct((count_rows, width), jnp.bfloat16),
         ),
         in_specs=[smem, smem, vmem, vmem],
         out_specs=(vmem, vmem),

time: 57.7 us -> 56.8 us (0.984)
  waiting for transfers between devices: 14.5 us -> 13.4 us
    ppermute x6, waiting for transfers between devices: 14.5 us -> 13.4 us  [across(): return lax.ppermute(shard, ('tok', 'ep'), pairs)]
where the time goes in v4:
time: 56.8 us; the launch traced here: 56.5 us
  Pallas kernels  20.6 us (36%)
  starting transfers between devices  14.2 us (25%)
  waiting for transfers between devices  13.4 us (24%)
  other arithmetic  5.6 us (10%)
  local copies, waits for them, and re-layouts  2.55 us (4%)
    pallas_call x1, Pallas kernels, on_device(): pl.pallas_call(make_band_kernel(slots, heads, head_dim, count_rows, width...  16.2 us
    ppermute x6, waiting for transfers between devices, across(): return lax.ppermute(shard, ('tok', 'ep'), pairs)  13.4 us
    ppermute x6, starting transfers between devices, across(): return lax.ppermute(shard, ('tok', 'ep'), pairs)  12.9 us
    select_n x1, other arithmetic, angle_tables(): signed = jnp.where(first[None, None, :], -sine, sine)  3.04 us
    pallas_call x1, Pallas kernels, on_device(): pl.pallas_call(make_query_kernel(head_dim), out_shape=jax.ShapeDtypeStruc...  2.46 us
    pallas_call x1, Pallas kernels, on_device(): pl.pallas_call(make_prep_kernel(tile_count, tile_rows, count_rows), out_s...  1.9 us
    reshape x1, local copies, waits for them, and re-layouts, on_device(): norm_gain.reshape(1, width)  1.28 us
    ppermute x2, starting transfers between devices, partner(): return lax.ppermute(block, axis, route)  1.24 us
  transfers between devices with their start and end apart: 8, of which 3 were waited for; matrix products, arithmetic and copies ran while one was open for 12% of the time, Pallas kernels for 4%

profile of v4, /device:TPU:27, one launch (start us, length us, event | category | flops | bytes accessed | tf_op | source)
XLA Modules:
  0.0 56.5 jit_solution(13520402467608866657)
XLA Ops:
  0.0 0.0 copy-start.8
  0.0 0.7 %collective-permute-start = (s32[4]{0:T(128)}, s32[4]{0:T(128)S(1)}, u32[]{:S(2)}, u32[]{:S(2)}) collective-permute-start(s32[4]{0:T(128)} %bitcast.9), channel_id=1, source_target_pairs={{0,1},{1,0},{2,3},{3,2},{4,5},{5,4},{6,7},{7,6},{8,9},{9,8},{10,11... | collective-permute-start | bytes 56 | tf_op jit(solution)/shard_map/ppermute | solution.py:23
  0.7 0.7 %broadcast_multiply_fusion = (s32[7]{0:T(128)S(1)}, s32[7]{0:T(128)S(1)}) fusion(s32[7]{0:T(128)} %constant.78.clone, s32[]{:T(128)S(6)} %axis_index.15), kind=kLoop, calls=%fused_computation.23 | loop fusion | flops 14 | bytes 88 | tf_op jit(solution)/shard_map/mul | solution.py:70
  1.4 0.7 %compare_reduce_fusion = pred[7]{0:T(512)(128)(4,1)S(1)} fusion(s32[7]{0:T(128)S(1)} %get-tuple-element.14, s32[4]{0:T(128)} %bitcast.8), kind=kLoop, calls=%fused_computation.19 | loop fusion | flops 49 | bytes 51 | tf_op jit(solution)/shard_map/reduce_or | solution.py:230
  2.1 0.5 convert_element_type.17.needed_ref
  2.7 1.3 %reshape.99.gain_ref = f32[1,768]{1,0:T(1,128)} reshape(f32[768]{0:T(1024)} %param.12) | data formatting | bytes 6144 | tf_op jit(solution)/shard_map/reshape | solution.py:226
  3.9 0.1 mul.15
  4.0 0.1 fusion.1
  4.1 0.0 collective-permute-done.order_ref
  4.1 0.0 copy-start.7
  4.1 0.5 copy-done.7
  4.6 1.9 %shard_map.109 = (bf16[128,768]{1,0:T(8,128)(2,1)}, bf16[128,768]{1,0:T(8,128)(2,1)}) custom-call(s32[4]{0:T(128)} %copy-done.7, s32[4]{0:T(128)} %bitcast.7, bf16[128,768]{1,0:T(8,128)(2,1)} %bitcast.5, f32[1,768]{1,0:T(1,128)} %reshape.99.gain_ref), custom_call_target="tpu_custom_call" | custom-call | tf_op jit(solution)/shard_map/pallas_call | solution.py:218
  6.5 2.8 %collective-permute-start.7 = (bf16[128,768]{1,0:T(8,128)(2,1)}, bf16[128,768]{1,0:T(8,128)(2,1)S(1)}, u32[]{:S(2)}, u32[]{:S(2)}) collective-permute-start(bf16[128,768]{1,0:T(8,128)(2,1)} %get-tuple-element.8), channel_id=1, source_target_pairs={{7,0},{6,1},{9,2},{8,3},{11,4},{10,5},{13,6},{12,7},{15,8},{14,9},... | collective-permute-start | bytes 589832 | tf_op jit(solution)/shard_map/ppermute | solution.py:199
  9.3 2.5 %collective-permute-start.6 = (bf16[128,768]{1,0:T(8,128)(2,1)}, bf16[128,768]{1,0:T(8,128)(2,1)S(1)}, u32[]{:S(2)}, u32[]{:S(2)}) collective-permute-start(bf16[128,768]{1,0:T(8,128)(2,1)} %get-tuple-element.8), channel_id=1, source_target_pairs={{5,0},{4,1},{7,2},{6,3},{9,4},{8,5},{11,6},{10,7},{13,8},{12,9},{1... | collective-permute-start | bytes 589832 | tf_op jit(solution)/shard_map/ppermute | solution.py:199
  11.8 3.0 %negate_select_fusion = (f32[7,128,128]{2,1,0:T(8,128)}, f32[7,128,128]{2,1,0:T(8,128)}) fusion(f32[128]{0:T(128)S(1)} %mul.15, f32[7,128]{1,0:T(8,128)S(1)} %get-tuple-element.12, f32[7,128]{1,0:T(8,128)S(1)} %get-tuple-element.11, pred[128]{0:T(512)(128)(4,1)S(1)} %get-tuple-element.16, pred[128]{0:T(512)(128)(4,1)S(1)} %get-tuple-element.15), kind=kLoop, calls=%fused_computation | loop fusion | flops 458752 | bytes 925440 | tf_op jit(solution)/shard_map/jit(_where)/select_n | solution.py:82
  14.8 2.0 %collective-permute-start.5 = (bf16[128,768]{1,0:T(8,128)(2,1)}, bf16[128,768]{1,0:T(8,128)(2,1)S(1)}, u32[]{:S(2)}, u32[]{:S(2)}) collective-permute-start(bf16[128,768]{1,0:T(8,128)(2,1)} %get-tuple-element.8), channel_id=1, source_target_pairs={{3,0},{2,1},{5,2},{4,3},{7,4},{6,5},{9,6},{8,7},{11,8},{10,9},{13,... | collective-permute-start | bytes 589832 | tf_op jit(solution)/shard_map/ppermute | solution.py:199
  16.9 0.6 collective-permute-start.4
  17.4 3.1 %collective-permute-start.3 = (bf16[128,768]{1,0:T(8,128)(2,1)}, bf16[128,768]{1,0:T(8,128)(2,1)S(1)}, u32[]{:S(2)}, u32[]{:S(2)}) collective-permute-start(bf16[128,768]{1,0:T(8,128)(2,1)} %get-tuple-element.8), channel_id=1, source_target_pairs={{1,2},{0,3},{3,4},{2,5},{5,6},{4,7},{7,8},{6,9},{9,10},{8,11},{11,... | collective-permute-start | bytes 589832 | tf_op jit(solution)/shard_map/ppermute | solution.py:199
  20.5 0.0 collective-permute-done.7.rest_6_
  20.5 0.0 copy-start
  20.5 1.3 %collective-permute-start.2 = (bf16[128,768]{1,0:T(8,128)(2,1)}, bf16[128,768]{1,0:T(8,128)(2,1)S(1)}, u32[]{:S(2)}, u32[]{:S(2)}) collective-permute-start(bf16[128,768]{1,0:T(8,128)(2,1)} %get-tuple-element.8), channel_id=1, source_target_pairs={{1,4},{0,5},{3,6},{2,7},{5,8},{4,9},{7,10},{6,11},{9,12},{8,13},{1... | collective-permute-start | bytes 589832 | tf_op jit(solution)/shard_map/ppermute | solution.py:199
  21.8 0.0 collective-permute-done.6.rest_5_
  21.8 0.0 copy-start.1
  21.8 1.3 %collective-permute-start.1 = (bf16[128,768]{1,0:T(8,128)(2,1)}, bf16[128,768]{1,0:T(8,128)(2,1)S(1)}, u32[]{:S(2)}, u32[]{:S(2)}) collective-permute-start(bf16[128,768]{1,0:T(8,128)(2,1)} %get-tuple-element.8), channel_id=1, source_target_pairs={{1,6},{0,7},{3,8},{2,9},{5,10},{4,11},{7,12},{6,13},{9,14},{8,15},... | collective-permute-start | bytes 589832 | tf_op jit(solution)/shard_map/ppermute | solution.py:199
  23.1 0.0 copy-done.8
  23.1 0.5 broadcast_multiply_fusion.1.scale_ref
  23.7 2.5 %shard_map.110.q_ref = bf16[128,768]{1,0:T(8,128)(2,1)} custom-call(bf16[128,768]{1,0:T(8,128)(2,1)} %get-tuple-element.7.x_ref, bf16[768,768]{1,0:T(8,128)(2,1)} %w_ref.1, f32[7,128,128]{2,1,0:T(8,128)} %get-tuple-element.10.cos_ref.rest_7_, f32[7,128,128]{2,1,0:T(8,128)} %get-tuple-element.9.sin_ref.rest_8_), custom_call_target="tpu_custom_call" | custom-call | tf_op jit(solution)/shard_map/pallas_call | solution.py:236
  26.1 0.0 copy-done
  26.1 0.0 copy-done.1
  26.1 1.9 %collective-permute-done.5.rest_4_ = bf16[128,768]{1,0:T(8,128)(2,1)S(1)} collective-permute-done((bf16[128,768]{1,0:T(8,128)(2,1)}, bf16[128,768]{1,0:T(8,128)(2,1)S(1)}, u32[]{:S(2)}, u32[]{:S(2)}) %collective-permute-start.5) | collective-permute-done | bytes 196640 | tf_op jit(solution)/shard_map/ppermute | solution.py:199
  28.0 0.0 copy-start.2
  28.0 0.0 collective-permute-done.4.rest_3_
  28.0 0.0 copy-start.3
  28.0 0.0 collective-permute-done.3.rest_2_
  28.0 0.0 copy-start.4
  28.0 1.8 %collective-permute-done.2.rest_1_ = bf16[128,768]{1,0:T(8,128)(2,1)S(1)} collective-permute-done((bf16[128,768]{1,0:T(8,128)(2,1)}, bf16[128,768]{1,0:T(8,128)(2,1)S(1)}, u32[]{:S(2)}, u32[]{:S(2)}) %collective-permute-start.2) | collective-permute-done | bytes 196640 | tf_op jit(solution)/shard_map/ppermute | solution.py:199
  29.8 0.0 copy-start.5
  29.8 9.7 %collective-permute-done.1.rest_0_ = bf16[128,768]{1,0:T(8,128)(2,1)S(1)} collective-permute-done((bf16[128,768]{1,0:T(8,128)(2,1)}, bf16[128,768]{1,0:T(8,128)(2,1)S(1)}, u32[]{:S(2)}, u32[]{:S(2)}) %collective-permute-start.1) | collective-permute-done | bytes 196640 | tf_op jit(solution)/shard_map/ppermute | solution.py:199
  39.5 0.0 copy-done.2
  39.6 0.0 copy-done.3
  39.6 0.0 copy-done.4
  39.6 0.0 copy-done.5
  39.6 0.0 copy-start.6
  39.6 0.7 %copy-done.6 = bf16[128,768]{1,0:T(8,128)(2,1)} copy-done((bf16[128,768]{1,0:T(8,128)(2,1)}, bf16[128,768]{1,0:T(8,128)(2,1)S(1)}, u32[]{:S(2)}) %copy-start.6) | copy-done | bytes 196632
  40.2 16.2 %shard_map.111 = bf16[128,768]{1,0:T(8,128)(2,1)} custom-call(s32[7]{0:T(128)} %convert_element_type.17.needed_ref, f32[12]{0:T(128)} %broadcast_multiply_fusion.1.scale_ref, bf16[128,768]{1,0:T(8,128)(2,1)} %shard_map.110.q_ref, bf16[128,768]{1,0:T(8,128)(2,1)} %copy-done.6, bf16[128,768]{1,0:T(8,128)(2,1)} %copy-done.5, bf16[128,768]{1,0:T(8,128)(2,1)} %copy-done.4, ...), custom_call_target="tpu_custom_call" | custom-call | tf_op jit(solution)/shard_map/pallas_call | solution.py:248
  (3 shorter events, 0.0 us)
Async XLA Ops:
  0.0 23.1 %copy-start.8 = (f32[12]{0:T(128)S(1)}, f32[12]{0:T(128)}, u32[]{:S(2)}) copy-start(f32[12]{0:T(128)} %param.17) | copy-start | bytes 148
  0.0 4.1 %collective-permute-start = (s32[4]{0:T(128)}, s32[4]{0:T(128)S(1)}, u32[]{:S(2)}, u32[]{:S(2)}) collective-permute-start(s32[4]{0:T(128)} %bitcast.9), channel_id=1, source_target_pairs={{0,1},{1,0},{2,3},{3,2},{4,5},{5,4},{6,7},{7,6},{8,9},{9,8},{10,11... | collective-permute-start | bytes 56 | tf_op jit(solution)/shard_map/ppermute | solution.py:23
  4.1 0.5 copy-start.7
  6.5 14.0 %collective-permute-start.7 = (bf16[128,768]{1,0:T(8,128)(2,1)}, bf16[128,768]{1,0:T(8,128)(2,1)S(1)}, u32[]{:S(2)}, u32[]{:S(2)}) collective-permute-start(bf16[128,768]{1,0:T(8,128)(2,1)} %get-tuple-element.8), channel_id=1, source_target_pairs={{7,0},{6,1},{9,2},{8,3},{11,4},{10,5},{13,6},{12,7},{15,8},{14,9},... | collective-permute-start | bytes 589832 | tf_op jit(solution)/shard_map/ppermute | solution.py:199
  9.3 12.5 %collective-permute-start.6 = (bf16[128,768]{1,0:T(8,128)(2,1)}, bf16[128,768]{1,0:T(8,128)(2,1)S(1)}, u32[]{:S(2)}, u32[]{:S(2)}) collective-permute-start(bf16[128,768]{1,0:T(8,128)(2,1)} %get-tuple-element.8), channel_id=1, source_target_pairs={{5,0},{4,1},{7,2},{6,3},{9,4},{8,5},{11,6},{10,7},{13,8},{12,9},{1... | collective-permute-start | bytes 589832 | tf_op jit(solution)/shard_map/ppermute | solution.py:199
  14.8 13.1 %collective-permute-start.5 = (bf16[128,768]{1,0:T(8,128)(2,1)}, bf16[128,768]{1,0:T(8,128)(2,1)S(1)}, u32[]{:S(2)}, u32[]{:S(2)}) collective-permute-start(bf16[128,768]{1,0:T(8,128)(2,1)} %get-tuple-element.8), channel_id=1, source_target_pairs={{3,0},{2,1},{5,2},{4,3},{7,4},{6,5},{9,6},{8,7},{11,8},{10,9},{13,... | collective-permute-start | bytes 589832 | tf_op jit(solution)/shard_map/ppermute | solution.py:199
  16.9 11.1 %collective-permute-start.4 = (bf16[128,768]{1,0:T(8,128)(2,1)}, bf16[128,768]{1,0:T(8,128)(2,1)S(1)}, u32[]{:S(2)}, u32[]{:S(2)}) collective-permute-start(bf16[128,768]{1,0:T(8,128)(2,1)} %get-tuple-element.8), channel_id=1, source_target_pairs={{0,1},{1,0},{2,3},{3,2},{4,5},{5,4},{6,7},{7,6},{8,9},{9,8},{10,11... | collective-permute-start | bytes 589832 | tf_op jit(solution)/shard_map/ppermute | solution.py:23
  17.4 10.6 %collective-permute-start.3 = (bf16[128,768]{1,0:T(8,128)(2,1)}, bf16[128,768]{1,0:T(8,128)(2,1)S(1)}, u32[]{:S(2)}, u32[]{:S(2)}) collective-permute-start(bf16[128,768]{1,0:T(8,128)(2,1)} %get-tuple-element.8), channel_id=1, source_target_pairs={{1,2},{0,3},{3,4},{2,5},{5,6},{4,7},{7,8},{6,9},{9,10},{8,11},{11,... | collective-permute-start | bytes 589832 | tf_op jit(solution)/shard_map/ppermute | solution.py:199
  20.5 5.6 %copy-start = (bf16[128,768]{1,0:T(8,128)(2,1)}, bf16[128,768]{1,0:T(8,128)(2,1)S(1)}, u32[]{:S(2)}) copy-start(bf16[128,768]{1,0:T(8,128)(2,1)S(1)} %collective-permute-done.7.rest_6_) | copy-start | bytes 589828
  20.5 9.3 %collective-permute-start.2 = (bf16[128,768]{1,0:T(8,128)(2,1)}, bf16[128,768]{1,0:T(8,128)(2,1)S(1)}, u32[]{:S(2)}, u32[]{:S(2)}) collective-permute-start(bf16[128,768]{1,0:T(8,128)(2,1)} %get-tuple-element.8), channel_id=1, source_target_pairs={{1,4},{0,5},{3,6},{2,7},{5,8},{4,9},{7,10},{6,11},{9,12},{8,13},{1... | collective-permute-start | bytes 589832 | tf_op jit(solution)/shard_map/ppermute | solution.py:199
  21.8 4.3 %copy-start.1 = (bf16[128,768]{1,0:T(8,128)(2,1)}, bf16[128,768]{1,0:T(8,128)(2,1)S(1)}, u32[]{:S(2)}) copy-start(bf16[128,768]{1,0:T(8,128)(2,1)S(1)} %collective-permute-done.6.rest_5_) | copy-start | bytes 589828
  21.8 17.7 %collective-permute-start.1 = (bf16[128,768]{1,0:T(8,128)(2,1)}, bf16[128,768]{1,0:T(8,128)(2,1)S(1)}, u32[]{:S(2)}, u32[]{:S(2)}) collective-permute-start(bf16[128,768]{1,0:T(8,128)(2,1)} %get-tuple-element.8), channel_id=1, source_target_pairs={{1,6},{0,7},{3,8},{2,9},{5,10},{4,11},{7,12},{6,13},{9,14},{8,15},... | collective-permute-start | bytes 589832 | tf_op jit(solution)/shard_map/ppermute | solution.py:199
  28.0 11.6 %copy-start.2 = (bf16[128,768]{1,0:T(8,128)(2,1)}, bf16[128,768]{1,0:T(8,128)(2,1)S(1)}, u32[]{:S(2)}) copy-start(bf16[128,768]{1,0:T(8,128)(2,1)S(1)} %collective-permute-done.5.rest_4_) | copy-start | bytes 589828
  28.0 11.6 %copy-start.3 = (bf16[128,768]{1,0:T(8,128)(2,1)}, bf16[128,768]{1,0:T(8,128)(2,1)S(1)}, u32[]{:S(2)}) copy-start(bf16[128,768]{1,0:T(8,128)(2,1)S(1)} %collective-permute-done.4.rest_3_) | copy-start | bytes 589828
  28.0 11.6 %copy-start.4 = (bf16[128,768]{1,0:T(8,128)(2,1)}, bf16[128,768]{1,0:T(8,128)(2,1)S(1)}, u32[]{:S(2)}) copy-start(bf16[128,768]{1,0:T(8,128)(2,1)S(1)} %collective-permute-done.3.rest_2_) | copy-start | bytes 589828
  29.8 9.7 %copy-start.5 = (bf16[128,768]{1,0:T(8,128)(2,1)}, bf16[128,768]{1,0:T(8,128)(2,1)S(1)}, u32[]{:S(2)}) copy-start(bf16[128,768]{1,0:T(8,128)(2,1)S(1)} %collective-permute-done.2.rest_1_) | copy-start | bytes 589828
  39.6 0.7 %copy-start.6 = (bf16[128,768]{1,0:T(8,128)(2,1)}, bf16[128,768]{1,0:T(8,128)(2,1)S(1)}, u32[]{:S(2)}) copy-start(bf16[128,768]{1,0:T(8,128)(2,1)S(1)} %collective-permute-done.1.rest_0_) | copy-start | bytes 589828

commit v5 on v4

--- a/solution.py
+++ b/solution.py
@@ -90,8 +90,19 @@
     stacked = per_pair * count_rows
 
     def kernel(needed_ref, scale_ref, q_ref, *rest):
-        payload_refs = rest[:slots]
-        cos_ref, sin_ref, wk_ref, wv_ref, wo_ref, tok_ref, out_ref, acc_ref, m_ref, l_ref = rest[slots:]
+        payload_hbm = rest[:slots]
+        (cos_ref, sin_ref, wk_ref, wv_ref, wo_hbm, tok_ref, out_ref, acc_ref, m_ref, l_ref,
+         pay_buf, wo_ref, sems) = rest[slots:]
+        copies = [pltpu.make_async_copy(payload_hbm[slot], pay_buf.at[slot], sems.at[slot])
+                  for slot in range(slots)]
+        wo_copy = pltpu.make_async_copy(wo_hbm, wo_ref, sems.at[slots])
+        for slot in range(slots):
+
+            @pl.when(needed_ref[slot] != 0)
+            def _():
+                copies[slot].start()
+
+        wo_copy.start()
         acc_ref[...] = jnp.zeros_like(acc_ref)
         m_ref[...] = jnp.full(m_ref.shape, NEG, jnp.float32)
         l_ref[...] = jnp.zeros_like(l_ref)
@@ -104,8 +115,8 @@
 
             @pl.when(needed_ref[slot] != 0)
             def _():
-                pref = payload_refs[slot]
-                rows = pref[...]
+                copies[slot].wait()
+                rows = pay_buf[slot]
                 kp = jnp.dot(rows, wk_ref[...], preferred_element_type=jnp.float32)
                 vp = jnp.dot(rows, wv_ref[...], preferred_element_type=jnp.float32)
                 vp = jnp.where(jnp.abs(vp) < jnp.inf, vp, jnp.float32(0)).astype(jnp.bfloat16)
@@ -146,6 +157,7 @@
                 res = jnp.where(head_of_lane == sub, acc_two[sub * count_rows:(sub + 1) * count_rows], res)
             parts.append(res.astype(jnp.bfloat16))
         attended = jnp.concatenate(parts, axis=1)
+        wo_copy.wait()
         mixed = tok_ref[...].astype(jnp.float32) + jnp.dot(
             attended, wo_ref[...], preferred_element_type=jnp.float32
         )
@@ -212,6 +224,7 @@
     block_index = lax.axis_index("tok")
     smem = pl.BlockSpec(memory_space=pltpu.SMEM)
     vmem = pl.BlockSpec(memory_space=pltpu.VMEM)
+    hbm = pl.BlockSpec(memory_space=pl.ANY)
     theirs = partner(matching[0], "ep", 0)
     tile_count = matching.shape[1]
     tile_rows = count_rows // tile_count
@@ -248,12 +261,15 @@
     out = pl.pallas_call(
         make_band_kernel(slots, heads, head_dim, count_rows, width),
         out_shape=jax.ShapeDtypeStruct((count_rows, width), jnp.bfloat16),
-        in_specs=[smem, smem] + [vmem] * (1 + slots + 6),
+        in_specs=[smem, smem, vmem] + [hbm] * slots + [vmem] * 4 + [hbm, vmem],
         out_specs=vmem,
         scratch_shapes=[
             pltpu.VMEM((pairs, stacked, 128), jnp.float32),
             pltpu.VMEM((pairs, stacked, 1), jnp.float32),
             pltpu.VMEM((pairs, stacked, 1), jnp.float32),
+            pltpu.VMEM((slots, count_rows, width), jnp.bfloat16),
+            pltpu.VMEM((width, width), jnp.bfloat16),
+            pltpu.SemaphoreType.DMA((slots + 1,)),
         ],
     )(needed.astype(jnp.int32), scales, queries, *received, cosine, signed, w_key, w_value, w_out,
       tokens[0])

time: 56.8 us -> 57.1 us (level)
  no operation moved by 1% of the time
where the time goes in v5:
time: 57.1 us; the launch traced here: 56.7 us
  Pallas kernels  20.7 us (36%)
  starting transfers between devices  14.2 us (25%)
  waiting for transfers between devices  13.4 us (23%)
  other arithmetic  5.6 us (10%)
  local copies, waits for them, and re-layouts  2.55 us (4%)
    pallas_call x1, Pallas kernels, on_device(): pl.pallas_call(make_band_kernel(slots, heads, head_dim, count_rows, width...  16.3 us
    ppermute x6, waiting for transfers between devices, across(): return lax.ppermute(shard, ('tok', 'ep'), pairs)  13.4 us
    ppermute x6, starting transfers between devices, across(): return lax.ppermute(shard, ('tok', 'ep'), pairs)  12.9 us
    select_n x1, other arithmetic, angle_tables(): signed = jnp.where(first[None, None, :], -sine, sine)  3.04 us
    pallas_call x1, Pallas kernels, on_device(): pl.pallas_call(make_query_kernel(head_dim), out_shape=jax.ShapeDtypeStruc...  2.46 us
    pallas_call x1, Pallas kernels, on_device(): pl.pallas_call(make_prep_kernel(tile_count, tile_rows, count_rows), out_s...  1.9 us
    reshape x1, local copies, waits for them, and re-layouts, on_device(): norm_gain.reshape(1, width)  1.28 us
    ppermute x2, starting transfers between devices, partner(): return lax.ppermute(block, axis, route)  1.24 us
  transfers between devices with their start and end apart: 8, of which 3 were waited for; matrix products, arithmetic and copies ran while one was open for 12% of the time, Pallas kernels for 4%

profile of v5, /device:TPU:27, one launch (start us, length us, event | category | flops | bytes accessed | tf_op | source)
XLA Modules:
  0.0 56.7 jit_solution(7146193002671318564)
XLA Ops:
  0.0 0.0 copy-start.8
  0.0 0.7 %collective-permute-start = (s32[4]{0:T(128)}, s32[4]{0:T(128)S(1)}, u32[]{:S(2)}, u32[]{:S(2)}) collective-permute-start(s32[4]{0:T(128)} %bitcast.9), channel_id=1, source_target_pairs={{0,1},{1,0},{2,3},{3,2},{4,5},{5,4},{6,7},{7,6},{8,9},{9,8},{10,11... | collective-permute-start | bytes 56 | tf_op jit(solution)/shard_map/ppermute | solution.py:23
  0.7 0.7 %broadcast_multiply_fusion = (s32[7]{0:T(128)S(1)}, s32[7]{0:T(128)S(1)}) fusion(s32[7]{0:T(128)} %constant.78.clone, s32[]{:T(128)S(6)} %axis_index.15), kind=kLoop, calls=%fused_computation.23 | loop fusion | flops 14 | bytes 88 | tf_op jit(solution)/shard_map/mul | solution.py:70
  1.4 0.7 %compare_reduce_fusion = pred[7]{0:T(512)(128)(4,1)S(1)} fusion(s32[7]{0:T(128)S(1)} %get-tuple-element.14, s32[4]{0:T(128)} %bitcast.8), kind=kLoop, calls=%fused_computation.19 | loop fusion | flops 49 | bytes 51 | tf_op jit(solution)/shard_map/reduce_or | solution.py:243
  2.1 0.5 convert_element_type.17.needed_ref
  2.7 1.3 %reshape.99.gain_ref = f32[1,768]{1,0:T(1,128)} reshape(f32[768]{0:T(1024)} %param.12) | data formatting | bytes 6144 | tf_op jit(solution)/shard_map/reshape | solution.py:239
  3.9 0.1 mul.15
  4.0 0.1 fusion.1
  4.1 0.0 collective-permute-done.order_ref
  4.1 0.0 copy-start.7
  4.1 0.5 copy-done.7
  4.6 1.9 %shard_map.109 = (bf16[128,768]{1,0:T(8,128)(2,1)}, bf16[128,768]{1,0:T(8,128)(2,1)}) custom-call(s32[4]{0:T(128)} %copy-done.7, s32[4]{0:T(128)} %bitcast.7, bf16[128,768]{1,0:T(8,128)(2,1)} %bitcast.5, f32[1,768]{1,0:T(1,128)} %reshape.99.gain_ref), custom_call_target="tpu_custom_call" | custom-call | tf_op jit(solution)/shard_map/pallas_call | solution.py:231
  6.5 2.8 %collective-permute-start.7 = (bf16[128,768]{1,0:T(8,128)(2,1)}, bf16[128,768]{1,0:T(8,128)(2,1)S(1)}, u32[]{:S(2)}, u32[]{:S(2)}) collective-permute-start(bf16[128,768]{1,0:T(8,128)(2,1)} %get-tuple-element.8), channel_id=1, source_target_pairs={{7,0},{6,1},{9,2},{8,3},{11,4},{10,5},{13,6},{12,7},{15,8},{14,9},... | collective-permute-start | bytes 589832 | tf_op jit(solution)/shard_map/ppermute | solution.py:211
  9.3 2.5 %collective-permute-start.6 = (bf16[128,768]{1,0:T(8,128)(2,1)}, bf16[128,768]{1,0:T(8,128)(2,1)S(1)}, u32[]{:S(2)}, u32[]{:S(2)}) collective-permute-start(bf16[128,768]{1,0:T(8,128)(2,1)} %get-tuple-element.8), channel_id=1, source_target_pairs={{5,0},{4,1},{7,2},{6,3},{9,4},{8,5},{11,6},{10,7},{13,8},{12,9},{1... | collective-permute-start | bytes 589832 | tf_op jit(solution)/shard_map/ppermute | solution.py:211
  11.8 3.0 %negate_select_fusion = (f32[7,128,128]{2,1,0:T(8,128)}, f32[7,128,128]{2,1,0:T(8,128)}) fusion(f32[128]{0:T(128)S(1)} %mul.15, f32[7,128]{1,0:T(8,128)S(1)} %get-tuple-element.12, f32[7,128]{1,0:T(8,128)S(1)} %get-tuple-element.11, pred[128]{0:T(512)(128)(4,1)S(1)} %get-tuple-element.16, pred[128]{0:T(512)(128)(4,1)S(1)} %get-tuple-element.15), kind=kLoop, calls=%fused_computation | loop fusion | flops 458752 | bytes 925440 | tf_op jit(solution)/shard_map/jit(_where)/select_n | solution.py:82
  14.8 2.0 %collective-permute-start.5 = (bf16[128,768]{1,0:T(8,128)(2,1)}, bf16[128,768]{1,0:T(8,128)(2,1)S(1)}, u32[]{:S(2)}, u32[]{:S(2)}) collective-permute-start(bf16[128,768]{1,0:T(8,128)(2,1)} %get-tuple-element.8), channel_id=1, source_target_pairs={{3,0},{2,1},{5,2},{4,3},{7,4},{6,5},{9,6},{8,7},{11,8},{10,9},{13,... | collective-permute-start | bytes 589832 | tf_op jit(solution)/shard_map/ppermute | solution.py:211
  16.9 0.6 collective-permute-start.4
  17.4 3.1 %collective-permute-start.3 = (bf16[128,768]{1,0:T(8,128)(2,1)}, bf16[128,768]{1,0:T(8,128)(2,1)S(1)}, u32[]{:S(2)}, u32[]{:S(2)}) collective-permute-start(bf16[128,768]{1,0:T(8,128)(2,1)} %get-tuple-element.8), channel_id=1, source_target_pairs={{1,2},{0,3},{3,4},{2,5},{5,6},{4,7},{7,8},{6,9},{9,10},{8,11},{11,... | collective-permute-start | bytes 589832 | tf_op jit(solution)/shard_map/ppermute | solution.py:211
  20.5 0.0 collective-permute-done.7.rest_6_
  20.5 0.0 copy-start
  20.5 1.3 %collective-permute-start.2 = (bf16[128,768]{1,0:T(8,128)(2,1)}, bf16[128,768]{1,0:T(8,128)(2,1)S(1)}, u32[]{:S(2)}, u32[]{:S(2)}) collective-permute-start(bf16[128,768]{1,0:T(8,128)(2,1)} %get-tuple-element.8), channel_id=1, source_target_pairs={{1,4},{0,5},{3,6},{2,7},{5,8},{4,9},{7,10},{6,11},{9,12},{8,13},{1... | collective-permute-start | bytes 589832 | tf_op jit(solution)/shard_map/ppermute | solution.py:211
  21.8 0.0 collective-permute-done.6.rest_5_
  21.8 0.0 copy-start.1
  21.8 1.3 %collective-permute-start.1 = (bf16[128,768]{1,0:T(8,128)(2,1)}, bf16[128,768]{1,0:T(8,128)(2,1)S(1)}, u32[]{:S(2)}, u32[]{:S(2)}) collective-permute-start(bf16[128,768]{1,0:T(8,128)(2,1)} %get-tuple-element.8), channel_id=1, source_target_pairs={{1,6},{0,7},{3,8},{2,9},{5,10},{4,11},{7,12},{6,13},{9,14},{8,15},... | collective-permute-start | bytes 589832 | tf_op jit(solution)/shard_map/ppermute | solution.py:211
  23.1 0.0 copy-done.8
  23.1 0.5 broadcast_multiply_fusion.1.scale_ref
  23.7 2.5 %shard_map.110.q_ref = bf16[128,768]{1,0:T(8,128)(2,1)} custom-call(bf16[128,768]{1,0:T(8,128)(2,1)} %get-tuple-element.7.x_ref, bf16[768,768]{1,0:T(8,128)(2,1)} %w_ref.1, f32[7,128,128]{2,1,0:T(8,128)} %get-tuple-element.10.cos_ref.rest_7_, f32[7,128,128]{2,1,0:T(8,128)} %get-tuple-element.9.sin_ref.rest_8_), custom_call_target="tpu_custom_call" | custom-call | tf_op jit(solution)/shard_map/pallas_call | solution.py:249
  26.1 0.0 copy-done
  26.1 0.0 copy-done.1
  26.1 1.9 %collective-permute-done.5.rest_4_ = bf16[128,768]{1,0:T(8,128)(2,1)S(1)} collective-permute-done((bf16[128,768]{1,0:T(8,128)(2,1)}, bf16[128,768]{1,0:T(8,128)(2,1)S(1)}, u32[]{:S(2)}, u32[]{:S(2)}) %collective-permute-start.5) | collective-permute-done | bytes 196640 | tf_op jit(solution)/shard_map/ppermute | solution.py:211
  28.0 0.0 copy-start.2
  28.0 0.0 collective-permute-done.4.rest_3_
  28.0 0.0 copy-start.3
  28.0 0.0 collective-permute-done.3.rest_2_
  28.0 0.0 copy-start.4
  28.0 1.8 %collective-permute-done.2.rest_1_ = bf16[128,768]{1,0:T(8,128)(2,1)S(1)} collective-permute-done((bf16[128,768]{1,0:T(8,128)(2,1)}, bf16[128,768]{1,0:T(8,128)(2,1)S(1)}, u32[]{:S(2)}, u32[]{:S(2)}) %collective-permute-start.2) | collective-permute-done | bytes 196640 | tf_op jit(solution)/shard_map/ppermute | solution.py:211
  29.8 0.0 copy-start.5
  29.8 9.7 %collective-permute-done.1.rest_0_ = bf16[128,768]{1,0:T(8,128)(2,1)S(1)} collective-permute-done((bf16[128,768]{1,0:T(8,128)(2,1)}, bf16[128,768]{1,0:T(8,128)(2,1)S(1)}, u32[]{:S(2)}, u32[]{:S(2)}) %collective-permute-start.1) | collective-permute-done | bytes 196640 | tf_op jit(solution)/shard_map/ppermute | solution.py:211
  39.5 0.0 copy-done.2
  39.6 0.0 copy-done.3
  39.6 0.0 copy-done.4
  39.6 0.0 copy-done.5
  39.6 0.0 copy-start.6
  39.6 0.7 %copy-done.6 = bf16[128,768]{1,0:T(8,128)(2,1)} copy-done((bf16[128,768]{1,0:T(8,128)(2,1)}, bf16[128,768]{1,0:T(8,128)(2,1)S(1)}, u32[]{:S(2)}) %copy-start.6) | copy-done | bytes 196632
  40.2 16.3 %shard_map.111 = bf16[128,768]{1,0:T(8,128)(2,1)} custom-call(s32[7]{0:T(128)} %convert_element_type.17.needed_ref, f32[12]{0:T(128)} %broadcast_multiply_fusion.1.scale_ref, bf16[128,768]{1,0:T(8,128)(2,1)} %shard_map.110.q_ref, bf16[128,768]{1,0:T(8,128)(2,1)} %copy-done.6, bf16[128,768]{1,0:T(8,128)(2,1)} %copy-done.5, bf16[128,768]{1,0:T(8,128)(2,1)} %copy-done.4, ...), custom_call_target="tpu_custom_call" | custom-call | tf_op jit(solution)/shard_map/pallas_call | solution.py:261
  (3 shorter events, 0.0 us)
Async XLA Ops:
  0.0 23.1 %copy-start.8 = (f32[12]{0:T(128)S(1)}, f32[12]{0:T(128)}, u32[]{:S(2)}) copy-start(f32[12]{0:T(128)} %param.17) | copy-start | bytes 148
  0.0 4.1 %collective-permute-start = (s32[4]{0:T(128)}, s32[4]{0:T(128)S(1)}, u32[]{:S(2)}, u32[]{:S(2)}) collective-permute-start(s32[4]{0:T(128)} %bitcast.9), channel_id=1, source_target_pairs={{0,1},{1,0},{2,3},{3,2},{4,5},{5,4},{6,7},{7,6},{8,9},{9,8},{10,11... | collective-permute-start | bytes 56 | tf_op jit(solution)/shard_map/ppermute | solution.py:23
  4.1 0.5 copy-start.7
  6.5 14.0 %collective-permute-start.7 = (bf16[128,768]{1,0:T(8,128)(2,1)}, bf16[128,768]{1,0:T(8,128)(2,1)S(1)}, u32[]{:S(2)}, u32[]{:S(2)}) collective-permute-start(bf16[128,768]{1,0:T(8,128)(2,1)} %get-tuple-element.8), channel_id=1, source_target_pairs={{7,0},{6,1},{9,2},{8,3},{11,4},{10,5},{13,6},{12,7},{15,8},{14,9},... | collective-permute-start | bytes 589832 | tf_op jit(solution)/shard_map/ppermute | solution.py:211
  9.3 12.5 %collective-permute-start.6 = (bf16[128,768]{1,0:T(8,128)(2,1)}, bf16[128,768]{1,0:T(8,128)(2,1)S(1)}, u32[]{:S(2)}, u32[]{:S(2)}) collective-permute-start(bf16[128,768]{1,0:T(8,128)(2,1)} %get-tuple-element.8), channel_id=1, source_target_pairs={{5,0},{4,1},{7,2},{6,3},{9,4},{8,5},{11,6},{10,7},{13,8},{12,9},{1... | collective-permute-start | bytes 589832 | tf_op jit(solution)/shard_map/ppermute | solution.py:211
  14.8 13.1 %collective-permute-start.5 = (bf16[128,768]{1,0:T(8,128)(2,1)}, bf16[128,768]{1,0:T(8,128)(2,1)S(1)}, u32[]{:S(2)}, u32[]{:S(2)}) collective-permute-start(bf16[128,768]{1,0:T(8,128)(2,1)} %get-tuple-element.8), channel_id=1, source_target_pairs={{3,0},{2,1},{5,2},{4,3},{7,4},{6,5},{9,6},{8,7},{11,8},{10,9},{13,... | collective-permute-start | bytes 589832 | tf_op jit(solution)/shard_map/ppermute | solution.py:211
  16.9 11.1 %collective-permute-start.4 = (bf16[128,768]{1,0:T(8,128)(2,1)}, bf16[128,768]{1,0:T(8,128)(2,1)S(1)}, u32[]{:S(2)}, u32[]{:S(2)}) collective-permute-start(bf16[128,768]{1,0:T(8,128)(2,1)} %get-tuple-element.8), channel_id=1, source_target_pairs={{0,1},{1,0},{2,3},{3,2},{4,5},{5,4},{6,7},{7,6},{8,9},{9,8},{10,11... | collective-permute-start | bytes 589832 | tf_op jit(solution)/shard_map/ppermute | solution.py:23
  17.4 10.6 %collective-permute-start.3 = (bf16[128,768]{1,0:T(8,128)(2,1)}, bf16[128,768]{1,0:T(8,128)(2,1)S(1)}, u32[]{:S(2)}, u32[]{:S(2)}) collective-permute-start(bf16[128,768]{1,0:T(8,128)(2,1)} %get-tuple-element.8), channel_id=1, source_target_pairs={{1,2},{0,3},{3,4},{2,5},{5,6},{4,7},{7,8},{6,9},{9,10},{8,11},{11,... | collective-permute-start | bytes 589832 | tf_op jit(solution)/shard_map/ppermute | solution.py:211
  20.5 5.6 %copy-start = (bf16[128,768]{1,0:T(8,128)(2,1)}, bf16[128,768]{1,0:T(8,128)(2,1)S(1)}, u32[]{:S(2)}) copy-start(bf16[128,768]{1,0:T(8,128)(2,1)S(1)} %collective-permute-done.7.rest_6_) | copy-start | bytes 589828
  20.5 9.3 %collective-permute-start.2 = (bf16[128,768]{1,0:T(8,128)(2,1)}, bf16[128,768]{1,0:T(8,128)(2,1)S(1)}, u32[]{:S(2)}, u32[]{:S(2)}) collective-permute-start(bf16[128,768]{1,0:T(8,128)(2,1)} %get-tuple-element.8), channel_id=1, source_target_pairs={{1,4},{0,5},{3,6},{2,7},{5,8},{4,9},{7,10},{6,11},{9,12},{8,13},{1... | collective-permute-start | bytes 589832 | tf_op jit(solution)/shard_map/ppermute | solution.py:211
  21.8 4.3 %copy-start.1 = (bf16[128,768]{1,0:T(8,128)(2,1)}, bf16[128,768]{1,0:T(8,128)(2,1)S(1)}, u32[]{:S(2)}) copy-start(bf16[128,768]{1,0:T(8,128)(2,1)S(1)} %collective-permute-done.6.rest_5_) | copy-start | bytes 589828
  21.8 17.7 %collective-permute-start.1 = (bf16[128,768]{1,0:T(8,128)(2,1)}, bf16[128,768]{1,0:T(8,128)(2,1)S(1)}, u32[]{:S(2)}, u32[]{:S(2)}) collective-permute-start(bf16[128,768]{1,0:T(8,128)(2,1)} %get-tuple-element.8), channel_id=1, source_target_pairs={{1,6},{0,7},{3,8},{2,9},{5,10},{4,11},{7,12},{6,13},{9,14},{8,15},... | collective-permute-start | bytes 589832 | tf_op jit(solution)/shard_map/ppermute | solution.py:211
  28.0 11.6 %copy-start.2 = (bf16[128,768]{1,0:T(8,128)(2,1)}, bf16[128,768]{1,0:T(8,128)(2,1)S(1)}, u32[]{:S(2)}) copy-start(bf16[128,768]{1,0:T(8,128)(2,1)S(1)} %collective-permute-done.5.rest_4_) | copy-start | bytes 589828
  28.0 11.6 %copy-start.3 = (bf16[128,768]{1,0:T(8,128)(2,1)}, bf16[128,768]{1,0:T(8,128)(2,1)S(1)}, u32[]{:S(2)}) copy-start(bf16[128,768]{1,0:T(8,128)(2,1)S(1)} %collective-permute-done.4.rest_3_) | copy-start | bytes 589828
  28.0 11.6 %copy-start.4 = (bf16[128,768]{1,0:T(8,128)(2,1)}, bf16[128,768]{1,0:T(8,128)(2,1)S(1)}, u32[]{:S(2)}) copy-start(bf16[128,768]{1,0:T(8,128)(2,1)S(1)} %collective-permute-done.3.rest_2_) | copy-start | bytes 589828
  29.8 9.7 %copy-start.5 = (bf16[128,768]{1,0:T(8,128)(2,1)}, bf16[128,768]{1,0:T(8,128)(2,1)S(1)}, u32[]{:S(2)}) copy-start(bf16[128,768]{1,0:T(8,128)(2,1)S(1)} %collective-permute-done.2.rest_1_) | copy-start | bytes 589828
  39.6 0.7 %copy-start.6 = (bf16[128,768]{1,0:T(8,128)(2,1)}, bf16[128,768]{1,0:T(8,128)(2,1)S(1)}, u32[]{:S(2)}) copy-start(bf16[128,768]{1,0:T(8,128)(2,1)S(1)} %collective-permute-done.1.rest_0_) | copy-start | bytes 589828

commit v6 on v4

--- a/solution.py
+++ b/solution.py
@@ -83,18 +83,15 @@
     return cosine, signed
 
 
-def make_band_kernel(slots, heads, head_dim, count_rows, width):
+def make_band_kernel(slots, reads, heads, head_dim, count_rows, width):
     pairs = width // 128
     quarter = head_dim // 4
     per_pair = 128 // head_dim
     stacked = per_pair * count_rows
 
-    def kernel(needed_ref, scale_ref, q_ref, *rest):
+    def kernel(needed_ref, place_ref, scale_ref, q_ref, *rest):
         payload_refs = rest[:slots]
-        cos_ref, sin_ref, wk_ref, wv_ref, wo_ref, tok_ref, out_ref, acc_ref, m_ref, l_ref = rest[slots:]
-        acc_ref[...] = jnp.zeros_like(acc_ref)
-        m_ref[...] = jnp.full(m_ref.shape, NEG, jnp.float32)
-        l_ref[...] = jnp.zeros_like(l_ref)
+        cos_ref, sin_ref, wk_ref, wv_ref, wo_ref, tok_ref, out_ref, k_buf, v_buf = rest[slots:]
         lane = lax.broadcasted_iota(jnp.int32, (count_rows, 128), 1)
         first = (lane % (2 * quarter)) < quarter
         head_of_lane = lane // head_dim
@@ -104,46 +101,43 @@
 
             @pl.when(needed_ref[slot] != 0)
             def _():
-                pref = payload_refs[slot]
-                rows = pref[...]
+                rows = payload_refs[slot][...]
+                at = pl.ds(pl.multiple_of(place_ref[slot] * count_rows, count_rows), count_rows)
                 kp = jnp.dot(rows, wk_ref[...], preferred_element_type=jnp.float32)
                 vp = jnp.dot(rows, wv_ref[...], preferred_element_type=jnp.float32)
-                vp = jnp.where(jnp.abs(vp) < jnp.inf, vp, jnp.float32(0)).astype(jnp.bfloat16)
+                v_buf[at, :] = jnp.where(jnp.abs(vp) < jnp.inf, vp, jnp.float32(0)).astype(jnp.bfloat16)
                 cosine = cos_ref[slot]
                 signed = sin_ref[slot]
                 for p in range(pairs):
                     lo = p * 128
                     x = kp[:, lo:lo + 128]
                     other = jnp.where(first, pltpu.roll(x, 128 - quarter, 1), pltpu.roll(x, quarter, 1))
-                    k_pair = (x * cosine + other * signed).astype(jnp.bfloat16)
-                    v_pair = vp[:, lo:lo + 128]
-                    q_pair = q_ref[:, lo:lo + 128]
-                    q_two = jnp.concatenate(
-                        [jnp.where(head_of_lane == sub, q_pair, jnp.zeros_like(q_pair))
-                         for sub in range(per_pair)], axis=0)
-                    scale_col = jnp.zeros((stacked, 1), jnp.float32)
-                    for sub in range(per_pair):
-                        scale_col = jnp.where(row // count_rows == sub, scale_ref[p * per_pair + sub], scale_col)
-                    scores = lax.dot_general(
-                        q_two, k_pair, (((1,), (1,)), ((), ())),
-                        preferred_element_type=jnp.float32,
-                    ) * scale_col
-                    scores = jnp.where(jnp.abs(scores) < jnp.inf, scores, jnp.float32(NEG))
-                    best = m_ref[p]
-                    fresh = jnp.maximum(best, jnp.max(scores, axis=1, keepdims=True))
-                    decay = jnp.exp(best - fresh)
-                    weights = jnp.exp(scores - fresh)
-                    l_ref[p] = l_ref[p] * decay + jnp.sum(weights, axis=1, keepdims=True)
-                    m_ref[p] = fresh
-                    pv = jnp.dot(weights.astype(jnp.bfloat16), v_pair, preferred_element_type=jnp.float32)
-                    acc_ref[p] = acc_ref[p] * decay + pv
+                    k_buf[at, lo:lo + 128] = (x * cosine + other * signed).astype(jnp.bfloat16)
 
         parts = []
         for p in range(pairs):
-            acc_two = acc_ref[p] / l_ref[p]
-            res = acc_two[0:count_rows]
+            lo = p * 128
+            q_pair = q_ref[:, lo:lo + 128]
+            q_two = jnp.concatenate(
+                [jnp.where(head_of_lane == sub, q_pair, jnp.zeros_like(q_pair))
+                 for sub in range(per_pair)], axis=0)
+            scale_col = jnp.zeros((stacked, 1), jnp.float32)
+            for sub in range(per_pair):
+                scale_col = jnp.where(row // count_rows == sub, scale_ref[p * per_pair + sub], scale_col)
+            scores = lax.dot_general(
+                q_two, k_buf[:, lo:lo + 128], (((1,), (1,)), ((), ())),
+                preferred_element_type=jnp.float32,
+            ) * scale_col
+            scores = jnp.where(jnp.abs(scores) < jnp.inf, scores, jnp.float32(NEG))
+            best = jnp.max(scores, axis=1, keepdims=True)
+            weights = jnp.exp(scores - best)
+            total = jnp.sum(weights, axis=1, keepdims=True)
+            summed = jnp.dot(weights.astype(jnp.bfloat16), v_buf[:, lo:lo + 128],
+                             preferred_element_type=jnp.float32)
+            two = summed / total
+            res = two[0:count_rows]
             for sub in range(1, per_pair):
-                res = jnp.where(head_of_lane == sub, acc_two[sub * count_rows:(sub + 1) * count_rows], res)
+                res = jnp.where(head_of_lane == sub, two[sub * count_rows:(sub + 1) * count_rows], res)
             parts.append(res.astype(jnp.bfloat16))
         attended = jnp.concatenate(parts, axis=1)
         mixed = tok_ref[...].astype(jnp.float32) + jnp.dot(
@@ -243,20 +237,19 @@
 
     slots = len(offsets)
     received = [partner(payload, "ep", 0) if d == 0 else across(payload, d) for d in offsets]
-    pairs = width // 128
-    stacked = (128 // head_dim) * count_rows
+    reads = stops.shape[-1]
+    flags = needed.astype(jnp.int32)
+    place = jnp.cumsum(flags) - flags
     out = pl.pallas_call(
-        make_band_kernel(slots, heads, head_dim, count_rows, width),
+        make_band_kernel(slots, reads, heads, head_dim, count_rows, width),
         out_shape=jax.ShapeDtypeStruct((count_rows, width), jnp.bfloat16),
-        in_specs=[smem, smem] + [vmem] * (1 + slots + 6),
+        in_specs=[smem, smem, smem] + [vmem] * (1 + slots + 6),
         out_specs=vmem,
         scratch_shapes=[
-            pltpu.VMEM((pairs, stacked, 128), jnp.float32),
-            pltpu.VMEM((pairs, stacked, 1), jnp.float32),
-            pltpu.VMEM((pairs, stacked, 1), jnp.float32),
+            pltpu.VMEM((reads * count_rows, width), jnp.bfloat16),
+            pltpu.VMEM((reads * count_rows, width), jnp.bfloat16),
         ],
-    )(needed.astype(jnp.int32), scales, queries, *received, cosine, signed, w_key, w_value, w_out,
-      tokens[0])
+    )(flags, place, scales, queries, *received, cosine, signed, w_key, w_value, w_out, tokens[0])
     return out[None]
 
 

time: 56.8 us -> 49.2 us (0.87)
  Pallas kernels: 20.6 us -> 12.3 us
  other arithmetic: 5.6 us -> 6.35 us
    pallas_call x1, Pallas kernels: 16.2 us -> 7.98 us  [on_device(): pl.pallas_call(make_band_kernel(slots, reads, heads, head_dim, count_rows...]
  transfers between devices with their start and end apart: 8 -> 8, of which waited for: 3 -> 3; matrix products, arithmetic and copies ran while one was open for 12% -> 16% of each run, Pallas kernels for 4% -> 5%
where the time goes in v6:
time: 49.2 us; the launch traced here: 48.9 us
  starting transfers between devices  14.2 us (29%)
  waiting for transfers between devices  13.4 us (27%)
  Pallas kernels  12.3 us (25%)
  other arithmetic  6.35 us (13%)
  local copies, waits for them, and re-layouts  2.56 us (5%)
    ppermute x6, waiting for transfers between devices, across(): return lax.ppermute(shard, ('tok', 'ep'), pairs)  13.4 us
    ppermute x6, starting transfers between devices, across(): return lax.ppermute(shard, ('tok', 'ep'), pairs)  12.9 us
    pallas_call x1, Pallas kernels, on_device(): pl.pallas_call(make_band_kernel(slots, reads, heads, head_dim, count_rows...  7.98 us
    select_n x1, other arithmetic, angle_tables(): signed = jnp.where(first[None, None, :], -sine, sine)  3 us
    pallas_call x1, Pallas kernels, on_device(): pl.pallas_call(make_query_kernel(head_dim), out_shape=jax.ShapeDtypeStruc...  2.44 us
    pallas_call x1, Pallas kernels, on_device(): pl.pallas_call(make_prep_kernel(tile_count, tile_rows, count_rows), out_s...  1.9 us
    reshape x1, local copies, waits for them, and re-layouts, on_device(): norm_gain.reshape(1, width)  1.28 us
    ppermute x2, starting transfers between devices, partner(): return lax.ppermute(block, axis, route)  1.24 us
  transfers between devices with their start and end apart: 8, of which 3 were waited for; matrix products, arithmetic and copies ran while one was open for 16% of the time, Pallas kernels for 5%

profile of v6, /device:TPU:27, one launch (start us, length us, event | category | flops | bytes accessed | tf_op | source)
XLA Modules:
  0.0 48.9 jit_solution(5295194136983721083)
XLA Ops:
  0.0 0.0 copy-start.8
  0.0 0.7 %collective-permute-start = (s32[4]{0:T(128)}, s32[4]{0:T(128)S(1)}, u32[]{:S(2)}, u32[]{:S(2)}) collective-permute-start(s32[4]{0:T(128)} %bitcast.13), channel_id=1, source_target_pairs={{0,1},{1,0},{2,3},{3,2},{4,5},{5,4},{6,7},{7,6},{8,9},{9,8},{10,11... | collective-permute-start | bytes 56 | tf_op jit(solution)/shard_map/ppermute | solution.py:23
  0.7 0.7 %broadcast_multiply_fusion = (s32[7]{0:T(128)S(1)}, s32[7]{0:T(128)S(1)}) fusion(s32[7]{0:T(128)} %constant.81.clone, s32[]{:T(128)S(6)} %axis_index.15), kind=kLoop, calls=%fused_computation.24 | loop fusion | flops 14 | bytes 88 | tf_op jit(solution)/shard_map/mul | solution.py:70
  1.4 0.7 %compare_reduce_fusion = pred[7]{0:T(512)(128)(4,1)S(1)} fusion(s32[7]{0:T(128)S(1)} %get-tuple-element.14, s32[4]{0:T(128)} %bitcast.12), kind=kLoop, calls=%fused_computation.19 | loop fusion | flops 49 | bytes 51 | tf_op jit(solution)/shard_map/reduce_or | solution.py:224
  2.1 0.6 %convert_bitcast_fusion = (s32[7,1]{0,1:T(1,128)S(1)}, s32[7]{0:T(128)}) fusion(pred[7]{0:T(512)(128)(4,1)S(1)} %compare_reduce_fusion), kind=kLoop, calls=%fused_computation.27 | loop fusion | flops 7 | bytes 63 | tf_op jit(solution)/shard_map/convert_element_type | solution.py:241
  2.7 1.3 %reshape.129.gain_ref = f32[1,768]{1,0:T(1,128)} reshape(f32[768]{0:T(1024)} %param.12) | data formatting | bytes 6144 | tf_op jit(solution)/shard_map/reshape | solution.py:220
  4.0 0.1 mul.15
  4.1 0.1 fusion.1
  4.1 0.2 reduce-window.9
  4.3 3.0 %negate_select_fusion = (f32[7,128,128]{2,1,0:T(8,128)}, f32[7,128,128]{2,1,0:T(8,128)}) fusion(f32[128]{0:T(128)S(1)} %mul.15, f32[7,128]{1,0:T(8,128)S(1)} %get-tuple-element.12, f32[7,128]{1,0:T(8,128)S(1)} %get-tuple-element.11, pred[128]{0:T(512)(128)(4,1)S(1)} %get-tuple-element.18, pred[128]{0:T(512)(128)(4,1)S(1)} %get-tuple-element.17), kind=kLoop, calls=%fused_computation | loop fusion | flops 458752 | bytes 925440 | tf_op jit(solution)/shard_map/jit(_where)/select_n | solution.py:82
  7.3 0.0 collective-permute-done.order_ref
  7.3 0.0 copy-start.7
  7.3 0.5 %copy-done.7 = s32[4]{0:T(128)} copy-done((s32[4]{0:T(128)}, s32[4]{0:T(128)S(1)}, u32[]{:S(2)}) %copy-start.7) | copy-done | bytes 40
  7.9 1.9 %shard_map.109 = (bf16[128,768]{1,0:T(8,128)(2,1)}, bf16[128,768]{1,0:T(8,128)(2,1)}) custom-call(s32[4]{0:T(128)} %copy-done.7, s32[4]{0:T(128)} %bitcast.11, bf16[128,768]{1,0:T(8,128)(2,1)} %bitcast.9, f32[1,768]{1,0:T(1,128)} %reshape.129.gain_ref), custom_call_target="tpu_custom_call" | custom-call | tf_op jit(solution)/shard_map/pallas_call | solution.py:212
  9.8 2.8 %collective-permute-start.7 = (bf16[128,768]{1,0:T(8,128)(2,1)}, bf16[128,768]{1,0:T(8,128)(2,1)S(1)}, u32[]{:S(2)}, u32[]{:S(2)}) collective-permute-start(bf16[128,768]{1,0:T(8,128)(2,1)} %get-tuple-element.8), channel_id=1, source_target_pairs={{7,0},{6,1},{9,2},{8,3},{11,4},{10,5},{13,6},{12,7},{15,8},{14,9},... | collective-permute-start | bytes 589832 | tf_op jit(solution)/shard_map/ppermute | solution.py:193
  12.6 2.5 %collective-permute-start.6 = (bf16[128,768]{1,0:T(8,128)(2,1)}, bf16[128,768]{1,0:T(8,128)(2,1)S(1)}, u32[]{:S(2)}, u32[]{:S(2)}) collective-permute-start(bf16[128,768]{1,0:T(8,128)(2,1)} %get-tuple-element.8), channel_id=1, source_target_pairs={{5,0},{4,1},{7,2},{6,3},{9,4},{8,5},{11,6},{10,7},{13,8},{12,9},{1... | collective-permute-start | bytes 589832 | tf_op jit(solution)/shard_map/ppermute | solution.py:193
  15.0 0.5 %bitcast_subtract_fusion.place_ref = s32[7]{0:T(128)} fusion(s32[7,1]{0,1:T(1,128)S(1)} %reduce-window.9, pred[7]{0:T(512)(128)(4,1)S(1)} %compare_reduce_fusion), kind=kLoop, calls=%fused_computation.22 | loop fusion | flops 14 | bytes 63 | tf_op jit(solution)/shard_map/sub | solution.py:242
  15.6 2.0 %collective-permute-start.5 = (bf16[128,768]{1,0:T(8,128)(2,1)}, bf16[128,768]{1,0:T(8,128)(2,1)S(1)}, u32[]{:S(2)}, u32[]{:S(2)}) collective-permute-start(bf16[128,768]{1,0:T(8,128)(2,1)} %get-tuple-element.8), channel_id=1, source_target_pairs={{3,0},{2,1},{5,2},{4,3},{7,4},{6,5},{9,6},{8,7},{11,8},{10,9},{13,... | collective-permute-start | bytes 589832 | tf_op jit(solution)/shard_map/ppermute | solution.py:193
  17.6 0.6 %collective-permute-start.4 = (bf16[128,768]{1,0:T(8,128)(2,1)}, bf16[128,768]{1,0:T(8,128)(2,1)S(1)}, u32[]{:S(2)}, u32[]{:S(2)}) collective-permute-start(bf16[128,768]{1,0:T(8,128)(2,1)} %get-tuple-element.8), channel_id=1, source_target_pairs={{0,1},{1,0},{2,3},{3,2},{4,5},{5,4},{6,7},{7,6},{8,9},{9,8},{10,11... | collective-permute-start | bytes 589832 | tf_op jit(solution)/shard_map/ppermute | solution.py:23
  18.2 3.1 %collective-permute-start.3 = (bf16[128,768]{1,0:T(8,128)(2,1)}, bf16[128,768]{1,0:T(8,128)(2,1)S(1)}, u32[]{:S(2)}, u32[]{:S(2)}) collective-permute-start(bf16[128,768]{1,0:T(8,128)(2,1)} %get-tuple-element.8), channel_id=1, source_target_pairs={{1,2},{0,3},{3,4},{2,5},{5,6},{4,7},{7,8},{6,9},{9,10},{8,11},{11,... | collective-permute-start | bytes 589832 | tf_op jit(solution)/shard_map/ppermute | solution.py:193
  21.2 0.0 collective-permute-done.7.rest_6_
  21.2 0.0 copy-start
  21.2 1.3 %collective-permute-start.2 = (bf16[128,768]{1,0:T(8,128)(2,1)}, bf16[128,768]{1,0:T(8,128)(2,1)S(1)}, u32[]{:S(2)}, u32[]{:S(2)}) collective-permute-start(bf16[128,768]{1,0:T(8,128)(2,1)} %get-tuple-element.8), channel_id=1, source_target_pairs={{1,4},{0,5},{3,6},{2,7},{5,8},{4,9},{7,10},{6,11},{9,12},{8,13},{1... | collective-permute-start | bytes 589832 | tf_op jit(solution)/shard_map/ppermute | solution.py:193
  22.5 0.0 collective-permute-done.6.rest_5_
  22.6 0.0 copy-start.1
  22.6 1.3 %collective-permute-start.1 = (bf16[128,768]{1,0:T(8,128)(2,1)}, bf16[128,768]{1,0:T(8,128)(2,1)S(1)}, u32[]{:S(2)}, u32[]{:S(2)}) collective-permute-start(bf16[128,768]{1,0:T(8,128)(2,1)} %get-tuple-element.8), channel_id=1, source_target_pairs={{1,6},{0,7},{3,8},{2,9},{5,10},{4,11},{7,12},{6,13},{9,14},{8,15},... | collective-permute-start | bytes 589832 | tf_op jit(solution)/shard_map/ppermute | solution.py:193
  23.9 0.0 copy-done.8
  23.9 0.5 %broadcast_multiply_fusion.1.scale_ref = f32[12]{0:T(128)} fusion(f32[12]{0:T(128)S(1)} %copy-done.8), kind=kLoop, calls=%fused_computation.25 | loop fusion | flops 12 | bytes 96 | tf_op jit(solution)/shard_map/div | solution.py:226
  24.4 2.4 %shard_map.110.q_ref = bf16[128,768]{1,0:T(8,128)(2,1)} custom-call(bf16[128,768]{1,0:T(8,128)(2,1)} %get-tuple-element.7.x_ref, bf16[768,768]{1,0:T(8,128)(2,1)} %w_ref.1, f32[7,128,128]{2,1,0:T(8,128)} %get-tuple-element.10.cos_ref.rest_7_, f32[7,128,128]{2,1,0:T(8,128)} %get-tuple-element.9.sin_ref.rest_8_), custom_call_target="tpu_custom_call" | custom-call | tf_op jit(solution)/shard_map/pallas_call | solution.py:230
  26.9 0.0 copy-done
  26.9 0.0 copy-done.1
  26.9 1.8 %collective-permute-done.5.rest_4_ = bf16[128,768]{1,0:T(8,128)(2,1)S(1)} collective-permute-done((bf16[128,768]{1,0:T(8,128)(2,1)}, bf16[128,768]{1,0:T(8,128)(2,1)S(1)}, u32[]{:S(2)}, u32[]{:S(2)}) %collective-permute-start.5) | collective-permute-done | bytes 196640 | tf_op jit(solution)/shard_map/ppermute | solution.py:193
  28.7 0.0 copy-start.2
  28.7 0.0 collective-permute-done.4.rest_3_
  28.7 0.0 copy-start.3
  28.7 0.0 collective-permute-done.3.rest_2_
  28.7 0.0 copy-start.4
  28.7 1.9 %collective-permute-done.2.rest_1_ = bf16[128,768]{1,0:T(8,128)(2,1)S(1)} collective-permute-done((bf16[128,768]{1,0:T(8,128)(2,1)}, bf16[128,768]{1,0:T(8,128)(2,1)S(1)}, u32[]{:S(2)}, u32[]{:S(2)}) %collective-permute-start.2) | collective-permute-done | bytes 196640 | tf_op jit(solution)/shard_map/ppermute | solution.py:193
  30.6 0.0 copy-start.5
  30.6 9.7 %collective-permute-done.1.rest_0_ = bf16[128,768]{1,0:T(8,128)(2,1)S(1)} collective-permute-done((bf16[128,768]{1,0:T(8,128)(2,1)}, bf16[128,768]{1,0:T(8,128)(2,1)S(1)}, u32[]{:S(2)}, u32[]{:S(2)}) %collective-permute-start.1) | collective-permute-done | bytes 196640 | tf_op jit(solution)/shard_map/ppermute | solution.py:193
  40.3 0.0 copy-start.6
  40.3 0.0 copy-done.2
  40.3 0.0 copy-done.3
  40.3 0.0 copy-done.4
  40.3 0.0 copy-done.5
  40.3 0.6 %copy-done.6 = bf16[128,768]{1,0:T(8,128)(2,1)} copy-done((bf16[128,768]{1,0:T(8,128)(2,1)}, bf16[128,768]{1,0:T(8,128)(2,1)S(1)}, u32[]{:S(2)}) %copy-start.6) | copy-done | bytes 196632
  40.9 8.0 %shard_map.111 = bf16[128,768]{1,0:T(8,128)(2,1)} custom-call(s32[7]{0:T(128)} %get-tuple-element.16.needed_ref, s32[7]{0:T(128)} %bitcast_subtract_fusion.place_ref, f32[12]{0:T(128)} %broadcast_multiply_fusion.1.scale_ref, bf16[128,768]{1,0:T(8,128)(2,1)} %shard_map.110.q_ref, bf16[128,768]{1,0:T(8,128)(2,1)} %copy-done.6, bf16[128,768]{1,0:T(8,128)(2,1)} %copy-done.5, ...), custom_call_target="tpu_custom_call" | custom-call | tf_op jit(solution)/shard_map/pallas_call | solution.py:243
  (3 shorter events, 0.0 us)
Async XLA Ops:
  0.0 23.9 %copy-start.8 = (f32[12]{0:T(128)S(1)}, f32[12]{0:T(128)}, u32[]{:S(2)}) copy-start(f32[12]{0:T(128)} %param.17) | copy-start | bytes 148
  0.0 7.3 %collective-permute-start = (s32[4]{0:T(128)}, s32[4]{0:T(128)S(1)}, u32[]{:S(2)}, u32[]{:S(2)}) collective-permute-start(s32[4]{0:T(128)} %bitcast.13), channel_id=1, source_target_pairs={{0,1},{1,0},{2,3},{3,2},{4,5},{5,4},{6,7},{7,6},{8,9},{9,8},{10,11... | collective-permute-start | bytes 56 | tf_op jit(solution)/shard_map/ppermute | solution.py:23
  7.3 0.5 %copy-start.7 = (s32[4]{0:T(128)}, s32[4]{0:T(128)S(1)}, u32[]{:S(2)}) copy-start(s32[4]{0:T(128)S(1)} %collective-permute-done.order_ref) | copy-start | bytes 52
  9.8 11.5 %collective-permute-start.7 = (bf16[128,768]{1,0:T(8,128)(2,1)}, bf16[128,768]{1,0:T(8,128)(2,1)S(1)}, u32[]{:S(2)}, u32[]{:S(2)}) collective-permute-start(bf16[128,768]{1,0:T(8,128)(2,1)} %get-tuple-element.8), channel_id=1, source_target_pairs={{7,0},{6,1},{9,2},{8,3},{11,4},{10,5},{13,6},{12,7},{15,8},{14,9},... | collective-permute-start | bytes 589832 | tf_op jit(solution)/shard_map/ppermute | solution.py:193
  12.6 10.0 %collective-permute-start.6 = (bf16[128,768]{1,0:T(8,128)(2,1)}, bf16[128,768]{1,0:T(8,128)(2,1)S(1)}, u32[]{:S(2)}, u32[]{:S(2)}) collective-permute-start(bf16[128,768]{1,0:T(8,128)(2,1)} %get-tuple-element.8), channel_id=1, source_target_pairs={{5,0},{4,1},{7,2},{6,3},{9,4},{8,5},{11,6},{10,7},{13,8},{12,9},{1... | collective-permute-start | bytes 589832 | tf_op jit(solution)/shard_map/ppermute | solution.py:193
  15.6 13.1 %collective-permute-start.5 = (bf16[128,768]{1,0:T(8,128)(2,1)}, bf16[128,768]{1,0:T(8,128)(2,1)S(1)}, u32[]{:S(2)}, u32[]{:S(2)}) collective-permute-start(bf16[128,768]{1,0:T(8,128)(2,1)} %get-tuple-element.8), channel_id=1, source_target_pairs={{3,0},{2,1},{5,2},{4,3},{7,4},{6,5},{9,6},{8,7},{11,8},{10,9},{13,... | collective-permute-start | bytes 589832 | tf_op jit(solution)/shard_map/ppermute | solution.py:193
  17.6 11.1 %collective-permute-start.4 = (bf16[128,768]{1,0:T(8,128)(2,1)}, bf16[128,768]{1,0:T(8,128)(2,1)S(1)}, u32[]{:S(2)}, u32[]{:S(2)}) collective-permute-start(bf16[128,768]{1,0:T(8,128)(2,1)} %get-tuple-element.8), channel_id=1, source_target_pairs={{0,1},{1,0},{2,3},{3,2},{4,5},{5,4},{6,7},{7,6},{8,9},{9,8},{10,11... | collective-permute-start | bytes 589832 | tf_op jit(solution)/shard_map/ppermute | solution.py:23
  18.2 10.6 %collective-permute-start.3 = (bf16[128,768]{1,0:T(8,128)(2,1)}, bf16[128,768]{1,0:T(8,128)(2,1)S(1)}, u32[]{:S(2)}, u32[]{:S(2)}) collective-permute-start(bf16[128,768]{1,0:T(8,128)(2,1)} %get-tuple-element.8), channel_id=1, source_target_pairs={{1,2},{0,3},{3,4},{2,5},{5,6},{4,7},{7,8},{6,9},{9,10},{8,11},{11,... | collective-permute-start | bytes 589832 | tf_op jit(solution)/shard_map/ppermute | solution.py:193
  21.2 5.6 %copy-start = (bf16[128,768]{1,0:T(8,128)(2,1)}, bf16[128,768]{1,0:T(8,128)(2,1)S(1)}, u32[]{:S(2)}) copy-start(bf16[128,768]{1,0:T(8,128)(2,1)S(1)} %collective-permute-done.7.rest_6_) | copy-start | bytes 589828
  21.2 9.3 %collective-permute-start.2 = (bf16[128,768]{1,0:T(8,128)(2,1)}, bf16[128,768]{1,0:T(8,128)(2,1)S(1)}, u32[]{:S(2)}, u32[]{:S(2)}) collective-permute-start(bf16[128,768]{1,0:T(8,128)(2,1)} %get-tuple-element.8), channel_id=1, source_target_pairs={{1,4},{0,5},{3,6},{2,7},{5,8},{4,9},{7,10},{6,11},{9,12},{8,13},{1... | collective-permute-start | bytes 589832 | tf_op jit(solution)/shard_map/ppermute | solution.py:193
  22.6 4.3 %copy-start.1 = (bf16[128,768]{1,0:T(8,128)(2,1)}, bf16[128,768]{1,0:T(8,128)(2,1)S(1)}, u32[]{:S(2)}) copy-start(bf16[128,768]{1,0:T(8,128)(2,1)S(1)} %collective-permute-done.6.rest_5_) | copy-start | bytes 589828
  22.6 17.7 %collective-permute-start.1 = (bf16[128,768]{1,0:T(8,128)(2,1)}, bf16[128,768]{1,0:T(8,128)(2,1)S(1)}, u32[]{:S(2)}, u32[]{:S(2)}) collective-permute-start(bf16[128,768]{1,0:T(8,128)(2,1)} %get-tuple-element.8), channel_id=1, source_target_pairs={{1,6},{0,7},{3,8},{2,9},{5,10},{4,11},{7,12},{6,13},{9,14},{8,15},... | collective-permute-start | bytes 589832 | tf_op jit(solution)/shard_map/ppermute | solution.py:193
  28.7 11.6 %copy-start.2 = (bf16[128,768]{1,0:T(8,128)(2,1)}, bf16[128,768]{1,0:T(8,128)(2,1)S(1)}, u32[]{:S(2)}) copy-start(bf16[128,768]{1,0:T(8,128)(2,1)S(1)} %collective-permute-done.5.rest_4_) | copy-start | bytes 589828
  28.7 11.6 %copy-start.3 = (bf16[128,768]{1,0:T(8,128)(2,1)}, bf16[128,768]{1,0:T(8,128)(2,1)S(1)}, u32[]{:S(2)}) copy-start(bf16[128,768]{1,0:T(8,128)(2,1)S(1)} %collective-permute-done.4.rest_3_) | copy-start | bytes 589828
  28.7 11.6 %copy-start.4 = (bf16[128,768]{1,0:T(8,128)(2,1)}, bf16[128,768]{1,0:T(8,128)(2,1)S(1)}, u32[]{:S(2)}) copy-start(bf16[128,768]{1,0:T(8,128)(2,1)S(1)} %collective-permute-done.3.rest_2_) | copy-start | bytes 589828
  30.6 9.7 %copy-start.5 = (bf16[128,768]{1,0:T(8,128)(2,1)}, bf16[128,768]{1,0:T(8,128)(2,1)S(1)}, u32[]{:S(2)}) copy-start(bf16[128,768]{1,0:T(8,128)(2,1)S(1)} %collective-permute-done.2.rest_1_) | copy-start | bytes 589828
  40.3 0.7 %copy-start.6 = (bf16[128,768]{1,0:T(8,128)(2,1)}, bf16[128,768]{1,0:T(8,128)(2,1)S(1)}, u32[]{:S(2)}) copy-start(bf16[128,768]{1,0:T(8,128)(2,1)S(1)} %collective-permute-done.1.rest_0_) | copy-start | bytes 589828

commit v7 on v6

--- a/solution.py
+++ b/solution.py
@@ -91,7 +91,8 @@
 
     def kernel(needed_ref, place_ref, scale_ref, q_ref, *rest):
         payload_refs = rest[:slots]
-        cos_ref, sin_ref, wk_ref, wv_ref, wo_ref, tok_ref, out_ref, k_buf, v_buf = rest[slots:]
+        (cos_ref, sin_ref, wk_ref, wv_ref, wo_ref, tok_ref, out_ref, k_buf, v_buf,
+         r_buf, c_buf, s_buf) = rest[slots:]
         lane = lax.broadcasted_iota(jnp.int32, (count_rows, 128), 1)
         first = (lane % (2 * quarter)) < quarter
         head_of_lane = lane // head_dim
@@ -101,18 +102,24 @@
 
             @pl.when(needed_ref[slot] != 0)
             def _():
-                rows = payload_refs[slot][...]
                 at = pl.ds(pl.multiple_of(place_ref[slot] * count_rows, count_rows), count_rows)
-                kp = jnp.dot(rows, wk_ref[...], preferred_element_type=jnp.float32)
-                vp = jnp.dot(rows, wv_ref[...], preferred_element_type=jnp.float32)
-                v_buf[at, :] = jnp.where(jnp.abs(vp) < jnp.inf, vp, jnp.float32(0)).astype(jnp.bfloat16)
-                cosine = cos_ref[slot]
-                signed = sin_ref[slot]
-                for p in range(pairs):
-                    lo = p * 128
-                    x = kp[:, lo:lo + 128]
-                    other = jnp.where(first, pltpu.roll(x, 128 - quarter, 1), pltpu.roll(x, quarter, 1))
-                    k_buf[at, lo:lo + 128] = (x * cosine + other * signed).astype(jnp.bfloat16)
+                r_buf[at, :] = payload_refs[slot][...]
+                c_buf[at, :] = cos_ref[slot]
+                s_buf[at, :] = sin_ref[slot]
+
+        rows = r_buf[...]
+        kp = jnp.dot(rows, wk_ref[...], preferred_element_type=jnp.float32)
+        vp = jnp.dot(rows, wv_ref[...], preferred_element_type=jnp.float32)
+        v_buf[...] = jnp.where(jnp.abs(vp) < jnp.inf, vp, jnp.float32(0)).astype(jnp.bfloat16)
+        cosine = c_buf[...]
+        signed = s_buf[...]
+        lane_k = lax.broadcasted_iota(jnp.int32, (reads * count_rows, 128), 1)
+        first_k = (lane_k % (2 * quarter)) < quarter
+        for p in range(pairs):
+            lo = p * 128
+            x = kp[:, lo:lo + 128]
+            other = jnp.where(first_k, pltpu.roll(x, 128 - quarter, 1), pltpu.roll(x, quarter, 1))
+            k_buf[:, lo:lo + 128] = (x * cosine + other * signed).astype(jnp.bfloat16)
 
         parts = []
         for p in range(pairs):
@@ -248,6 +255,9 @@
         scratch_shapes=[
             pltpu.VMEM((reads * count_rows, width), jnp.bfloat16),
             pltpu.VMEM((reads * count_rows, width), jnp.bfloat16),
+            pltpu.VMEM((reads * count_rows, width), jnp.bfloat16),
+            pltpu.VMEM((reads * count_rows, 128), jnp.float32),
+            pltpu.VMEM((reads * count_rows, 128), jnp.float32),
         ],
     )(flags, place, scales, queries, *received, cosine, signed, w_key, w_value, w_out, tokens[0])
     return out[None]

time: 49.2 us -> 48.7 us (0.990)
  Pallas kernels: 12.3 us -> 11.8 us
    pallas_call x1, Pallas kernels: 7.98 us -> 7.44 us  [on_device(): pl.pallas_call(make_band_kernel(slots, reads, heads, head_dim, count_rows...]
where the time goes in v7:
time: 48.7 us; the launch traced here: 48.4 us
  starting transfers between devices  14.2 us (29%)
  waiting for transfers between devices  13.4 us (28%)
  Pallas kernels  11.8 us (24%)
  other arithmetic  6.35 us (13%)
  local copies, waits for them, and re-layouts  2.56 us (5%)
    ppermute x6, waiting for transfers between devices, across(): return lax.ppermute(shard, ('tok', 'ep'), pairs)  13.4 us
    ppermute x6, starting transfers between devices, across(): return lax.ppermute(shard, ('tok', 'ep'), pairs)  12.9 us
    pallas_call x1, Pallas kernels, on_device(): pl.pallas_call(make_band_kernel(slots, reads, heads, head_dim, count_rows...  7.44 us
    select_n x1, other arithmetic, angle_tables(): signed = jnp.where(first[None, None, :], -sine, sine)  3 us
    pallas_call x1, Pallas kernels, on_device(): pl.pallas_call(make_query_kernel(head_dim), out_shape=jax.ShapeDtypeStruc...  2.44 us
    pallas_call x1, Pallas kernels, on_device(): pl.pallas_call(make_prep_kernel(tile_count, tile_rows, count_rows), out_s...  1.9 us
    reshape x1, local copies, waits for them, and re-layouts, on_device(): norm_gain.reshape(1, width)  1.28 us
    ppermute x2, starting transfers between devices, partner(): return lax.ppermute(block, axis, route)  1.24 us
  transfers between devices with their start and end apart: 8, of which 3 were waited for; matrix products, arithmetic and copies ran while one was open for 16% of the time, Pallas kernels for 5%

profile of v7, /device:TPU:27, one launch (start us, length us, event | category | flops | bytes accessed | tf_op | source)
XLA Modules:
  0.0 48.4 jit_solution(15781664573757995577)
XLA Ops:
  0.0 0.0 copy-start.8
  0.0 0.7 %collective-permute-start = (s32[4]{0:T(128)}, s32[4]{0:T(128)S(1)}, u32[]{:S(2)}, u32[]{:S(2)}) collective-permute-start(s32[4]{0:T(128)} %bitcast.13), channel_id=1, source_target_pairs={{0,1},{1,0},{2,3},{3,2},{4,5},{5,4},{6,7},{7,6},{8,9},{9,8},{10,11... | collective-permute-start | bytes 56 | tf_op jit(solution)/shard_map/ppermute | solution.py:23
  0.7 0.7 %broadcast_multiply_fusion = (s32[7]{0:T(128)S(1)}, s32[7]{0:T(128)S(1)}) fusion(s32[7]{0:T(128)} %constant.81.clone, s32[]{:T(128)S(6)} %axis_index.15), kind=kLoop, calls=%fused_computation.24 | loop fusion | flops 14 | bytes 88 | tf_op jit(solution)/shard_map/mul | solution.py:70
  1.4 0.7 %compare_reduce_fusion = pred[7]{0:T(512)(128)(4,1)S(1)} fusion(s32[7]{0:T(128)S(1)} %get-tuple-element.14, s32[4]{0:T(128)} %bitcast.12), kind=kLoop, calls=%fused_computation.19 | loop fusion | flops 49 | bytes 51 | tf_op jit(solution)/shard_map/reduce_or | solution.py:231
  2.1 0.6 %convert_bitcast_fusion = (s32[7,1]{0,1:T(1,128)S(1)}, s32[7]{0:T(128)}) fusion(pred[7]{0:T(512)(128)(4,1)S(1)} %compare_reduce_fusion), kind=kLoop, calls=%fused_computation.27 | loop fusion | flops 7 | bytes 63 | tf_op jit(solution)/shard_map/convert_element_type | solution.py:248
  2.7 1.3 %reshape.129.gain_ref = f32[1,768]{1,0:T(1,128)} reshape(f32[768]{0:T(1024)} %param.12) | data formatting | bytes 6144 | tf_op jit(solution)/shard_map/reshape | solution.py:227
  4.0 0.1 mul.15
  4.1 0.1 fusion.1
  4.1 0.2 reduce-window.9
  4.3 3.0 %negate_select_fusion = (f32[7,128,128]{2,1,0:T(8,128)}, f32[7,128,128]{2,1,0:T(8,128)}) fusion(f32[128]{0:T(128)S(1)} %mul.15, f32[7,128]{1,0:T(8,128)S(1)} %get-tuple-element.12, f32[7,128]{1,0:T(8,128)S(1)} %get-tuple-element.11, pred[128]{0:T(512)(128)(4,1)S(1)} %get-tuple-element.18, pred[128]{0:T(512)(128)(4,1)S(1)} %get-tuple-element.17), kind=kLoop, calls=%fused_computation | loop fusion | flops 458752 | bytes 925440 | tf_op jit(solution)/shard_map/jit(_where)/select_n | solution.py:82
  7.3 0.0 collective-permute-done.order_ref
  7.3 0.0 copy-start.7
  7.3 0.5 %copy-done.7 = s32[4]{0:T(128)} copy-done((s32[4]{0:T(128)}, s32[4]{0:T(128)S(1)}, u32[]{:S(2)}) %copy-start.7) | copy-done | bytes 40
  7.9 1.9 %shard_map.109 = (bf16[128,768]{1,0:T(8,128)(2,1)}, bf16[128,768]{1,0:T(8,128)(2,1)}) custom-call(s32[4]{0:T(128)} %copy-done.7, s32[4]{0:T(128)} %bitcast.11, bf16[128,768]{1,0:T(8,128)(2,1)} %bitcast.9, f32[1,768]{1,0:T(1,128)} %reshape.129.gain_ref), custom_call_target="tpu_custom_call" | custom-call | tf_op jit(solution)/shard_map/pallas_call | solution.py:219
  9.8 2.8 %collective-permute-start.7 = (bf16[128,768]{1,0:T(8,128)(2,1)}, bf16[128,768]{1,0:T(8,128)(2,1)S(1)}, u32[]{:S(2)}, u32[]{:S(2)}) collective-permute-start(bf16[128,768]{1,0:T(8,128)(2,1)} %get-tuple-element.8), channel_id=1, source_target_pairs={{7,0},{6,1},{9,2},{8,3},{11,4},{10,5},{13,6},{12,7},{15,8},{14,9},... | collective-permute-start | bytes 589832 | tf_op jit(solution)/shard_map/ppermute | solution.py:200
  12.6 2.5 %collective-permute-start.6 = (bf16[128,768]{1,0:T(8,128)(2,1)}, bf16[128,768]{1,0:T(8,128)(2,1)S(1)}, u32[]{:S(2)}, u32[]{:S(2)}) collective-permute-start(bf16[128,768]{1,0:T(8,128)(2,1)} %get-tuple-element.8), channel_id=1, source_target_pairs={{5,0},{4,1},{7,2},{6,3},{9,4},{8,5},{11,6},{10,7},{13,8},{12,9},{1... | collective-permute-start | bytes 589832 | tf_op jit(solution)/shard_map/ppermute | solution.py:200
  15.0 0.5 %bitcast_subtract_fusion.place_ref = s32[7]{0:T(128)} fusion(s32[7,1]{0,1:T(1,128)S(1)} %reduce-window.9, pred[7]{0:T(512)(128)(4,1)S(1)} %compare_reduce_fusion), kind=kLoop, calls=%fused_computation.22 | loop fusion | flops 14 | bytes 63 | tf_op jit(solution)/shard_map/sub | solution.py:249
  15.6 2.0 %collective-permute-start.5 = (bf16[128,768]{1,0:T(8,128)(2,1)}, bf16[128,768]{1,0:T(8,128)(2,1)S(1)}, u32[]{:S(2)}, u32[]{:S(2)}) collective-permute-start(bf16[128,768]{1,0:T(8,128)(2,1)} %get-tuple-element.8), channel_id=1, source_target_pairs={{3,0},{2,1},{5,2},{4,3},{7,4},{6,5},{9,6},{8,7},{11,8},{10,9},{13,... | collective-permute-start | bytes 589832 | tf_op jit(solution)/shard_map/ppermute | solution.py:200
  17.6 0.6 %collective-permute-start.4 = (bf16[128,768]{1,0:T(8,128)(2,1)}, bf16[128,768]{1,0:T(8,128)(2,1)S(1)}, u32[]{:S(2)}, u32[]{:S(2)}) collective-permute-start(bf16[128,768]{1,0:T(8,128)(2,1)} %get-tuple-element.8), channel_id=1, source_target_pairs={{0,1},{1,0},{2,3},{3,2},{4,5},{5,4},{6,7},{7,6},{8,9},{9,8},{10,11... | collective-permute-start | bytes 589832 | tf_op jit(solution)/shard_map/ppermute | solution.py:23
  18.2 3.1 %collective-permute-start.3 = (bf16[128,768]{1,0:T(8,128)(2,1)}, bf16[128,768]{1,0:T(8,128)(2,1)S(1)}, u32[]{:S(2)}, u32[]{:S(2)}) collective-permute-start(bf16[128,768]{1,0:T(8,128)(2,1)} %get-tuple-element.8), channel_id=1, source_target_pairs={{1,2},{0,3},{3,4},{2,5},{5,6},{4,7},{7,8},{6,9},{9,10},{8,11},{11,... | collective-permute-start | bytes 589832 | tf_op jit(solution)/shard_map/ppermute | solution.py:200
  21.2 0.0 collective-permute-done.7.rest_6_
  21.2 0.0 copy-start
  21.2 1.3 %collective-permute-start.2 = (bf16[128,768]{1,0:T(8,128)(2,1)}, bf16[128,768]{1,0:T(8,128)(2,1)S(1)}, u32[]{:S(2)}, u32[]{:S(2)}) collective-permute-start(bf16[128,768]{1,0:T(8,128)(2,1)} %get-tuple-element.8), channel_id=1, source_target_pairs={{1,4},{0,5},{3,6},{2,7},{5,8},{4,9},{7,10},{6,11},{9,12},{8,13},{1... | collective-permute-start | bytes 589832 | tf_op jit(solution)/shard_map/ppermute | solution.py:200
  22.5 0.0 collective-permute-done.6.rest_5_
  22.6 0.0 copy-start.1
  22.6 1.3 %collective-permute-start.1 = (bf16[128,768]{1,0:T(8,128)(2,1)}, bf16[128,768]{1,0:T(8,128)(2,1)S(1)}, u32[]{:S(2)}, u32[]{:S(2)}) collective-permute-start(bf16[128,768]{1,0:T(8,128)(2,1)} %get-tuple-element.8), channel_id=1, source_target_pairs={{1,6},{0,7},{3,8},{2,9},{5,10},{4,11},{7,12},{6,13},{9,14},{8,15},... | collective-permute-start | bytes 589832 | tf_op jit(solution)/shard_map/ppermute | solution.py:200
  23.9 0.0 copy-done.8
  23.9 0.5 %broadcast_multiply_fusion.1.scale_ref = f32[12]{0:T(128)} fusion(f32[12]{0:T(128)S(1)} %copy-done.8), kind=kLoop, calls=%fused_computation.25 | loop fusion | flops 12 | bytes 96 | tf_op jit(solution)/shard_map/div | solution.py:233
  24.4 2.4 %shard_map.110.q_ref = bf16[128,768]{1,0:T(8,128)(2,1)} custom-call(bf16[128,768]{1,0:T(8,128)(2,1)} %get-tuple-element.7.x_ref, bf16[768,768]{1,0:T(8,128)(2,1)} %w_ref.1, f32[7,128,128]{2,1,0:T(8,128)} %get-tuple-element.10.cos_ref.rest_7_, f32[7,128,128]{2,1,0:T(8,128)} %get-tuple-element.9.sin_ref.rest_8_), custom_call_target="tpu_custom_call" | custom-call | tf_op jit(solution)/shard_map/pallas_call | solution.py:237
  26.9 0.0 copy-done
  26.9 0.0 copy-done.1
  26.9 1.8 %collective-permute-done.5.rest_4_ = bf16[128,768]{1,0:T(8,128)(2,1)S(1)} collective-permute-done((bf16[128,768]{1,0:T(8,128)(2,1)}, bf16[128,768]{1,0:T(8,128)(2,1)S(1)}, u32[]{:S(2)}, u32[]{:S(2)}) %collective-permute-start.5) | collective-permute-done | bytes 196640 | tf_op jit(solution)/shard_map/ppermute | solution.py:200
  28.7 0.0 copy-start.2
  28.7 0.0 collective-permute-done.4.rest_3_
  28.7 0.0 copy-start.3
  28.7 0.0 collective-permute-done.3.rest_2_
  28.7 0.0 copy-start.4
  28.7 1.9 %collective-permute-done.2.rest_1_ = bf16[128,768]{1,0:T(8,128)(2,1)S(1)} collective-permute-done((bf16[128,768]{1,0:T(8,128)(2,1)}, bf16[128,768]{1,0:T(8,128)(2,1)S(1)}, u32[]{:S(2)}, u32[]{:S(2)}) %collective-permute-start.2) | collective-permute-done | bytes 196640 | tf_op jit(solution)/shard_map/ppermute | solution.py:200
  30.6 0.0 copy-start.5
  30.6 9.7 %collective-permute-done.1.rest_0_ = bf16[128,768]{1,0:T(8,128)(2,1)S(1)} collective-permute-done((bf16[128,768]{1,0:T(8,128)(2,1)}, bf16[128,768]{1,0:T(8,128)(2,1)S(1)}, u32[]{:S(2)}, u32[]{:S(2)}) %collective-permute-start.1) | collective-permute-done | bytes 196640 | tf_op jit(solution)/shard_map/ppermute | solution.py:200
  40.3 0.0 copy-start.6
  40.3 0.0 copy-done.2
  40.3 0.0 copy-done.3
  40.3 0.0 copy-done.4
  40.3 0.0 copy-done.5
  40.3 0.6 %copy-done.6 = bf16[128,768]{1,0:T(8,128)(2,1)} copy-done((bf16[128,768]{1,0:T(8,128)(2,1)}, bf16[128,768]{1,0:T(8,128)(2,1)S(1)}, u32[]{:S(2)}) %copy-start.6) | copy-done | bytes 196632
  40.9 7.4 %shard_map.111 = bf16[128,768]{1,0:T(8,128)(2,1)} custom-call(s32[7]{0:T(128)} %get-tuple-element.16.needed_ref, s32[7]{0:T(128)} %bitcast_subtract_fusion.place_ref, f32[12]{0:T(128)} %broadcast_multiply_fusion.1.scale_ref, bf16[128,768]{1,0:T(8,128)(2,1)} %shard_map.110.q_ref, bf16[128,768]{1,0:T(8,128)(2,1)} %copy-done.6, bf16[128,768]{1,0:T(8,128)(2,1)} %copy-done.5, ...), custom_call_target="tpu_custom_call" | custom-call | tf_op jit(solution)/shard_map/pallas_call | solution.py:250
  (3 shorter events, 0.0 us)
Async XLA Ops:
  0.0 23.9 %copy-start.8 = (f32[12]{0:T(128)S(1)}, f32[12]{0:T(128)}, u32[]{:S(2)}) copy-start(f32[12]{0:T(128)} %param.17) | copy-start | bytes 148
  0.0 7.3 %collective-permute-start = (s32[4]{0:T(128)}, s32[4]{0:T(128)S(1)}, u32[]{:S(2)}, u32[]{:S(2)}) collective-permute-start(s32[4]{0:T(128)} %bitcast.13), channel_id=1, source_target_pairs={{0,1},{1,0},{2,3},{3,2},{4,5},{5,4},{6,7},{7,6},{8,9},{9,8},{10,11... | collective-permute-start | bytes 56 | tf_op jit(solution)/shard_map/ppermute | solution.py:23
  7.3 0.5 %copy-start.7 = (s32[4]{0:T(128)}, s32[4]{0:T(128)S(1)}, u32[]{:S(2)}) copy-start(s32[4]{0:T(128)S(1)} %collective-permute-done.order_ref) | copy-start | bytes 52
  9.8 11.5 %collective-permute-start.7 = (bf16[128,768]{1,0:T(8,128)(2,1)}, bf16[128,768]{1,0:T(8,128)(2,1)S(1)}, u32[]{:S(2)}, u32[]{:S(2)}) collective-permute-start(bf16[128,768]{1,0:T(8,128)(2,1)} %get-tuple-element.8), channel_id=1, source_target_pairs={{7,0},{6,1},{9,2},{8,3},{11,4},{10,5},{13,6},{12,7},{15,8},{14,9},... | collective-permute-start | bytes 589832 | tf_op jit(solution)/shard_map/ppermute | solution.py:200
  12.6 10.0 %collective-permute-start.6 = (bf16[128,768]{1,0:T(8,128)(2,1)}, bf16[128,768]{1,0:T(8,128)(2,1)S(1)}, u32[]{:S(2)}, u32[]{:S(2)}) collective-permute-start(bf16[128,768]{1,0:T(8,128)(2,1)} %get-tuple-element.8), channel_id=1, source_target_pairs={{5,0},{4,1},{7,2},{6,3},{9,4},{8,5},{11,6},{10,7},{13,8},{12,9},{1... | collective-permute-start | bytes 589832 | tf_op jit(solution)/shard_map/ppermute | solution.py:200
  15.6 13.1 %collective-permute-start.5 = (bf16[128,768]{1,0:T(8,128)(2,1)}, bf16[128,768]{1,0:T(8,128)(2,1)S(1)}, u32[]{:S(2)}, u32[]{:S(2)}) collective-permute-start(bf16[128,768]{1,0:T(8,128)(2,1)} %get-tuple-element.8), channel_id=1, source_target_pairs={{3,0},{2,1},{5,2},{4,3},{7,4},{6,5},{9,6},{8,7},{11,8},{10,9},{13,... | collective-permute-start | bytes 589832 | tf_op jit(solution)/shard_map/ppermute | solution.py:200
  17.6 11.1 %collective-permute-start.4 = (bf16[128,768]{1,0:T(8,128)(2,1)}, bf16[128,768]{1,0:T(8,128)(2,1)S(1)}, u32[]{:S(2)}, u32[]{:S(2)}) collective-permute-start(bf16[128,768]{1,0:T(8,128)(2,1)} %get-tuple-element.8), channel_id=1, source_target_pairs={{0,1},{1,0},{2,3},{3,2},{4,5},{5,4},{6,7},{7,6},{8,9},{9,8},{10,11... | collective-permute-start | bytes 589832 | tf_op jit(solution)/shard_map/ppermute | solution.py:23
  18.2 10.6 %collective-permute-start.3 = (bf16[128,768]{1,0:T(8,128)(2,1)}, bf16[128,768]{1,0:T(8,128)(2,1)S(1)}, u32[]{:S(2)}, u32[]{:S(2)}) collective-permute-start(bf16[128,768]{1,0:T(8,128)(2,1)} %get-tuple-element.8), channel_id=1, source_target_pairs={{1,2},{0,3},{3,4},{2,5},{5,6},{4,7},{7,8},{6,9},{9,10},{8,11},{11,... | collective-permute-start | bytes 589832 | tf_op jit(solution)/shard_map/ppermute | solution.py:200
  21.2 5.6 %copy-start = (bf16[128,768]{1,0:T(8,128)(2,1)}, bf16[128,768]{1,0:T(8,128)(2,1)S(1)}, u32[]{:S(2)}) copy-start(bf16[128,768]{1,0:T(8,128)(2,1)S(1)} %collective-permute-done.7.rest_6_) | copy-start | bytes 589828
  21.2 9.3 %collective-permute-start.2 = (bf16[128,768]{1,0:T(8,128)(2,1)}, bf16[128,768]{1,0:T(8,128)(2,1)S(1)}, u32[]{:S(2)}, u32[]{:S(2)}) collective-permute-start(bf16[128,768]{1,0:T(8,128)(2,1)} %get-tuple-element.8), channel_id=1, source_target_pairs={{1,4},{0,5},{3,6},{2,7},{5,8},{4,9},{7,10},{6,11},{9,12},{8,13},{1... | collective-permute-start | bytes 589832 | tf_op jit(solution)/shard_map/ppermute | solution.py:200
  22.6 4.3 %copy-start.1 = (bf16[128,768]{1,0:T(8,128)(2,1)}, bf16[128,768]{1,0:T(8,128)(2,1)S(1)}, u32[]{:S(2)}) copy-start(bf16[128,768]{1,0:T(8,128)(2,1)S(1)} %collective-permute-done.6.rest_5_) | copy-start | bytes 589828
  22.6 17.7 %collective-permute-start.1 = (bf16[128,768]{1,0:T(8,128)(2,1)}, bf16[128,768]{1,0:T(8,128)(2,1)S(1)}, u32[]{:S(2)}, u32[]{:S(2)}) collective-permute-start(bf16[128,768]{1,0:T(8,128)(2,1)} %get-tuple-element.8), channel_id=1, source_target_pairs={{1,6},{0,7},{3,8},{2,9},{5,10},{4,11},{7,12},{6,13},{9,14},{8,15},... | collective-permute-start | bytes 589832 | tf_op jit(solution)/shard_map/ppermute | solution.py:200
  28.7 11.6 %copy-start.2 = (bf16[128,768]{1,0:T(8,128)(2,1)}, bf16[128,768]{1,0:T(8,128)(2,1)S(1)}, u32[]{:S(2)}) copy-start(bf16[128,768]{1,0:T(8,128)(2,1)S(1)} %collective-permute-done.5.rest_4_) | copy-start | bytes 589828
  28.7 11.6 %copy-start.3 = (bf16[128,768]{1,0:T(8,128)(2,1)}, bf16[128,768]{1,0:T(8,128)(2,1)S(1)}, u32[]{:S(2)}) copy-start(bf16[128,768]{1,0:T(8,128)(2,1)S(1)} %collective-permute-done.4.rest_3_) | copy-start | bytes 589828
  28.7 11.6 %copy-start.4 = (bf16[128,768]{1,0:T(8,128)(2,1)}, bf16[128,768]{1,0:T(8,128)(2,1)S(1)}, u32[]{:S(2)}) copy-start(bf16[128,768]{1,0:T(8,128)(2,1)S(1)} %collective-permute-done.3.rest_2_) | copy-start | bytes 589828
  30.6 9.7 %copy-start.5 = (bf16[128,768]{1,0:T(8,128)(2,1)}, bf16[128,768]{1,0:T(8,128)(2,1)S(1)}, u32[]{:S(2)}) copy-start(bf16[128,768]{1,0:T(8,128)(2,1)S(1)} %collective-permute-done.2.rest_1_) | copy-start | bytes 589828
  40.3 0.7 %copy-start.6 = (bf16[128,768]{1,0:T(8,128)(2,1)}, bf16[128,768]{1,0:T(8,128)(2,1)S(1)}, u32[]{:S(2)}) copy-start(bf16[128,768]{1,0:T(8,128)(2,1)S(1)} %collective-permute-done.1.rest_0_) | copy-start | bytes 589828

commit v8 on v6

--- a/solution.py
+++ b/solution.py
@@ -83,36 +83,67 @@
     return cosine, signed
 
 
-def make_band_kernel(slots, reads, heads, head_dim, count_rows, width):
+def rotate_keys(kp, cosine, signed, k_ref, quarter):
+    lane = lax.broadcasted_iota(jnp.int32, (kp.shape[0], 128), 1)
+    first = (lane % (2 * quarter)) < quarter
+    for p in range(kp.shape[1] // 128):
+        lo = p * 128
+        x = kp[:, lo:lo + 128]
+        other = jnp.where(first, pltpu.roll(x, 128 - quarter, 1), pltpu.roll(x, quarter, 1))
+        k_ref[:, lo:lo + 128] = (x * cosine + other * signed).astype(k_ref.dtype)
+
+
+def finite_values(vp):
+    return jnp.where(jnp.abs(vp) < jnp.inf, vp, jnp.float32(0)).astype(jnp.bfloat16)
+
+
+def make_project_kernel(slots, late, head_dim, count_rows):
+    quarter = head_dim // 4
+    early = [slot for slot in range(slots) if slot != late]
+
+    def kernel(needed_ref, place_ref, *rest):
+        payload_refs = rest[:len(early)]
+        cos_ref, sin_ref, wk_ref, wv_ref, k_out, v_out, r_buf, c_buf, s_buf = rest[len(early):]
+        for pref, slot in zip(payload_refs, early):
+
+            @pl.when(needed_ref[slot] != 0)
+            def _():
+                at = pl.ds(pl.multiple_of(place_ref[slot] * count_rows, count_rows), count_rows)
+                r_buf[at, :] = pref[...]
+                c_buf[at, :] = cos_ref[slot]
+                s_buf[at, :] = sin_ref[slot]
+
+        rows = r_buf[...]
+        kp = jnp.dot(rows, wk_ref[...], preferred_element_type=jnp.float32)
+        vp = jnp.dot(rows, wv_ref[...], preferred_element_type=jnp.float32)
+        v_out[...] = finite_values(vp)
+        rotate_keys(kp, c_buf[...], s_buf[...], k_out, quarter)
+
+    return kernel
+
+
+def make_band_kernel(late, heads, head_dim, count_rows, width):
     pairs = width // 128
     quarter = head_dim // 4
     per_pair = 128 // head_dim
     stacked = per_pair * count_rows
 
-    def kernel(needed_ref, place_ref, scale_ref, q_ref, *rest):
-        payload_refs = rest[:slots]
-        cos_ref, sin_ref, wk_ref, wv_ref, wo_ref, tok_ref, out_ref, k_buf, v_buf = rest[slots:]
+    def kernel(needed_ref, place_ref, scale_ref, q_ref, pay_ref, cos_ref, sin_ref, wk_ref, wv_ref,
+               wo_ref, tok_ref, k_in, v_in, out_ref, k_buf, v_buf):
         lane = lax.broadcasted_iota(jnp.int32, (count_rows, 128), 1)
-        first = (lane % (2 * quarter)) < quarter
         head_of_lane = lane // head_dim
         row = lax.broadcasted_iota(jnp.int32, (stacked, 1), 0)
-
-        for slot in range(slots):
-
-            @pl.when(needed_ref[slot] != 0)
-            def _():
-                rows = payload_refs[slot][...]
-                at = pl.ds(pl.multiple_of(place_ref[slot] * count_rows, count_rows), count_rows)
-                kp = jnp.dot(rows, wk_ref[...], preferred_element_type=jnp.float32)
-                vp = jnp.dot(rows, wv_ref[...], preferred_element_type=jnp.float32)
-                v_buf[at, :] = jnp.where(jnp.abs(vp) < jnp.inf, vp, jnp.float32(0)).astype(jnp.bfloat16)
-                cosine = cos_ref[slot]
-                signed = sin_ref[slot]
-                for p in range(pairs):
-                    lo = p * 128
-                    x = kp[:, lo:lo + 128]
-                    other = jnp.where(first, pltpu.roll(x, 128 - quarter, 1), pltpu.roll(x, quarter, 1))
-                    k_buf[at, lo:lo + 128] = (x * cosine + other * signed).astype(jnp.bfloat16)
+        k_buf[...] = k_in[...]
+        v_buf[...] = v_in[...]
+
+        @pl.when(needed_ref[late] != 0)
+        def _():
+            at = pl.ds(pl.multiple_of(place_ref[late] * count_rows, count_rows), count_rows)
+            rows = pay_ref[...]
+            kp = jnp.dot(rows, wk_ref[...], preferred_element_type=jnp.float32)
+            vp = jnp.dot(rows, wv_ref[...], preferred_element_type=jnp.float32)
+            v_buf[at, :] = finite_values(vp)
+            rotate_keys(kp, cos_ref[late], sin_ref[late], k_buf.at[at], quarter)
 
         parts = []
         for p in range(pairs):
@@ -240,16 +271,27 @@
     reads = stops.shape[-1]
     flags = needed.astype(jnp.int32)
     place = jnp.cumsum(flags) - flags
+    late = offsets.index(-BAND)
+    packed = (reads * count_rows, width)
+    keys, values = pl.pallas_call(
+        make_project_kernel(slots, late, head_dim, count_rows),
+        out_shape=(jax.ShapeDtypeStruct(packed, jnp.bfloat16), jax.ShapeDtypeStruct(packed, jnp.bfloat16)),
+        in_specs=[smem, smem] + [vmem] * (slots - 1 + 4),
+        out_specs=(vmem, vmem),
+        scratch_shapes=[
+            pltpu.VMEM(packed, jnp.bfloat16),
+            pltpu.VMEM((reads * count_rows, 128), jnp.float32),
+            pltpu.VMEM((reads * count_rows, 128), jnp.float32),
+        ],
+    )(flags, place, *[r for i, r in enumerate(received) if i != late], cosine, signed, w_key, w_value)
     out = pl.pallas_call(
-        make_band_kernel(slots, reads, heads, head_dim, count_rows, width),
+        make_band_kernel(late, heads, head_dim, count_rows, width),
         out_shape=jax.ShapeDtypeStruct((count_rows, width), jnp.bfloat16),
-        in_specs=[smem, smem, smem] + [vmem] * (1 + slots + 6),
+        in_specs=[smem, smem, smem] + [vmem] * 10,
         out_specs=vmem,
-        scratch_shapes=[
-            pltpu.VMEM((reads * count_rows, width), jnp.bfloat16),
-            pltpu.VMEM((reads * count_rows, width), jnp.bfloat16),
-        ],
-    )(flags, place, scales, queries, *received, cosine, signed, w_key, w_value, w_out, tokens[0])
+        scratch_shapes=[pltpu.VMEM(packed, jnp.bfloat16), pltpu.VMEM(packed, jnp.bfloat16)],
+    )(flags, place, scales, queries, received[late], cosine, signed, w_key, w_value, w_out,
+      tokens[0], keys, values)
     return out[None]
 
 

time: 49.2 us -> 53.5 us (1.087)
  the two profiles are of different devices: /device:TPU:27 before, /device:TPU:5 now
where the time goes in v8:
time: 53.5 us; the launch traced here: 53.1 us
  starting transfers between devices  20.4 us (38%)
  Pallas kernels  15.5 us (29%)
  waiting for transfers between devices  7.55 us (14%)
  other arithmetic  6.32 us (12%)
  local copies, waits for them, and re-layouts  3.27 us (6%)
    ppermute x6, starting transfers between devices, across(): return lax.ppermute(shard, ('tok', 'ep'), pairs)  19.7 us
    ppermute x6, waiting for transfers between devices, across(): return lax.ppermute(shard, ('tok', 'ep'), pairs)  7.55 us
    pallas_call x1, Pallas kernels, on_device(): pl.pallas_call(make_band_kernel(late, heads, head_dim, count_rows, width)...  6.05 us
    pallas_call x1, Pallas kernels, on_device(): pl.pallas_call(make_project_kernel(slots, late, head_dim, count_rows), ou...  5.05 us
    select_n x1, other arithmetic, angle_tables(): signed = jnp.where(first[None, None, :], -sine, sine)  3.06 us
    pallas_call x1, Pallas kernels, on_device(): pl.pallas_call(make_query_kernel(head_dim), out_shape=jax.ShapeDtypeStruc...  2.46 us
    unnamed x18, local copies, waits for them, and re-layouts  1.91 us
    pallas_call x1, Pallas kernels, on_device(): pl.pallas_call(make_prep_kernel(tile_count, tile_rows, count_rows), out_s...  1.9 us
  transfers between devices with their start and end apart: 8, of which 1 were waited for; matrix products, arithmetic and copies ran while one was open for 14% of the time, Pallas kernels for 14%

profile of v8, /device:TPU:5, one launch (start us, length us, event | category | flops | bytes accessed | tf_op | source)
XLA Modules:
  0.0 53.1 jit_solution(12085675576336744576)
XLA Ops:
  0.0 0.0 copy-start.8
  0.0 0.7 %collective-permute-start = (s32[4]{0:T(128)}, s32[4]{0:T(128)S(1)}, u32[]{:S(2)}, u32[]{:S(2)}) collective-permute-start(s32[4]{0:T(128)} %bitcast.13), channel_id=1, source_target_pairs={{0,1},{1,0},{2,3},{3,2},{4,5},{5,4},{6,7},{7,6},{8,9},{9,8},{10,11... | collective-permute-start | bytes 56 | tf_op jit(solution)/shard_map/ppermute | solution.py:23
  0.7 0.7 %broadcast_multiply_fusion = (s32[7]{0:T(128)S(1)}, s32[7]{0:T(128)S(1)}) fusion(s32[7]{0:T(128)} %constant.81.clone, s32[]{:T(128)S(6)} %axis_index.15), kind=kLoop, calls=%fused_computation.24 | loop fusion | flops 14 | bytes 88 | tf_op jit(solution)/shard_map/mul | solution.py:70
  1.4 0.1 fusion.1
  1.4 0.1 mul.15
  1.5 1.3 %reshape.129.gain_ref = f32[1,768]{1,0:T(1,128)} reshape(f32[768]{0:T(1024)} %param.12) | data formatting | bytes 6144 | tf_op jit(solution)/shard_map/reshape | solution.py:251
  2.8 0.7 %compare_reduce_fusion = pred[7]{0:T(512)(128)(4,1)S(1)} fusion(s32[7]{0:T(128)S(1)} %get-tuple-element.18, s32[4]{0:T(128)} %bitcast.12), kind=kLoop, calls=%fused_computation.19 | loop fusion | flops 49 | bytes 51 | tf_op jit(solution)/shard_map/reduce_or | solution.py:255
  3.6 0.5 convert_bitcast_fusion
  4.1 0.2 reduce-window.9
  4.3 3.1 %negate_select_fusion = (f32[7,128,128]{2,1,0:T(8,128)}, f32[7,128,128]{2,1,0:T(8,128)}) fusion(f32[128]{0:T(128)S(1)} %mul.15, f32[7,128]{1,0:T(8,128)S(1)} %get-tuple-element.16, f32[7,128]{1,0:T(8,128)S(1)} %get-tuple-element.15, pred[128]{0:T(512)(128)(4,1)S(1)} %get-tuple-element.22, pred[128]{0:T(512)(128)(4,1)S(1)} %get-tuple-element.21), kind=kLoop, calls=%fused_computation | loop fusion | flops 458752 | bytes 925440 | tf_op jit(solution)/shard_map/jit(_where)/select_n | solution.py:82
  7.3 0.0 collective-permute-done.order_ref
  7.3 0.0 copy-start.7
  7.3 0.5 copy-done.7
  7.8 1.9 %shard_map.109 = (bf16[128,768]{1,0:T(8,128)(2,1)}, bf16[128,768]{1,0:T(8,128)(2,1)}) custom-call(s32[4]{0:T(128)} %copy-done.7, s32[4]{0:T(128)} %bitcast.11, bf16[128,768]{1,0:T(8,128)(2,1)} %bitcast.9, f32[1,768]{1,0:T(1,128)} %reshape.129.gain_ref), custom_call_target="tpu_custom_call" | custom-call | tf_op jit(solution)/shard_map/pallas_call | solution.py:243
  9.7 3.1 %collective-permute-start.2 = (bf16[128,768]{1,0:T(8,128)(2,1)}, bf16[128,768]{1,0:T(8,128)(2,1)S(1)}, u32[]{:S(2)}, u32[]{:S(2)}) collective-permute-start(bf16[128,768]{1,0:T(8,128)(2,1)} %get-tuple-element.10), channel_id=1, source_target_pairs={{1,4},{0,5},{3,6},{2,7},{5,8},{4,9},{7,10},{6,11},{9,12},{8,13},{1... | collective-permute-start | bytes 589832 | tf_op jit(solution)/shard_map/ppermute | solution.py:224
  12.8 3.5 %collective-permute-start.3 = (bf16[128,768]{1,0:T(8,128)(2,1)}, bf16[128,768]{1,0:T(8,128)(2,1)S(1)}, u32[]{:S(2)}, u32[]{:S(2)}) collective-permute-start(bf16[128,768]{1,0:T(8,128)(2,1)} %get-tuple-element.10), channel_id=1, source_target_pairs={{1,2},{0,3},{3,4},{2,5},{5,6},{4,7},{7,8},{6,9},{9,10},{8,11},{11,... | collective-permute-start | bytes 589832 | tf_op jit(solution)/shard_map/ppermute | solution.py:224
  16.4 0.5 bitcast_subtract_fusion.place_ref
  16.9 0.0 collective-permute-start.4
  16.9 2.5 %collective-permute-start.5 = (bf16[128,768]{1,0:T(8,128)(2,1)}, bf16[128,768]{1,0:T(8,128)(2,1)S(1)}, u32[]{:S(2)}, u32[]{:S(2)}) collective-permute-start(bf16[128,768]{1,0:T(8,128)(2,1)} %get-tuple-element.10), channel_id=1, source_target_pairs={{3,0},{2,1},{5,2},{4,3},{7,4},{6,5},{9,6},{8,7},{11,8},{10,9},{13,... | collective-permute-start | bytes 589832 | tf_op jit(solution)/shard_map/ppermute | solution.py:224
  19.4 1.3 %collective-permute-start.6 = (bf16[128,768]{1,0:T(8,128)(2,1)}, bf16[128,768]{1,0:T(8,128)(2,1)S(1)}, u32[]{:S(2)}, u32[]{:S(2)}) collective-permute-start(bf16[128,768]{1,0:T(8,128)(2,1)} %get-tuple-element.10), channel_id=1, source_target_pairs={{5,0},{4,1},{7,2},{6,3},{9,4},{8,5},{11,6},{10,7},{13,8},{12,9},{1... | collective-permute-start | bytes 589832 | tf_op jit(solution)/shard_map/ppermute | solution.py:224
  20.7 0.0 collective-permute-done.2.rest_0_
  20.7 0.0 copy-start
  20.8 1.3 %collective-permute-start.7 = (bf16[128,768]{1,0:T(8,128)(2,1)}, bf16[128,768]{1,0:T(8,128)(2,1)S(1)}, u32[]{:S(2)}, u32[]{:S(2)}) collective-permute-start(bf16[128,768]{1,0:T(8,128)(2,1)} %get-tuple-element.10), channel_id=1, source_target_pairs={{7,0},{6,1},{9,2},{8,3},{11,4},{10,5},{13,6},{12,7},{15,8},{14,9},... | collective-permute-start | bytes 589832 | tf_op jit(solution)/shard_map/ppermute | solution.py:224
  22.1 0.0 collective-permute-done.3.rest_1_
  22.1 0.0 copy-start.1
  22.1 8.0 %collective-permute-start.1 = (bf16[128,768]{1,0:T(8,128)(2,1)}, bf16[128,768]{1,0:T(8,128)(2,1)S(1)}, u32[]{:S(2)}, u32[]{:S(2)}) collective-permute-start(bf16[128,768]{1,0:T(8,128)(2,1)} %get-tuple-element.10), channel_id=1, source_target_pairs={{1,6},{0,7},{3,8},{2,9},{5,10},{4,11},{7,12},{6,13},{9,14},{8,15},... | collective-permute-start | bytes 589832 | tf_op jit(solution)/shard_map/ppermute | solution.py:224
  30.1 0.0 copy-done.8
  30.1 0.5 %broadcast_multiply_fusion.1.scale_ref = f32[12]{0:T(128)} fusion(f32[12]{0:T(128)S(1)} %copy-done.8), kind=kLoop, calls=%fused_computation.25 | loop fusion | flops 12 | bytes 96 | tf_op jit(solution)/shard_map/div | solution.py:257
  30.6 2.5 %shard_map.110.q_ref = bf16[128,768]{1,0:T(8,128)(2,1)} custom-call(bf16[128,768]{1,0:T(8,128)(2,1)} %get-tuple-element.9.x_ref, bf16[768,768]{1,0:T(8,128)(2,1)} %w_ref.1, f32[7,128,128]{2,1,0:T(8,128)} %get-tuple-element.14.cos_ref.rest_6_, f32[7,128,128]{2,1,0:T(8,128)} %get-tuple-element.13.sin_ref.rest_7_), custom_call_target="tpu_custom_call" | custom-call | tf_op jit(solution)/shard_map/pallas_call | solution.py:261
  33.1 0.0 copy-done
  33.1 0.0 copy-done.1
  33.1 0.0 collective-permute-done.4.rest_2_
  33.1 0.0 copy-start.2
  33.1 0.0 collective-permute-done.5.rest_3_
  33.1 0.0 copy-start.3
  33.1 0.0 collective-permute-done.6.rest_4_
  33.1 0.0 copy-start.4
  33.1 7.5 %collective-permute-done.7.rest_5_ = bf16[128,768]{1,0:T(8,128)(2,1)S(1)} collective-permute-done((bf16[128,768]{1,0:T(8,128)(2,1)}, bf16[128,768]{1,0:T(8,128)(2,1)S(1)}, u32[]{:S(2)}, u32[]{:S(2)}) %collective-permute-start.7) | collective-permute-done | bytes 196640 | tf_op jit(solution)/shard_map/ppermute | solution.py:224
  40.7 0.0 copy-start.6
  40.7 0.0 copy-done.2
  40.7 0.0 copy-done.3
  40.7 0.0 copy-done.4
  40.7 0.7 %copy-done.6 = bf16[128,768]{1,0:T(8,128)(2,1)} copy-done((bf16[128,768]{1,0:T(8,128)(2,1)}, bf16[128,768]{1,0:T(8,128)(2,1)S(1)}, u32[]{:S(2)}) %copy-start.6) | copy-done | bytes 196632
  41.4 5.0 %shard_map.111 = (bf16[512,768]{1,0:T(8,128)(2,1)}, bf16[512,768]{1,0:T(8,128)(2,1)}) custom-call(s32[7]{0:T(128)} %get-tuple-element.20.needed_ref, s32[7]{0:T(128)} %bitcast_subtract_fusion.place_ref, bf16[128,768]{1,0:T(8,128)(2,1)} %copy-done, bf16[128,768]{1,0:T(8,128)(2,1)} %copy-done.1, bf16[128,768]{1,0:T(8,128)(2,1)} %copy-done.2, ...), custom_call_target="tpu_custom_call" | custom-call | tf_op jit(solution)/shard_map/pallas_call | solution.py:276
  46.4 0.0 collective-permute-done.1.pay_ref
  46.4 0.0 copy-start.5
  46.4 0.7 %copy-done.5 = bf16[128,768]{1,0:T(8,128)(2,1)} copy-done((bf16[128,768]{1,0:T(8,128)(2,1)}, bf16[128,768]{1,0:T(8,128)(2,1)S(1)}, u32[]{:S(2)}) %copy-start.5) | copy-done | bytes 196632
  47.1 6.1 %shard_map.112 = bf16[128,768]{1,0:T(8,128)(2,1)} custom-call(s32[7]{0:T(128)} %get-tuple-element.20.needed_ref, s32[7]{0:T(128)} %bitcast_subtract_fusion.place_ref, f32[12]{0:T(128)} %broadcast_multiply_fusion.1.scale_ref, bf16[128,768]{1,0:T(8,128)(2,1)} %shard_map.110.q_ref, bf16[128,768]{1,0:T(8,128)(2,1)} %copy-done.5, ...), custom_call_target="tpu_custom_call" | custom-call | tf_op jit(solution)/shard_map/pallas_call | solution.py:287
  (3 shorter events, 0.0 us)
Async XLA Ops:
  0.0 30.1 %copy-start.8 = (f32[12]{0:T(128)S(1)}, f32[12]{0:T(128)}, u32[]{:S(2)}) copy-start(f32[12]{0:T(128)} %param.17) | copy-start | bytes 148
  0.0 7.3 %collective-permute-start = (s32[4]{0:T(128)}, s32[4]{0:T(128)S(1)}, u32[]{:S(2)}, u32[]{:S(2)}) collective-permute-start(s32[4]{0:T(128)} %bitcast.13), channel_id=1, source_target_pairs={{0,1},{1,0},{2,3},{3,2},{4,5},{5,4},{6,7},{7,6},{8,9},{9,8},{10,11... | collective-permute-start | bytes 56 | tf_op jit(solution)/shard_map/ppermute | solution.py:23
  7.3 0.5 copy-start.7
  9.7 11.0 %collective-permute-start.2 = (bf16[128,768]{1,0:T(8,128)(2,1)}, bf16[128,768]{1,0:T(8,128)(2,1)S(1)}, u32[]{:S(2)}, u32[]{:S(2)}) collective-permute-start(bf16[128,768]{1,0:T(8,128)(2,1)} %get-tuple-element.10), channel_id=1, source_target_pairs={{1,4},{0,5},{3,6},{2,7},{5,8},{4,9},{7,10},{6,11},{9,12},{8,13},{1... | collective-permute-start | bytes 589832 | tf_op jit(solution)/shard_map/ppermute | solution.py:224
  12.8 9.2 %collective-permute-start.3 = (bf16[128,768]{1,0:T(8,128)(2,1)}, bf16[128,768]{1,0:T(8,128)(2,1)S(1)}, u32[]{:S(2)}, u32[]{:S(2)}) collective-permute-start(bf16[128,768]{1,0:T(8,128)(2,1)} %get-tuple-element.10), channel_id=1, source_target_pairs={{1,2},{0,3},{3,4},{2,5},{5,6},{4,7},{7,8},{6,9},{9,10},{8,11},{11,... | collective-permute-start | bytes 589832 | tf_op jit(solution)/shard_map/ppermute | solution.py:224
  16.9 16.2 %collective-permute-start.4 = (bf16[128,768]{1,0:T(8,128)(2,1)}, bf16[128,768]{1,0:T(8,128)(2,1)S(1)}, u32[]{:S(2)}, u32[]{:S(2)}) collective-permute-start(bf16[128,768]{1,0:T(8,128)(2,1)} %get-tuple-element.10), channel_id=1, source_target_pairs={{0,1},{1,0},{2,3},{3,2},{4,5},{5,4},{6,7},{7,6},{8,9},{9,8},{10,11... | collective-permute-start | bytes 589832 | tf_op jit(solution)/shard_map/ppermute | solution.py:23
  16.9 16.2 %collective-permute-start.5 = (bf16[128,768]{1,0:T(8,128)(2,1)}, bf16[128,768]{1,0:T(8,128)(2,1)S(1)}, u32[]{:S(2)}, u32[]{:S(2)}) collective-permute-start(bf16[128,768]{1,0:T(8,128)(2,1)} %get-tuple-element.10), channel_id=1, source_target_pairs={{3,0},{2,1},{5,2},{4,3},{7,4},{6,5},{9,6},{8,7},{11,8},{10,9},{13,... | collective-permute-start | bytes 589832 | tf_op jit(solution)/shard_map/ppermute | solution.py:224
  19.4 13.7 %collective-permute-start.6 = (bf16[128,768]{1,0:T(8,128)(2,1)}, bf16[128,768]{1,0:T(8,128)(2,1)S(1)}, u32[]{:S(2)}, u32[]{:S(2)}) collective-permute-start(bf16[128,768]{1,0:T(8,128)(2,1)} %get-tuple-element.10), channel_id=1, source_target_pairs={{5,0},{4,1},{7,2},{6,3},{9,4},{8,5},{11,6},{10,7},{13,8},{12,9},{1... | collective-permute-start | bytes 589832 | tf_op jit(solution)/shard_map/ppermute | solution.py:224
  20.7 12.3 %copy-start = (bf16[128,768]{1,0:T(8,128)(2,1)}, bf16[128,768]{1,0:T(8,128)(2,1)S(1)}, u32[]{:S(2)}) copy-start(bf16[128,768]{1,0:T(8,128)(2,1)S(1)} %collective-permute-done.2.rest_0_) | copy-start | bytes 589828
  20.8 19.9 %collective-permute-start.7 = (bf16[128,768]{1,0:T(8,128)(2,1)}, bf16[128,768]{1,0:T(8,128)(2,1)S(1)}, u32[]{:S(2)}, u32[]{:S(2)}) collective-permute-start(bf16[128,768]{1,0:T(8,128)(2,1)} %get-tuple-element.10), channel_id=1, source_target_pairs={{7,0},{6,1},{9,2},{8,3},{11,4},{10,5},{13,6},{12,7},{15,8},{14,9},... | collective-permute-start | bytes 589832 | tf_op jit(solution)/shard_map/ppermute | solution.py:224
  22.1 11.0 %copy-start.1 = (bf16[128,768]{1,0:T(8,128)(2,1)}, bf16[128,768]{1,0:T(8,128)(2,1)S(1)}, u32[]{:S(2)}) copy-start(bf16[128,768]{1,0:T(8,128)(2,1)S(1)} %collective-permute-done.3.rest_1_) | copy-start | bytes 589828
  22.1 24.3 %collective-permute-start.1 = (bf16[128,768]{1,0:T(8,128)(2,1)}, bf16[128,768]{1,0:T(8,128)(2,1)S(1)}, u32[]{:S(2)}, u32[]{:S(2)}) collective-permute-start(bf16[128,768]{1,0:T(8,128)(2,1)} %get-tuple-element.10), channel_id=1, source_target_pairs={{1,6},{0,7},{3,8},{2,9},{5,10},{4,11},{7,12},{6,13},{9,14},{8,15},... | collective-permute-start | bytes 589832 | tf_op jit(solution)/shard_map/ppermute | solution.py:224
  33.1 7.6 %copy-start.2 = (bf16[128,768]{1,0:T(8,128)(2,1)}, bf16[128,768]{1,0:T(8,128)(2,1)S(1)}, u32[]{:S(2)}) copy-start(bf16[128,768]{1,0:T(8,128)(2,1)S(1)} %collective-permute-done.4.rest_2_) | copy-start | bytes 589828
  33.1 7.6 %copy-start.3 = (bf16[128,768]{1,0:T(8,128)(2,1)}, bf16[128,768]{1,0:T(8,128)(2,1)S(1)}, u32[]{:S(2)}) copy-start(bf16[128,768]{1,0:T(8,128)(2,1)S(1)} %collective-permute-done.5.rest_3_) | copy-start | bytes 589828
  33.1 7.6 %copy-start.4 = (bf16[128,768]{1,0:T(8,128)(2,1)}, bf16[128,768]{1,0:T(8,128)(2,1)S(1)}, u32[]{:S(2)}) copy-start(bf16[128,768]{1,0:T(8,128)(2,1)S(1)} %collective-permute-done.6.rest_4_) | copy-start | bytes 589828
  40.7 0.7 %copy-start.6 = (bf16[128,768]{1,0:T(8,128)(2,1)}, bf16[128,768]{1,0:T(8,128)(2,1)S(1)}, u32[]{:S(2)}) copy-start(bf16[128,768]{1,0:T(8,128)(2,1)S(1)} %collective-permute-done.7.rest_5_) | copy-start | bytes 589828
  46.4 0.7 %copy-start.5 = (bf16[128,768]{1,0:T(8,128)(2,1)}, bf16[128,768]{1,0:T(8,128)(2,1)S(1)}, u32[]{:S(2)}) copy-start(bf16[128,768]{1,0:T(8,128)(2,1)S(1)} %collective-permute-done.1.pay_ref) | copy-start | bytes 589828

commit v9 on v7

--- a/solution.py
+++ b/solution.py
@@ -90,9 +90,20 @@
     stacked = per_pair * count_rows
 
     def kernel(needed_ref, place_ref, scale_ref, q_ref, *rest):
-        payload_refs = rest[:slots]
-        (cos_ref, sin_ref, wk_ref, wv_ref, wo_ref, tok_ref, out_ref, k_buf, v_buf,
-         r_buf, c_buf, s_buf) = rest[slots:]
+        payload_hbm = rest[:slots]
+        (cos_ref, sin_ref, wk_ref, wv_ref, wo_hbm, tok_ref, out_ref, k_buf, v_buf,
+         r_buf, c_buf, s_buf, wo_ref, sems) = rest[slots:]
+        wo_copy = pltpu.make_async_copy(wo_hbm, wo_ref, sems.at[slots])
+        wo_copy.start()
+        copies = []
+        for slot in range(slots):
+            at = pl.ds(pl.multiple_of(place_ref[slot] * count_rows, count_rows), count_rows)
+            copies.append(pltpu.make_async_copy(payload_hbm[slot], r_buf.at[at], sems.at[slot]))
+
+            @pl.when(needed_ref[slot] != 0)
+            def _():
+                copies[slot].start()
+
         lane = lax.broadcasted_iota(jnp.int32, (count_rows, 128), 1)
         first = (lane % (2 * quarter)) < quarter
         head_of_lane = lane // head_dim
@@ -103,9 +114,14 @@
             @pl.when(needed_ref[slot] != 0)
             def _():
                 at = pl.ds(pl.multiple_of(place_ref[slot] * count_rows, count_rows), count_rows)
-                r_buf[at, :] = payload_refs[slot][...]
                 c_buf[at, :] = cos_ref[slot]
                 s_buf[at, :] = sin_ref[slot]
+
+        for slot in range(slots):
+
+            @pl.when(needed_ref[slot] != 0)
+            def _():
+                copies[slot].wait()
 
         rows = r_buf[...]
         kp = jnp.dot(rows, wk_ref[...], preferred_element_type=jnp.float32)
@@ -147,6 +163,7 @@
                 res = jnp.where(head_of_lane == sub, two[sub * count_rows:(sub + 1) * count_rows], res)
             parts.append(res.astype(jnp.bfloat16))
         attended = jnp.concatenate(parts, axis=1)
+        wo_copy.wait()
         mixed = tok_ref[...].astype(jnp.float32) + jnp.dot(
             attended, wo_ref[...], preferred_element_type=jnp.float32
         )
@@ -213,6 +230,7 @@
     block_index = lax.axis_index("tok")
     smem = pl.BlockSpec(memory_space=pltpu.SMEM)
     vmem = pl.BlockSpec(memory_space=pltpu.VMEM)
+    hbm = pl.BlockSpec(memory_space=pl.ANY)
     theirs = partner(matching[0], "ep", 0)
     tile_count = matching.shape[1]
     tile_rows = count_rows // tile_count
@@ -246,11 +264,11 @@
     received = [partner(payload, "ep", 0) if d == 0 else across(payload, d) for d in offsets]
     reads = stops.shape[-1]
     flags = needed.astype(jnp.int32)
-    place = jnp.cumsum(flags) - flags
+    place = jnp.minimum(jnp.cumsum(flags) - flags, reads - 1)
     out = pl.pallas_call(
         make_band_kernel(slots, reads, heads, head_dim, count_rows, width),
         out_shape=jax.ShapeDtypeStruct((count_rows, width), jnp.bfloat16),
-        in_specs=[smem, smem, smem] + [vmem] * (1 + slots + 6),
+        in_specs=[smem, smem, smem, vmem] + [hbm] * slots + [vmem] * 4 + [hbm, vmem],
         out_specs=vmem,
         scratch_shapes=[
             pltpu.VMEM((reads * count_rows, width), jnp.bfloat16),
@@ -258,6 +276,8 @@
             pltpu.VMEM((reads * count_rows, width), jnp.bfloat16),
             pltpu.VMEM((reads * count_rows, 128), jnp.float32),
             pltpu.VMEM((reads * count_rows, 128), jnp.float32),
+            pltpu.VMEM((width, width), jnp.bfloat16),
+            pltpu.SemaphoreType.DMA((slots + 1,)),
         ],
     )(flags, place, scales, queries, *received, cosine, signed, w_key, w_value, w_out, tokens[0])
     return out[None]

time: 48.7 us -> 49.4 us (1.014)
  Pallas kernels: 11.8 us -> 12.4 us
    pallas_call x1, Pallas kernels: 7.44 us -> 8.09 us  [on_device(): pl.pallas_call(make_band_kernel(slots, reads, heads, head_dim, count_rows...]
    min x0 -> x1, other arithmetic: none -> 0.52 us  [on_device(): place = jnp.minimum(jnp.cumsum(flags) - flags, reads - 1)]
    sub x1 -> x0, other arithmetic: 0.52 us -> none  [on_device(): place = jnp.cumsum(flags) - flags]
where the time goes in v9:
time: 49.4 us; the launch traced here: 49 us
  starting transfers between devices  14.2 us (29%)
  waiting for transfers between devices  13.4 us (27%)
  Pallas kernels  12.4 us (25%)
  other arithmetic  6.35 us (13%)
  local copies, waits for them, and re-layouts  2.56 us (5%)
    ppermute x6, waiting for transfers between devices, across(): return lax.ppermute(shard, ('tok', 'ep'), pairs)  13.4 us
    ppermute x6, starting transfers between devices, across(): return lax.ppermute(shard, ('tok', 'ep'), pairs)  12.9 us
    pallas_call x1, Pallas kernels, on_device(): pl.pallas_call(make_band_kernel(slots, reads, heads, head_dim, count_rows...  8.09 us
    select_n x1, other arithmetic, angle_tables(): signed = jnp.where(first[None, None, :], -sine, sine)  3 us
    pallas_call x1, Pallas kernels, on_device(): pl.pallas_call(make_query_kernel(head_dim), out_shape=jax.ShapeDtypeStruc...  2.44 us
    pallas_call x1, Pallas kernels, on_device(): pl.pallas_call(make_prep_kernel(tile_count, tile_rows, count_rows), out_s...  1.9 us
    reshape x1, local copies, waits for them, and re-layouts, on_device(): norm_gain.reshape(1, width)  1.28 us
    ppermute x2, starting transfers between devices, partner(): return lax.ppermute(block, axis, route)  1.24 us
  transfers between devices with their start and end apart: 8, of which 3 were waited for; matrix products, arithmetic and copies ran while one was open for 16% of the time, Pallas kernels for 5%

profile of v9, /device:TPU:27, one launch (start us, length us, event | category | flops | bytes accessed | tf_op | source)
XLA Modules:
  0.0 49.0 jit_solution(13743271472201843072)
XLA Ops:
  0.0 0.0 copy-start.8
  0.0 0.7 %collective-permute-start = (s32[4]{0:T(128)}, s32[4]{0:T(128)S(1)}, u32[]{:S(2)}, u32[]{:S(2)}) collective-permute-start(s32[4]{0:T(128)} %bitcast.15), channel_id=1, source_target_pairs={{0,1},{1,0},{2,3},{3,2},{4,5},{5,4},{6,7},{7,6},{8,9},{9,8},{10,11... | collective-permute-start | bytes 56 | tf_op jit(solution)/shard_map/ppermute | solution.py:23
  0.7 0.7 %broadcast_multiply_fusion = (s32[7]{0:T(128)S(1)}, s32[7]{0:T(128)S(1)}) fusion(s32[7]{0:T(128)} %constant.83.clone, s32[]{:T(128)S(6)} %axis_index.15), kind=kLoop, calls=%fused_computation.25 | loop fusion | flops 14 | bytes 88 | tf_op jit(solution)/shard_map/mul | solution.py:70
  1.4 0.7 %compare_reduce_fusion = pred[7]{0:T(512)(128)(4,1)S(1)} fusion(s32[7]{0:T(128)S(1)} %get-tuple-element.14, s32[4]{0:T(128)} %bitcast.14), kind=kLoop, calls=%fused_computation.19 | loop fusion | flops 49 | bytes 51 | tf_op jit(solution)/shard_map/reduce_or | solution.py:249
  2.1 0.6 %convert_bitcast_fusion = (s32[7,1]{0,1:T(1,128)S(1)}, s32[7]{0:T(128)}) fusion(pred[7]{0:T(512)(128)(4,1)S(1)} %compare_reduce_fusion), kind=kLoop, calls=%fused_computation.28 | loop fusion | flops 7 | bytes 63 | tf_op jit(solution)/shard_map/convert_element_type | solution.py:266
  2.7 1.3 %reshape.129.gain_ref = f32[1,768]{1,0:T(1,128)} reshape(f32[768]{0:T(1024)} %param.12) | data formatting | bytes 6144 | tf_op jit(solution)/shard_map/reshape | solution.py:245
  4.0 0.1 mul.15
  4.1 0.1 fusion.1
  4.1 0.2 reduce-window.9
  4.3 3.0 %negate_select_fusion = (f32[7,128,128]{2,1,0:T(8,128)}, f32[7,128,128]{2,1,0:T(8,128)}) fusion(f32[128]{0:T(128)S(1)} %mul.15, f32[7,128]{1,0:T(8,128)S(1)} %get-tuple-element.12, f32[7,128]{1,0:T(8,128)S(1)} %get-tuple-element.11, pred[128]{0:T(512)(128)(4,1)S(1)} %get-tuple-element.18, pred[128]{0:T(512)(128)(4,1)S(1)} %get-tuple-element.17), kind=kLoop, calls=%fused_computation | loop fusion | flops 458752 | bytes 925440 | tf_op jit(solution)/shard_map/jit(_where)/select_n | solution.py:82
  7.3 0.0 collective-permute-done.order_ref
  7.3 0.0 copy-start.7
  7.3 0.5 %copy-done.7 = s32[4]{0:T(128)} copy-done((s32[4]{0:T(128)}, s32[4]{0:T(128)S(1)}, u32[]{:S(2)}) %copy-start.7) | copy-done | bytes 40
  7.9 1.9 %shard_map.109 = (bf16[128,768]{1,0:T(8,128)(2,1)}, bf16[128,768]{1,0:T(8,128)(2,1)}) custom-call(s32[4]{0:T(128)} %copy-done.7, s32[4]{0:T(128)} %bitcast.13, bf16[128,768]{1,0:T(8,128)(2,1)} %bitcast.11, f32[1,768]{1,0:T(1,128)} %reshape.129.gain_ref), custom_call_target="tpu_custom_call" | custom-call | tf_op jit(solution)/shard_map/pallas_call | solution.py:237
  9.8 2.8 %collective-permute-start.7 = (bf16[128,768]{1,0:T(8,128)(2,1)}, bf16[128,768]{1,0:T(8,128)(2,1)S(1)}, u32[]{:S(2)}, u32[]{:S(2)}) collective-permute-start(bf16[128,768]{1,0:T(8,128)(2,1)} %get-tuple-element.8), channel_id=1, source_target_pairs={{7,0},{6,1},{9,2},{8,3},{11,4},{10,5},{13,6},{12,7},{15,8},{14,9},... | collective-permute-start | bytes 589832 | tf_op jit(solution)/shard_map/ppermute | solution.py:217
  12.6 2.5 %collective-permute-start.6 = (bf16[128,768]{1,0:T(8,128)(2,1)}, bf16[128,768]{1,0:T(8,128)(2,1)S(1)}, u32[]{:S(2)}, u32[]{:S(2)}) collective-permute-start(bf16[128,768]{1,0:T(8,128)(2,1)} %get-tuple-element.8), channel_id=1, source_target_pairs={{5,0},{4,1},{7,2},{6,3},{9,4},{8,5},{11,6},{10,7},{13,8},{12,9},{1... | collective-permute-start | bytes 589832 | tf_op jit(solution)/shard_map/ppermute | solution.py:217
  15.0 0.5 %fusion.10.place_ref = s32[7]{0:T(128)} fusion(s32[7,1]{0,1:T(1,128)S(1)} %reduce-window.9, pred[7]{0:T(512)(128)(4,1)S(1)} %compare_reduce_fusion), kind=kLoop, calls=%fused_computation.23 | loop fusion | flops 21 | bytes 63 | tf_op jit(solution)/shard_map/min | solution.py:267
  15.6 2.0 %collective-permute-start.5 = (bf16[128,768]{1,0:T(8,128)(2,1)}, bf16[128,768]{1,0:T(8,128)(2,1)S(1)}, u32[]{:S(2)}, u32[]{:S(2)}) collective-permute-start(bf16[128,768]{1,0:T(8,128)(2,1)} %get-tuple-element.8), channel_id=1, source_target_pairs={{3,0},{2,1},{5,2},{4,3},{7,4},{6,5},{9,6},{8,7},{11,8},{10,9},{13,... | collective-permute-start | bytes 589832 | tf_op jit(solution)/shard_map/ppermute | solution.py:217
  17.6 0.6 %collective-permute-start.4 = (bf16[128,768]{1,0:T(8,128)(2,1)}, bf16[128,768]{1,0:T(8,128)(2,1)S(1)}, u32[]{:S(2)}, u32[]{:S(2)}) collective-permute-start(bf16[128,768]{1,0:T(8,128)(2,1)} %get-tuple-element.8), channel_id=1, source_target_pairs={{0,1},{1,0},{2,3},{3,2},{4,5},{5,4},{6,7},{7,6},{8,9},{9,8},{10,11... | collective-permute-start | bytes 589832 | tf_op jit(solution)/shard_map/ppermute | solution.py:23
  18.2 3.1 %collective-permute-start.3 = (bf16[128,768]{1,0:T(8,128)(2,1)}, bf16[128,768]{1,0:T(8,128)(2,1)S(1)}, u32[]{:S(2)}, u32[]{:S(2)}) collective-permute-start(bf16[128,768]{1,0:T(8,128)(2,1)} %get-tuple-element.8), channel_id=1, source_target_pairs={{1,2},{0,3},{3,4},{2,5},{5,6},{4,7},{7,8},{6,9},{9,10},{8,11},{11,... | collective-permute-start | bytes 589832 | tf_op jit(solution)/shard_map/ppermute | solution.py:217
  21.2 0.0 collective-permute-done.7.rest_6_
  21.2 0.0 copy-start
  21.2 1.3 %collective-permute-start.2 = (bf16[128,768]{1,0:T(8,128)(2,1)}, bf16[128,768]{1,0:T(8,128)(2,1)S(1)}, u32[]{:S(2)}, u32[]{:S(2)}) collective-permute-start(bf16[128,768]{1,0:T(8,128)(2,1)} %get-tuple-element.8), channel_id=1, source_target_pairs={{1,4},{0,5},{3,6},{2,7},{5,8},{4,9},{7,10},{6,11},{9,12},{8,13},{1... | collective-permute-start | bytes 589832 | tf_op jit(solution)/shard_map/ppermute | solution.py:217
  22.5 0.0 collective-permute-done.6.rest_5_
  22.6 0.0 copy-start.1
  22.6 1.3 %collective-permute-start.1 = (bf16[128,768]{1,0:T(8,128)(2,1)}, bf16[128,768]{1,0:T(8,128)(2,1)S(1)}, u32[]{:S(2)}, u32[]{:S(2)}) collective-permute-start(bf16[128,768]{1,0:T(8,128)(2,1)} %get-tuple-element.8), channel_id=1, source_target_pairs={{1,6},{0,7},{3,8},{2,9},{5,10},{4,11},{7,12},{6,13},{9,14},{8,15},... | collective-permute-start | bytes 589832 | tf_op jit(solution)/shard_map/ppermute | solution.py:217
  23.9 0.0 copy-done.8
  23.9 0.5 %broadcast_multiply_fusion.1.scale_ref = f32[12]{0:T(128)} fusion(f32[12]{0:T(128)S(1)} %copy-done.8), kind=kLoop, calls=%fused_computation.26 | loop fusion | flops 12 | bytes 96 | tf_op jit(solution)/shard_map/div | solution.py:251
  24.4 2.4 %shard_map.110.q_ref = bf16[128,768]{1,0:T(8,128)(2,1)} custom-call(bf16[128,768]{1,0:T(8,128)(2,1)} %get-tuple-element.7.x_ref, bf16[768,768]{1,0:T(8,128)(2,1)} %w_ref.1, f32[7,128,128]{2,1,0:T(8,128)} %get-tuple-element.10.cos_ref.rest_7_, f32[7,128,128]{2,1,0:T(8,128)} %get-tuple-element.9.sin_ref.rest_8_), custom_call_target="tpu_custom_call" | custom-call | tf_op jit(solution)/shard_map/pallas_call | solution.py:255
  26.9 0.0 copy-done
  26.9 0.0 copy-done.1
  26.9 1.8 %collective-permute-done.5.rest_4_ = bf16[128,768]{1,0:T(8,128)(2,1)S(1)} collective-permute-done((bf16[128,768]{1,0:T(8,128)(2,1)}, bf16[128,768]{1,0:T(8,128)(2,1)S(1)}, u32[]{:S(2)}, u32[]{:S(2)}) %collective-permute-start.5) | collective-permute-done | bytes 196640 | tf_op jit(solution)/shard_map/ppermute | solution.py:217
  28.7 0.0 copy-start.2
  28.7 0.0 collective-permute-done.4.rest_3_
  28.7 0.0 copy-start.3
  28.7 0.0 collective-permute-done.3.rest_2_
  28.7 0.0 copy-start.4
  28.7 1.9 %collective-permute-done.2.rest_1_ = bf16[128,768]{1,0:T(8,128)(2,1)S(1)} collective-permute-done((bf16[128,768]{1,0:T(8,128)(2,1)}, bf16[128,768]{1,0:T(8,128)(2,1)S(1)}, u32[]{:S(2)}, u32[]{:S(2)}) %collective-permute-start.2) | collective-permute-done | bytes 196640 | tf_op jit(solution)/shard_map/ppermute | solution.py:217
  30.6 0.0 copy-start.5
  30.6 9.7 %collective-permute-done.1.rest_0_ = bf16[128,768]{1,0:T(8,128)(2,1)S(1)} collective-permute-done((bf16[128,768]{1,0:T(8,128)(2,1)}, bf16[128,768]{1,0:T(8,128)(2,1)S(1)}, u32[]{:S(2)}, u32[]{:S(2)}) %collective-permute-start.1) | collective-permute-done | bytes 196640 | tf_op jit(solution)/shard_map/ppermute | solution.py:217
  40.3 0.0 copy-start.6
  40.3 0.0 copy-done.2
  40.3 0.0 copy-done.3
  40.3 0.0 copy-done.4
  40.3 0.0 copy-done.5
  40.3 0.6 %copy-done.6 = bf16[128,768]{1,0:T(8,128)(2,1)} copy-done((bf16[128,768]{1,0:T(8,128)(2,1)}, bf16[128,768]{1,0:T(8,128)(2,1)S(1)}, u32[]{:S(2)}) %copy-start.6) | copy-done | bytes 196632
  40.9 8.1 %shard_map.111 = bf16[128,768]{1,0:T(8,128)(2,1)} custom-call(s32[7]{0:T(128)} %get-tuple-element.16.needed_ref, s32[7]{0:T(128)} %fusion.10.place_ref, f32[12]{0:T(128)} %broadcast_multiply_fusion.1.scale_ref, bf16[128,768]{1,0:T(8,128)(2,1)} %shard_map.110.q_ref, bf16[128,768]{1,0:T(8,128)(2,1)} %copy-done.6, bf16[128,768]{1,0:T(8,128)(2,1)} %copy-done.5, ...), custom_call_target="tpu_custom_call" | custom-call | tf_op jit(solution)/shard_map/pallas_call | solution.py:268
  (3 shorter events, 0.0 us)
Async XLA Ops:
  0.0 23.9 %copy-start.8 = (f32[12]{0:T(128)S(1)}, f32[12]{0:T(128)}, u32[]{:S(2)}) copy-start(f32[12]{0:T(128)} %param.17) | copy-start | bytes 148
  0.0 7.3 %collective-permute-start = (s32[4]{0:T(128)}, s32[4]{0:T(128)S(1)}, u32[]{:S(2)}, u32[]{:S(2)}) collective-permute-start(s32[4]{0:T(128)} %bitcast.15), channel_id=1, source_target_pairs={{0,1},{1,0},{2,3},{3,2},{4,5},{5,4},{6,7},{7,6},{8,9},{9,8},{10,11... | collective-permute-start | bytes 56 | tf_op jit(solution)/shard_map/ppermute | solution.py:23
  7.3 0.5 %copy-start.7 = (s32[4]{0:T(128)}, s32[4]{0:T(128)S(1)}, u32[]{:S(2)}) copy-start(s32[4]{0:T(128)S(1)} %collective-permute-done.order_ref) | copy-start | bytes 52
  9.8 11.5 %collective-permute-start.7 = (bf16[128,768]{1,0:T(8,128)(2,1)}, bf16[128,768]{1,0:T(8,128)(2,1)S(1)}, u32[]{:S(2)}, u32[]{:S(2)}) collective-permute-start(bf16[128,768]{1,0:T(8,128)(2,1)} %get-tuple-element.8), channel_id=1, source_target_pairs={{7,0},{6,1},{9,2},{8,3},{11,4},{10,5},{13,6},{12,7},{15,8},{14,9},... | collective-permute-start | bytes 589832 | tf_op jit(solution)/shard_map/ppermute | solution.py:217
  12.6 10.0 %collective-permute-start.6 = (bf16[128,768]{1,0:T(8,128)(2,1)}, bf16[128,768]{1,0:T(8,128)(2,1)S(1)}, u32[]{:S(2)}, u32[]{:S(2)}) collective-permute-start(bf16[128,768]{1,0:T(8,128)(2,1)} %get-tuple-element.8), channel_id=1, source_target_pairs={{5,0},{4,1},{7,2},{6,3},{9,4},{8,5},{11,6},{10,7},{13,8},{12,9},{1... | collective-permute-start | bytes 589832 | tf_op jit(solution)/shard_map/ppermute | solution.py:217
  15.6 13.1 %collective-permute-start.5 = (bf16[128,768]{1,0:T(8,128)(2,1)}, bf16[128,768]{1,0:T(8,128)(2,1)S(1)}, u32[]{:S(2)}, u32[]{:S(2)}) collective-permute-start(bf16[128,768]{1,0:T(8,128)(2,1)} %get-tuple-element.8), channel_id=1, source_target_pairs={{3,0},{2,1},{5,2},{4,3},{7,4},{6,5},{9,6},{8,7},{11,8},{10,9},{13,... | collective-permute-start | bytes 589832 | tf_op jit(solution)/shard_map/ppermute | solution.py:217
  17.6 11.1 %collective-permute-start.4 = (bf16[128,768]{1,0:T(8,128)(2,1)}, bf16[128,768]{1,0:T(8,128)(2,1)S(1)}, u32[]{:S(2)}, u32[]{:S(2)}) collective-permute-start(bf16[128,768]{1,0:T(8,128)(2,1)} %get-tuple-element.8), channel_id=1, source_target_pairs={{0,1},{1,0},{2,3},{3,2},{4,5},{5,4},{6,7},{7,6},{8,9},{9,8},{10,11... | collective-permute-start | bytes 589832 | tf_op jit(solution)/shard_map/ppermute | solution.py:23
  18.2 10.6 %collective-permute-start.3 = (bf16[128,768]{1,0:T(8,128)(2,1)}, bf16[128,768]{1,0:T(8,128)(2,1)S(1)}, u32[]{:S(2)}, u32[]{:S(2)}) collective-permute-start(bf16[128,768]{1,0:T(8,128)(2,1)} %get-tuple-element.8), channel_id=1, source_target_pairs={{1,2},{0,3},{3,4},{2,5},{5,6},{4,7},{7,8},{6,9},{9,10},{8,11},{11,... | collective-permute-start | bytes 589832 | tf_op jit(solution)/shard_map/ppermute | solution.py:217
  21.2 5.6 %copy-start = (bf16[128,768]{1,0:T(8,128)(2,1)}, bf16[128,768]{1,0:T(8,128)(2,1)S(1)}, u32[]{:S(2)}) copy-start(bf16[128,768]{1,0:T(8,128)(2,1)S(1)} %collective-permute-done.7.rest_6_) | copy-start | bytes 589828
  21.2 9.3 %collective-permute-start.2 = (bf16[128,768]{1,0:T(8,128)(2,1)}, bf16[128,768]{1,0:T(8,128)(2,1)S(1)}, u32[]{:S(2)}, u32[]{:S(2)}) collective-permute-start(bf16[128,768]{1,0:T(8,128)(2,1)} %get-tuple-element.8), channel_id=1, source_target_pairs={{1,4},{0,5},{3,6},{2,7},{5,8},{4,9},{7,10},{6,11},{9,12},{8,13},{1... | collective-permute-start | bytes 589832 | tf_op jit(solution)/shard_map/ppermute | solution.py:217
  22.6 4.3 %copy-start.1 = (bf16[128,768]{1,0:T(8,128)(2,1)}, bf16[128,768]{1,0:T(8,128)(2,1)S(1)}, u32[]{:S(2)}) copy-start(bf16[128,768]{1,0:T(8,128)(2,1)S(1)} %collective-permute-done.6.rest_5_) | copy-start | bytes 589828
  22.6 17.7 %collective-permute-start.1 = (bf16[128,768]{1,0:T(8,128)(2,1)}, bf16[128,768]{1,0:T(8,128)(2,1)S(1)}, u32[]{:S(2)}, u32[]{:S(2)}) collective-permute-start(bf16[128,768]{1,0:T(8,128)(2,1)} %get-tuple-element.8), channel_id=1, source_target_pairs={{1,6},{0,7},{3,8},{2,9},{5,10},{4,11},{7,12},{6,13},{9,14},{8,15},... | collective-permute-start | bytes 589832 | tf_op jit(solution)/shard_map/ppermute | solution.py:217
  28.7 11.6 %copy-start.2 = (bf16[128,768]{1,0:T(8,128)(2,1)}, bf16[128,768]{1,0:T(8,128)(2,1)S(1)}, u32[]{:S(2)}) copy-start(bf16[128,768]{1,0:T(8,128)(2,1)S(1)} %collective-permute-done.5.rest_4_) | copy-start | bytes 589828
  28.7 11.6 %copy-start.3 = (bf16[128,768]{1,0:T(8,128)(2,1)}, bf16[128,768]{1,0:T(8,128)(2,1)S(1)}, u32[]{:S(2)}) copy-start(bf16[128,768]{1,0:T(8,128)(2,1)S(1)} %collective-permute-done.4.rest_3_) | copy-start | bytes 589828
  28.7 11.6 %copy-start.4 = (bf16[128,768]{1,0:T(8,128)(2,1)}, bf16[128,768]{1,0:T(8,128)(2,1)S(1)}, u32[]{:S(2)}) copy-start(bf16[128,768]{1,0:T(8,128)(2,1)S(1)} %collective-permute-done.3.rest_2_) | copy-start | bytes 589828
  30.6 9.7 %copy-start.5 = (bf16[128,768]{1,0:T(8,128)(2,1)}, bf16[128,768]{1,0:T(8,128)(2,1)S(1)}, u32[]{:S(2)}) copy-start(bf16[128,768]{1,0:T(8,128)(2,1)S(1)} %collective-permute-done.2.rest_1_) | copy-start | bytes 589828
  40.3 0.7 %copy-start.6 = (bf16[128,768]{1,0:T(8,128)(2,1)}, bf16[128,768]{1,0:T(8,128)(2,1)S(1)}, u32[]{:S(2)}) copy-start(bf16[128,768]{1,0:T(8,128)(2,1)S(1)} %collective-permute-done.1.rest_0_) | copy-start | bytes 589828

commit v10 on v7

--- a/solution.py
+++ b/solution.py
@@ -226,6 +226,7 @@
         out_specs=(vmem, vmem),
     )(theirs, valid[0], tokens[0], norm_gain.reshape(1, width))
 
+    _, block_index = lax.optimization_barrier((payload, block_index))
     offsets = list(range(-BAND, BAND + 1))
     blocks = block_index + jnp.array(offsets, dtype=jnp.int32)
     needed = jnp.any(stops[0, 0][None, :] == blocks[:, None], axis=1)

time: 48.7 us -> 51.2 us (1.051)
  waiting for transfers between devices: 13.4 us -> 15 us
  other arithmetic: 6.35 us -> 7 us
    ppermute x6, waiting for transfers between devices: 13.4 us -> 15 us  [across(): return lax.ppermute(shard, ('tok', 'ep'), pairs)]
    div x1, other arithmetic: 0.55 us -> 1.25 us  [on_device(): scales = (head_scale / math.sqrt(head_dim)).astype(jnp.float32)]
  transfers between devices with their start and end apart: 8 -> 8, of which waited for: 3 -> 2; matrix products, arithmetic and copies ran while one was open for 16% -> 16% of each run, Pallas kernels for 5% -> 5%
where the time goes in v10:
time: 51.2 us; the launch traced here: 50.8 us
  waiting for transfers between devices  15 us (29%)
  starting transfers between devices  14.2 us (28%)
  Pallas kernels  11.8 us (23%)
  other arithmetic  7 us (14%)
  local copies, waits for them, and re-layouts  2.62 us (5%)
    ppermute x6, waiting for transfers between devices, across(): return lax.ppermute(shard, ('tok', 'ep'), pairs)  15 us
    ppermute x6, starting transfers between devices, across(): return lax.ppermute(shard, ('tok', 'ep'), pairs)  12.9 us
    pallas_call x1, Pallas kernels, on_device(): pl.pallas_call(make_band_kernel(slots, reads, heads, head_dim, count_rows...  7.43 us
    select_n x1, other arithmetic, angle_tables(): signed = jnp.where(first[None, None, :], -sine, sine)  3 us
    pallas_call x1, Pallas kernels, on_device(): pl.pallas_call(make_query_kernel(head_dim), out_shape=jax.ShapeDtypeStruc...  2.48 us
    pallas_call x1, Pallas kernels, on_device(): pl.pallas_call(make_prep_kernel(tile_count, tile_rows, count_rows), out_s...  1.92 us
    reshape x1, local copies, waits for them, and re-layouts, on_device(): norm_gain.reshape(1, width)  1.28 us
    unnamed x18, local copies, waits for them, and re-layouts  1.26 us
  transfers between devices with their start and end apart: 8, of which 2 were waited for; matrix products, arithmetic and copies ran while one was open for 16% of the time, Pallas kernels for 5%

profile of v10, /device:TPU:27, one launch (start us, length us, event | category | flops | bytes accessed | tf_op | source)
XLA Modules:
  0.0 50.8 jit_solution(4378231807135881989)
XLA Ops:
  0.0 0.7 %collective-permute-start = (s32[4]{0:T(128)}, s32[4]{0:T(128)S(1)}, u32[]{:S(2)}, u32[]{:S(2)}) collective-permute-start(s32[4]{0:T(128)} %bitcast.12), channel_id=1, source_target_pairs={{0,1},{1,0},{2,3},{3,2},{4,5},{5,4},{6,7},{7,6},{8,9},{9,8},{10,11... | collective-permute-start | bytes 56 | tf_op jit(solution)/shard_map/ppermute | solution.py:23
  0.7 1.3 %broadcast_multiply_fusion.1.scale_ref = f32[12]{0:T(128)} fusion(f32[12]{0:T(128)} %param.17), kind=kLoop, calls=%fused_computation.25 | loop fusion | flops 12 | bytes 96 | tf_op jit(solution)/shard_map/div | solution.py:234
  1.9 1.3 %reshape.128.gain_ref = f32[1,768]{1,0:T(1,128)} reshape(f32[768]{0:T(1024)} %param.12) | data formatting | bytes 6144 | tf_op jit(solution)/shard_map/reshape | solution.py:227
  3.2 0.1 mul.15
  3.3 0.0 collective-permute-done.order_ref
  3.3 0.0 copy-start.7
  3.3 0.6 %copy-done.7 = s32[4]{0:T(128)} copy-done((s32[4]{0:T(128)}, s32[4]{0:T(128)S(1)}, u32[]{:S(2)}) %copy-start.7) | copy-done | bytes 40
  3.9 1.9 %shard_map.109 = (bf16[128,768]{1,0:T(8,128)(2,1)}, bf16[128,768]{1,0:T(8,128)(2,1)}) custom-call(s32[4]{0:T(128)} %copy-done.7, s32[4]{0:T(128)} %bitcast.11, bf16[128,768]{1,0:T(8,128)(2,1)} %bitcast.9, f32[1,768]{1,0:T(1,128)} %reshape.128.gain_ref), custom_call_target="tpu_custom_call" | custom-call | tf_op jit(solution)/shard_map/pallas_call | solution.py:219
  5.8 2.8 %collective-permute-start.7 = (bf16[128,768]{1,0:T(8,128)(2,1)}, bf16[128,768]{1,0:T(8,128)(2,1)S(1)}, u32[]{:S(2)}, u32[]{:S(2)}) collective-permute-start(bf16[128,768]{1,0:T(8,128)(2,1)} %get-tuple-element.8), channel_id=1, source_target_pairs={{7,0},{6,1},{9,2},{8,3},{11,4},{10,5},{13,6},{12,7},{15,8},{14,9},... | collective-permute-start | bytes 589832 | tf_op jit(solution)/shard_map/ppermute | solution.py:200
  8.6 2.5 %collective-permute-start.6 = (bf16[128,768]{1,0:T(8,128)(2,1)}, bf16[128,768]{1,0:T(8,128)(2,1)S(1)}, u32[]{:S(2)}, u32[]{:S(2)}) collective-permute-start(bf16[128,768]{1,0:T(8,128)(2,1)} %get-tuple-element.8), channel_id=1, source_target_pairs={{5,0},{4,1},{7,2},{6,3},{9,4},{8,5},{11,6},{10,7},{13,8},{12,9},{1... | collective-permute-start | bytes 589832 | tf_op jit(solution)/shard_map/ppermute | solution.py:200
  11.1 2.0 %collective-permute-start.5 = (bf16[128,768]{1,0:T(8,128)(2,1)}, bf16[128,768]{1,0:T(8,128)(2,1)S(1)}, u32[]{:S(2)}, u32[]{:S(2)}) collective-permute-start(bf16[128,768]{1,0:T(8,128)(2,1)} %get-tuple-element.8), channel_id=1, source_target_pairs={{3,0},{2,1},{5,2},{4,3},{7,4},{6,5},{9,6},{8,7},{11,8},{10,9},{13,... | collective-permute-start | bytes 589832 | tf_op jit(solution)/shard_map/ppermute | solution.py:200
  13.2 0.6 %collective-permute-start.4 = (bf16[128,768]{1,0:T(8,128)(2,1)}, bf16[128,768]{1,0:T(8,128)(2,1)S(1)}, u32[]{:S(2)}, u32[]{:S(2)}) collective-permute-start(bf16[128,768]{1,0:T(8,128)(2,1)} %get-tuple-element.8), channel_id=1, source_target_pairs={{0,1},{1,0},{2,3},{3,2},{4,5},{5,4},{6,7},{7,6},{8,9},{9,8},{10,11... | collective-permute-start | bytes 589832 | tf_op jit(solution)/shard_map/ppermute | solution.py:23
  13.7 3.1 %collective-permute-start.3 = (bf16[128,768]{1,0:T(8,128)(2,1)}, bf16[128,768]{1,0:T(8,128)(2,1)S(1)}, u32[]{:S(2)}, u32[]{:S(2)}) collective-permute-start(bf16[128,768]{1,0:T(8,128)(2,1)} %get-tuple-element.8), channel_id=1, source_target_pairs={{1,2},{0,3},{3,4},{2,5},{5,6},{4,7},{7,8},{6,9},{9,10},{8,11},{11,... | collective-permute-start | bytes 589832 | tf_op jit(solution)/shard_map/ppermute | solution.py:200
  16.8 0.7 %broadcast_multiply_fusion = (s32[7]{0:T(128)S(1)}, s32[7]{0:T(128)S(1)}) fusion(s32[7]{0:T(128)} %constant.81.clone, s32[]{:T(128)S(6)} %axis_index.15), kind=kLoop, calls=%fused_computation.24 | loop fusion | flops 14 | bytes 88 | tf_op jit(solution)/shard_map/mul | solution.py:70
  17.4 0.7 %compare_reduce_fusion = pred[7]{0:T(512)(128)(4,1)S(1)} fusion(s32[7]{0:T(128)S(1)} %get-tuple-element.16, s32[4]{0:T(128)} %bitcast.13), kind=kLoop, calls=%fused_computation.19 | loop fusion | flops 49 | bytes 51 | tf_op jit(solution)/shard_map/reduce_or | solution.py:232
  18.2 0.5 %convert_bitcast_fusion = (s32[7,1]{0,1:T(1,128)S(1)}, s32[7]{0:T(128)}) fusion(pred[7]{0:T(512)(128)(4,1)S(1)} %compare_reduce_fusion), kind=kLoop, calls=%fused_computation.27 | loop fusion | flops 7 | bytes 63 | tf_op jit(solution)/shard_map/convert_element_type | solution.py:249
  18.7 0.1 fusion.1
  18.8 0.2 reduce-window.9
  19.0 3.0 %negate_select_fusion = (f32[7,128,128]{2,1,0:T(8,128)}, f32[7,128,128]{2,1,0:T(8,128)}) fusion(f32[128]{0:T(128)S(1)} %mul.15, f32[7,128]{1,0:T(8,128)S(1)} %get-tuple-element.14, f32[7,128]{1,0:T(8,128)S(1)} %get-tuple-element.13, pred[128]{0:T(512)(128)(4,1)S(1)} %get-tuple-element.20, pred[128]{0:T(512)(128)(4,1)S(1)} %get-tuple-element.19), kind=kLoop, calls=%fused_computation | loop fusion | flops 458752 | bytes 925440 | tf_op jit(solution)/shard_map/jit(_where)/select_n | solution.py:82
  22.0 0.0 copy-start.8
  22.0 2.5 %shard_map.110.q_ref = bf16[128,768]{1,0:T(8,128)(2,1)} custom-call(bf16[128,768]{1,0:T(8,128)(2,1)} %get-tuple-element.10.x_ref, bf16[768,768]{1,0:T(8,128)(2,1)} %w_ref.1, f32[7,128,128]{2,1,0:T(8,128)} %get-tuple-element.12.cos_ref.rest_7_, f32[7,128,128]{2,1,0:T(8,128)} %get-tuple-element.11.sin_ref.rest_8_), custom_call_target="tpu_custom_call" | custom-call | tf_op jit(solution)/shard_map/pallas_call | solution.py:238
  24.5 0.0 collective-permute-done.7.rest_6_
  24.5 0.0 copy-done.8
  24.5 0.0 copy-start
  24.5 1.3 %collective-permute-start.2 = (bf16[128,768]{1,0:T(8,128)(2,1)S(1)}, bf16[128,768]{1,0:T(8,128)(2,1)S(1)}, u32[]{:S(2)}, u32[]{:S(2)}) collective-permute-start(bf16[128,768]{1,0:T(8,128)(2,1)S(1)} %copy-done.8), channel_id=1, source_target_pairs={{1,4},{0,5},{3,6},{2,7},{5,8},{4,9},{7,10},{6,11},{9,12},{8,13},{1... | collective-permute-start | bytes 589832 | tf_op jit(solution)/shard_map/ppermute | solution.py:200
  25.8 0.0 collective-permute-done.6.rest_5_
  25.8 0.0 copy-start.1
  25.8 1.3 %collective-permute-start.1 = (bf16[128,768]{1,0:T(8,128)(2,1)S(1)}, bf16[128,768]{1,0:T(8,128)(2,1)S(1)}, u32[]{:S(2)}, u32[]{:S(2)}) collective-permute-start(bf16[128,768]{1,0:T(8,128)(2,1)S(1)} %copy-done.8), channel_id=1, source_target_pairs={{1,6},{0,7},{3,8},{2,9},{5,10},{4,11},{7,12},{6,13},{9,14},{8,15},... | collective-permute-start | bytes 589832 | tf_op jit(solution)/shard_map/ppermute | solution.py:200
  27.1 0.5 %bitcast_subtract_fusion.place_ref = s32[7]{0:T(128)} fusion(s32[7,1]{0,1:T(1,128)S(1)} %reduce-window.9, pred[7]{0:T(512)(128)(4,1)S(1)} %compare_reduce_fusion), kind=kLoop, calls=%fused_computation.22 | loop fusion | flops 14 | bytes 63 | tf_op jit(solution)/shard_map/sub | solution.py:250
  27.6 0.0 collective-permute-done.5.rest_4_
  27.6 0.0 copy-start.2
  27.6 0.0 collective-permute-done.4.rest_3_
  27.6 0.0 copy-start.3
  27.7 0.0 collective-permute-done.3.rest_2_
  27.7 0.0 copy-start.4
  27.7 5.9 %collective-permute-done.2.rest_1_ = bf16[128,768]{1,0:T(8,128)(2,1)S(1)} collective-permute-done((bf16[128,768]{1,0:T(8,128)(2,1)S(1)}, bf16[128,768]{1,0:T(8,128)(2,1)S(1)}, u32[]{:S(2)}, u32[]{:S(2)}) %collective-permute-start.2) | collective-permute-done | bytes 196640 | tf_op jit(solution)/shard_map/ppermute | solution.py:200
  33.6 0.0 copy-start.5
  33.6 9.1 %collective-permute-done.1.rest_0_ = bf16[128,768]{1,0:T(8,128)(2,1)S(1)} collective-permute-done((bf16[128,768]{1,0:T(8,128)(2,1)S(1)}, bf16[128,768]{1,0:T(8,128)(2,1)S(1)}, u32[]{:S(2)}, u32[]{:S(2)}) %collective-permute-start.1) | collective-permute-done | bytes 196640 | tf_op jit(solution)/shard_map/ppermute | solution.py:200
  42.7 0.0 copy-start.6
  42.7 0.0 copy-done
  42.7 0.0 copy-done.1
  42.7 0.0 copy-done.2
  42.7 0.0 copy-done.3
  42.7 0.0 copy-done.4
  42.7 0.0 copy-done.5
  42.7 0.6 %copy-done.6 = bf16[128,768]{1,0:T(8,128)(2,1)} copy-done((bf16[128,768]{1,0:T(8,128)(2,1)}, bf16[128,768]{1,0:T(8,128)(2,1)S(1)}, u32[]{:S(2)}) %copy-start.6) | copy-done | bytes 196632
  43.4 7.4 %shard_map.111 = bf16[128,768]{1,0:T(8,128)(2,1)} custom-call(s32[7]{0:T(128)} %get-tuple-element.18.needed_ref, s32[7]{0:T(128)} %bitcast_subtract_fusion.place_ref, f32[12]{0:T(128)} %broadcast_multiply_fusion.1.scale_ref, bf16[128,768]{1,0:T(8,128)(2,1)} %shard_map.110.q_ref, bf16[128,768]{1,0:T(8,128)(2,1)} %copy-done.6, bf16[128,768]{1,0:T(8,128)(2,1)} %copy-done.5, ...), custom_call_target="tpu_custom_call" | custom-call | tf_op jit(solution)/shard_map/pallas_call | solution.py:251
  (3 shorter events, 0.0 us)
Async XLA Ops:
  0.0 3.3 %collective-permute-start = (s32[4]{0:T(128)}, s32[4]{0:T(128)S(1)}, u32[]{:S(2)}, u32[]{:S(2)}) collective-permute-start(s32[4]{0:T(128)} %bitcast.12), channel_id=1, source_target_pairs={{0,1},{1,0},{2,3},{3,2},{4,5},{5,4},{6,7},{7,6},{8,9},{9,8},{10,11... | collective-permute-start | bytes 56 | tf_op jit(solution)/shard_map/ppermute | solution.py:23
  3.3 0.6 %copy-start.7 = (s32[4]{0:T(128)}, s32[4]{0:T(128)S(1)}, u32[]{:S(2)}) copy-start(s32[4]{0:T(128)S(1)} %collective-permute-done.order_ref) | copy-start | bytes 52
  5.8 18.6 %collective-permute-start.7 = (bf16[128,768]{1,0:T(8,128)(2,1)}, bf16[128,768]{1,0:T(8,128)(2,1)S(1)}, u32[]{:S(2)}, u32[]{:S(2)}) collective-permute-start(bf16[128,768]{1,0:T(8,128)(2,1)} %get-tuple-element.8), channel_id=1, source_target_pairs={{7,0},{6,1},{9,2},{8,3},{11,4},{10,5},{13,6},{12,7},{15,8},{14,9},... | collective-permute-start | bytes 589832 | tf_op jit(solution)/shard_map/ppermute | solution.py:200
  8.6 17.1 %collective-permute-start.6 = (bf16[128,768]{1,0:T(8,128)(2,1)}, bf16[128,768]{1,0:T(8,128)(2,1)S(1)}, u32[]{:S(2)}, u32[]{:S(2)}) collective-permute-start(bf16[128,768]{1,0:T(8,128)(2,1)} %get-tuple-element.8), channel_id=1, source_target_pairs={{5,0},{4,1},{7,2},{6,3},{9,4},{8,5},{11,6},{10,7},{13,8},{12,9},{1... | collective-permute-start | bytes 589832 | tf_op jit(solution)/shard_map/ppermute | solution.py:200
  11.1 16.5 %collective-permute-start.5 = (bf16[128,768]{1,0:T(8,128)(2,1)}, bf16[128,768]{1,0:T(8,128)(2,1)S(1)}, u32[]{:S(2)}, u32[]{:S(2)}) collective-permute-start(bf16[128,768]{1,0:T(8,128)(2,1)} %get-tuple-element.8), channel_id=1, source_target_pairs={{3,0},{2,1},{5,2},{4,3},{7,4},{6,5},{9,6},{8,7},{11,8},{10,9},{13,... | collective-permute-start | bytes 589832 | tf_op jit(solution)/shard_map/ppermute | solution.py:200
  13.2 14.5 %collective-permute-start.4 = (bf16[128,768]{1,0:T(8,128)(2,1)}, bf16[128,768]{1,0:T(8,128)(2,1)S(1)}, u32[]{:S(2)}, u32[]{:S(2)}) collective-permute-start(bf16[128,768]{1,0:T(8,128)(2,1)} %get-tuple-element.8), channel_id=1, source_target_pairs={{0,1},{1,0},{2,3},{3,2},{4,5},{5,4},{6,7},{7,6},{8,9},{9,8},{10,11... | collective-permute-start | bytes 589832 | tf_op jit(solution)/shard_map/ppermute | solution.py:23
  13.7 13.9 %collective-permute-start.3 = (bf16[128,768]{1,0:T(8,128)(2,1)}, bf16[128,768]{1,0:T(8,128)(2,1)S(1)}, u32[]{:S(2)}, u32[]{:S(2)}) collective-permute-start(bf16[128,768]{1,0:T(8,128)(2,1)} %get-tuple-element.8), channel_id=1, source_target_pairs={{1,2},{0,3},{3,4},{2,5},{5,6},{4,7},{7,8},{6,9},{9,10},{8,11},{11,... | collective-permute-start | bytes 589832 | tf_op jit(solution)/shard_map/ppermute | solution.py:200
  22.0 2.5 %copy-start.8 = (bf16[128,768]{1,0:T(8,128)(2,1)S(1)}, bf16[128,768]{1,0:T(8,128)(2,1)}, u32[]{:S(2)}) copy-start(bf16[128,768]{1,0:T(8,128)(2,1)} %get-tuple-element.8) | copy-start | bytes 589828
  24.5 18.2 %copy-start = (bf16[128,768]{1,0:T(8,128)(2,1)}, bf16[128,768]{1,0:T(8,128)(2,1)S(1)}, u32[]{:S(2)}) copy-start(bf16[128,768]{1,0:T(8,128)(2,1)S(1)} %collective-permute-done.7.rest_6_) | copy-start | bytes 589828
  24.5 9.1 %collective-permute-start.2 = (bf16[128,768]{1,0:T(8,128)(2,1)S(1)}, bf16[128,768]{1,0:T(8,128)(2,1)S(1)}, u32[]{:S(2)}, u32[]{:S(2)}) collective-permute-start(bf16[128,768]{1,0:T(8,128)(2,1)S(1)} %copy-done.8), channel_id=1, source_target_pairs={{1,4},{0,5},{3,6},{2,7},{5,8},{4,9},{7,10},{6,11},{9,12},{8,13},{1... | collective-permute-start | bytes 589832 | tf_op jit(solution)/shard_map/ppermute | solution.py:200
  25.8 16.9 %copy-start.1 = (bf16[128,768]{1,0:T(8,128)(2,1)}, bf16[128,768]{1,0:T(8,128)(2,1)S(1)}, u32[]{:S(2)}) copy-start(bf16[128,768]{1,0:T(8,128)(2,1)S(1)} %collective-permute-done.6.rest_5_) | copy-start | bytes 589828
  25.8 16.9 %collective-permute-start.1 = (bf16[128,768]{1,0:T(8,128)(2,1)S(1)}, bf16[128,768]{1,0:T(8,128)(2,1)S(1)}, u32[]{:S(2)}, u32[]{:S(2)}) collective-permute-start(bf16[128,768]{1,0:T(8,128)(2,1)S(1)} %copy-done.8), channel_id=1, source_target_pairs={{1,6},{0,7},{3,8},{2,9},{5,10},{4,11},{7,12},{6,13},{9,14},{8,15},... | collective-permute-start | bytes 589832 | tf_op jit(solution)/shard_map/ppermute | solution.py:200
  27.6 15.1 %copy-start.2 = (bf16[128,768]{1,0:T(8,128)(2,1)}, bf16[128,768]{1,0:T(8,128)(2,1)S(1)}, u32[]{:S(2)}) copy-start(bf16[128,768]{1,0:T(8,128)(2,1)S(1)} %collective-permute-done.5.rest_4_) | copy-start | bytes 589828
  27.6 15.1 %copy-start.3 = (bf16[128,768]{1,0:T(8,128)(2,1)}, bf16[128,768]{1,0:T(8,128)(2,1)S(1)}, u32[]{:S(2)}) copy-start(bf16[128,768]{1,0:T(8,128)(2,1)S(1)} %collective-permute-done.4.rest_3_) | copy-start | bytes 589828
  27.7 15.1 %copy-start.4 = (bf16[128,768]{1,0:T(8,128)(2,1)}, bf16[128,768]{1,0:T(8,128)(2,1)S(1)}, u32[]{:S(2)}) copy-start(bf16[128,768]{1,0:T(8,128)(2,1)S(1)} %collective-permute-done.3.rest_2_) | copy-start | bytes 589828
  33.6 9.2 %copy-start.5 = (bf16[128,768]{1,0:T(8,128)(2,1)}, bf16[128,768]{1,0:T(8,128)(2,1)S(1)}, u32[]{:S(2)}) copy-start(bf16[128,768]{1,0:T(8,128)(2,1)S(1)} %collective-permute-done.2.rest_1_) | copy-start | bytes 589828
  42.7 0.7 %copy-start.6 = (bf16[128,768]{1,0:T(8,128)(2,1)}, bf16[128,768]{1,0:T(8,128)(2,1)S(1)}, u32[]{:S(2)}) copy-start(bf16[128,768]{1,0:T(8,128)(2,1)S(1)} %collective-permute-done.1.rest_0_) | copy-start | bytes 589828
